TPU v7x, 256 devices: a whole 4x4x8 slice. The times are simulated.
256 devices in a mesh: gx: 4 (over x), gy: 8 (over z_hi, core), gz: 8 (over z_lo, y).
Axes of the slice: x: 4, y: 4, z: 8 (z_hi: 4, z_lo: 2; z = z_hi * 2 + z_lo), core: 2. Of those that a mesh axis runs over, the one named last changes fastest.
Arguments:
- fine: float32 [5, 64, 128, 1024], P(None, 'gx', 'gy', 'gz'), as said below
- shell: float32 [4, 512, 3840], P('gx', ('gy', 'gz')), as said below
- parent: int32 [4, 512], P('gx'), may hold values from 0 to 511, as said below
- link: int32 [6, 4, 8, 64], P(None, 'gx', 'gy', 'gz'), may hold values 0 or 1
Outputs:
- fine_new: float32 [5, 64, 128, 1024], P(None, 'gx', 'gy', 'gz')
- coarse_new: float32 [4, 512, 2560], P('gx', ('gy', 'gz'))
Inputs may be any that keep to these rules, and one draw needn't show every extreme that they name: Each row parent[i, :] names every slot 0 to 511 exactly once. Of the 8 blocks q = d * 8 to d * 8 + 7 of a row, at most 2 have parents among the slots o * 8 to o * 8 + 7 of any one o, and every such pair that meets at all holds exactly 2. `fine`: density and energy make pressure positive in every cell; velocities stay well below the sound speed times a few. `shell`: same physical ranges as fine.
All inputs are finite; a program needn't handle non-finite values. No bound on the sum of `link` on one device may be relied on, other than what follows from the above.
Results may differ from a plain program's by a relative error of at most 0.0003.
Values sent between devices are 32-bit elements; how exact they have to be, the bound alone decides.
No kernel may reach another device: no remote copies, remote signals or barrier semaphores. Data moves between devices by JAX's collectives and lax.ppermute only.
A program may use at most 128 MiB of HBM per device.

v0:
```python
import jax
import jax.numpy as jnp
from jax import lax
from jax.experimental import pallas as pl
from jax.experimental.pallas import tpu as pltpu
from jax.sharding import PartitionSpec as P

BS = 16
CAP = 2

GAMMA = 1.4
LAMBDA = 0.05


def shift_in(plane, axis, forward):
    count = lax.axis_size(axis)
    if forward:
        pairs = [(i, (i + 1) % count) for i in range(count)]
    else:
        pairs = [((i + 1) % count, i) for i in range(count)]
    return lax.ppermute(plane, axis, pairs)


def prims(v):
    rho, mx, my, mz, energy = v
    ux = mx / rho
    uy = my / rho
    uz = mz / rho
    press = (GAMMA - 1.0) * (energy - 0.5 * (mx * ux + my * uy + mz * uz))
    sound = jnp.sqrt(GAMMA * press / rho)
    return (ux, uy, uz), press, sound


def flux_of(v, prim, direc):
    rho, mx, my, mz, energy = v
    vel, press, sound = prim
    normal = vel[direc]
    mom = (mx, my, mz)
    parts = [mom[direc], mx * normal, my * normal, mz * normal, (energy + press) * normal]
    parts[1 + direc] = parts[1 + direc] + press
    return parts, jnp.abs(normal) + sound


def face_of(fa, sa, va, fb, sb, vb):
    wave = 0.5 * jnp.maximum(sa, sb)
    return [0.5 * (fa[i] + fb[i]) - wave * (vb[i] - va[i]) for i in range(5)]


def substep_kernel(u_ref, gx_ref, gy_ref, zfix_ref, zflag_ref, o_ref):
    nx = u_ref.shape[1]
    ny = u_ref.shape[2]
    nz = u_ref.shape[3]
    row = lax.broadcasted_iota(jnp.int32, (ny, nz), 0)
    over_lo = zflag_ref[0] != 0
    over_hi = zflag_ref[1] != 0

    def body(x, carry):
        cen = [u_ref[f, x] for f in range(5)]
        below = jnp.maximum(x - 1, 0)
        above = jnp.minimum(x + 1, nx - 1)
        xm = [jnp.where(x == 0, gx_ref[0, f], u_ref[f, below]) for f in range(5)]
        xp = [jnp.where(x == nx - 1, gx_ref[1, f], u_ref[f, above]) for f in range(5)]
        ym = [
            jnp.where(row == 0, jnp.broadcast_to(gy_ref[0, x, f], (ny, nz)), pltpu.roll(cen[f], 1, 0))
            for f in range(5)
        ]
        yp = [
            jnp.where(
                row == ny - 1, jnp.broadcast_to(gy_ref[1, x, f], (ny, nz)), pltpu.roll(cen[f], ny - 1, 0)
            )
            for f in range(5)
        ]
        zm = [jnp.where(over_lo, zfix_ref[f, x], pltpu.roll(cen[f], 1, 1)) for f in range(5)]
        zp = [jnp.where(over_hi, zfix_ref[f, x], pltpu.roll(cen[f], nz - 1, 1)) for f in range(5)]
        pc = prims(cen)
        total = None
        for direc, (lo, hi) in enumerate(((xm, xp), (ym, yp), (zm, zp))):
            fc, sc = flux_of(cen, pc, direc)
            fl, sl = flux_of(lo, prims(lo), direc)
            fh, sh = flux_of(hi, prims(hi), direc)
            left = face_of(fl, sl, lo, fc, sc, cen)
            right = face_of(fc, sc, cen, fh, sh, hi)
            diff = [right[i] - left[i] for i in range(5)]
            total = diff if total is None else [total[i] + diff[i] for i in range(5)]
        for f in range(5):
            o_ref[f, x] = cen[f] - LAMBDA * total[f]
        return carry

    lax.fori_loop(0, nx, body, 0)


def substep(state, gx, gy, zfix, zflag):
    return pl.pallas_call(
        substep_kernel, out_shape=jax.ShapeDtypeStruct(state.shape, state.dtype)
    )(state, gx, gy, zfix, zflag)


def replicate(rows, cols):
    step = cols // rows
    return (jnp.arange(cols)[None, :] // step == jnp.arange(rows)[:, None]).astype(jnp.float32)


def exact_dot(spec, *ops):
    return jnp.einsum(spec, *ops, precision=lax.Precision.HIGHEST, preferred_element_type=jnp.float32)


def coarse_faces(fetched, nblk):
    half = BS // 2
    lv = fetched.reshape(nblk, 2, 6, 5, half, half)
    rows = replicate(half, BS)
    side = lv[:, :, 0:4].transpose(1, 2, 3, 4, 0, 5).reshape(2, 4, 5, half, nblk * half)
    side = exact_dot("ay,lkfab,bz->lkfyz", rows, side, replicate(nblk * half, nblk * BS))
    ends = lv[:, :, 4:6].transpose(1, 2, 3, 4, 5, 0)
    ends = exact_dot("ax,by,lkfabc,cz->lkfxyz", rows, rows, ends, replicate(nblk, nblk * BS))
    return side, ends


def ghost_inputs(state, side, ends, links):
    nz_dev = state.shape[3]
    chosen = [jnp.repeat(links[:, face] == 1, BS)[None, None, :] for face in range(4)]
    gx = jnp.stack(
        [
            jnp.where(chosen[0], shift_in(state[:, -1], "gx", True), side[0]),
            jnp.where(chosen[1], shift_in(state[:, 0], "gx", False), side[1]),
        ]
    )
    gy = jnp.stack(
        [
            jnp.where(chosen[2], shift_in(state[:, :, -1], "gy", True), side[2]),
            jnp.where(chosen[3], shift_in(state[:, :, 0], "gy", False), side[3]),
        ]
    )
    gy = gy.transpose(0, 2, 1, 3)[:, :, :, None, :]
    far_lo = shift_in(state[..., -1], "gz", True)
    far_hi = shift_in(state[..., 0], "gz", False)
    lane = jnp.arange(nz_dev, dtype=jnp.int32)
    at_lo = lane % BS == 0
    at_hi = lane % BS == BS - 1
    link_lo = jnp.repeat(links[:, 4] == 1, BS)
    link_hi = jnp.repeat(links[:, 5] == 1, BS)
    lo_val = jnp.where(link_lo & (lane == 0), far_lo[..., None], ends[0])
    hi_val = jnp.where(link_hi & (lane == nz_dev - 1), far_hi[..., None], ends[1])
    zfix = jnp.where(at_lo, lo_val, hi_val)
    flag_lo = at_lo & (~link_lo | (lane == 0))
    flag_hi = at_hi & (~link_hi | (lane == nz_dev - 1))
    zflag = jnp.broadcast_to(
        jnp.stack([flag_lo, flag_hi]).astype(jnp.int32)[:, None, :], (2, state.shape[2], nz_dev)
    )
    return gx, gy, zfix, zflag


def restrict_state(state, nblk):
    half = BS // 2
    nz_dev = state.shape[3]
    pairs = state.reshape(5, half, 2, BS, nz_dev)
    planes = pairs[:, :, 0] + pairs[:, :, 1]
    means = 0.125 * exact_dot(
        "ay,fxyl,lm->fxam", replicate(half, BS), planes, replicate(nblk * half, nz_dev).T
    )
    means = means.reshape(5, half, half, nblk, half)
    return means.transpose(3, 0, 1, 2, 4).reshape(nblk, -1)


def routes(parent_row, nblk):
    ndev = parent_row.shape[0] // nblk
    owner = (parent_row // nblk).reshape(ndev, nblk)
    slot = (parent_row % nblk).reshape(ndev, nblk)
    pos = jnp.arange(nblk, dtype=jnp.int32)
    same = owner[:, :, None] == owner[:, None, :]
    earlier = (pos[None, :] < pos[:, None])[None]
    rank = jnp.sum((same & earlier).astype(jnp.int32), axis=2)
    return owner, slot, rank


def shards(fine, shell, parent, link):
    half = BS // 2
    nz_dev = fine.shape[3]
    nblk = nz_dev // BS
    me = lax.axis_index("gy") * lax.axis_size("gz") + lax.axis_index("gz")
    parent_row = parent[0]
    ndev = parent_row.shape[0] // nblk
    links = link[:, 0, 0, :].T
    width = shell.shape[2] // 2
    owner, slot, rank = routes(parent_row, nblk)

    mine = owner == me
    picks = jnp.stack(
        [jnp.sum(jnp.where(mine & (rank == c), slot, 0), axis=1) for c in range(CAP)], axis=1
    )
    local = shell[0]
    levels = jnp.concatenate(
        [local[:, :width], 0.5 * (local[:, :width] + local[:, width:])], axis=1
    )
    outgoing = jnp.take(levels, picks.reshape(-1), axis=0, mode="clip").reshape(
        ndev, CAP, levels.shape[1]
    )
    incoming = lax.all_to_all(outgoing, ("gy", "gz"), 0, 0, tiled=True)
    my_owner = lax.dynamic_index_in_dim(owner, me, keepdims=False)
    my_rank = lax.dynamic_index_in_dim(rank, me, keepdims=False)
    fetched = jnp.take(
        incoming.reshape(ndev * CAP, -1), my_owner * CAP + my_rank, axis=0, mode="clip"
    )
    side, ends = coarse_faces(fetched, nblk)
    state = fine
    for step in range(2):
        state = substep(state, *ghost_inputs(state, side[step], ends[step], links))
    restricted = restrict_state(state, nblk)

    pos = jnp.arange(nblk, dtype=jnp.int32)
    dest = jnp.arange(ndev, dtype=jnp.int32)[:, None, None]
    cell = jnp.arange(CAP, dtype=jnp.int32)[None, :, None]
    hit = (my_owner[None, None, :] == dest) & (my_rank[None, None, :] == cell)
    which = jnp.sum(jnp.where(hit, pos[None, None, :], 0), axis=2)
    back = jnp.take(restricted, which.reshape(-1), axis=0, mode="clip").reshape(
        ndev, CAP, restricted.shape[1]
    )
    returned = lax.all_to_all(back, ("gy", "gz"), 0, 0, tiled=True)
    target = me * nblk + pos
    source = (jnp.arange(ndev * nblk, dtype=jnp.int32) // nblk) * CAP + rank.reshape(-1)
    match = parent_row[None, :] == target[:, None]
    origin = jnp.sum(jnp.where(match, source[None, :], 0), axis=1)
    gathered = jnp.take(returned.reshape(ndev * CAP, -1), origin, axis=0, mode="clip")
    coarse_new = gathered.reshape(1, nblk, restricted.shape[1])
    return (state, coarse_new)


def solution(mesh):
    return jax.shard_map(
        shards,
        mesh=mesh,
        in_specs=(
            P(None, "gx", "gy", "gz"),
            P("gx", ("gy", "gz"), None),
            P("gx", None),
            P(None, "gx", "gy", "gz"),
        ),
        out_specs=(P(None, "gx", "gy", "gz"), P("gx", ("gy", "gz"), None)),
        check_vma=False,
    )
```

profile of v0, /device:TPU:8, one launch (start us, length us, event | category | flops | bytes accessed | tf_op | source)
XLA Modules:
  0.0 164.2 jit_solution(15409491212956186589)
XLA Ops:
  1.2 1.3 reduce.13
  3.1 0.9 fusion.65
  4.0 1.3 gather_fusion
  5.3 2.5 %reshape.471 = f32[64,2,3840]{2,1,0:T(2,128)} reshape(f32[128,3840]{1,0:T(8,128)S(1)} %gather_fusion) | data formatting | bytes 3932160 | tf_op jit(solution)/shard_map/reshape | solution.py:194
  7.8 12.2 %all-to-all-start = ((f32[64,2,3840]{2,1,0:T(2,128)}), f32[64,2,3840]{2,1,0:T(2,128)S(1)}, u32[]{:S(2)}, u32[]{:S(2)}) async-start(f32[64,2,3840]{2,1,0:T(2,128)} %reshape.471), calls=%async_computation | async-start | bytes 3932160 | tf_op jit(solution)/shard_map/all_to_all | solution.py:197
  20.0 0.7 fusion.64
  20.7 3.6 %collective-permute-start.3 = (f32[5,16,128]{2,1,0:T(8,128)}, f32[5,16,128]{2,1,0:T(8,128)}, u32[]{:S(2)}, u32[]{:S(2)}) collective-permute-start(f32[5,16,128]{2,1,0:T(8,128)} %bitcast.23), channel_id=1, source_target_pairs={{8,0},{16,8},{24,16},{32,24},{40,32},{48,40},{56,48},{0,56},{9,1},... | collective-permute-start | bytes 122888 | tf_op jit(solution)/shard_map/ppermute | solution.py:21
  24.9 1.5 collective-permute-start
  26.4 1.7 %collective-permute-start.1 = (f32[5,16,128]{2,1,0:T(8,128)S(1)}, f32[5,16,128]{2,1,0:T(8,128)}, u32[]{:S(2)}, u32[]{:S(2)}) collective-permute-start(f32[5,16,128]{2,1,0:T(8,128)S(1)} %get-tuple-element.20), channel_id=1, source_target_pairs={{64,0},{128,64},{192,128},{0,192},{65,1},{129,65},{193,129},{1,193... | collective-permute-start | bytes 122888 | tf_op jit(solution)/shard_map/ppermute | solution.py:21
  28.1 1.0 fusion.63
  29.2 2.2 %copy.97 = f32[5,16,16,1]{2,1,0,3:T(8,128)} copy(f32[5,16,16,1]{3,2,1,0:T(8,128)} %get-tuple-element.16) | data formatting | bytes 10240
  33.2 0.6 broadcast_in_dim.192
  34.5 1.2 copy.95
  37.3 31.9 %all-to-all-done = f32[64,2,3840]{2,1,0:T(2,128)S(1)} async-done(((f32[64,2,3840]{2,1,0:T(2,128)}), f32[64,2,3840]{2,1,0:T(2,128)S(1)}, u32[]{:S(2)}, u32[]{:S(2)}) %all-to-all-start) | async-done | bytes 1966112 | tf_op jit(solution)/shard_map/all_to_all | solution.py:197
  69.2 2.6 %reshape.472 = f32[128,3840]{1,0:T(8,128)} reshape(f32[64,2,3840]{2,1,0:T(2,128)S(1)} %all-to-all-done) | data formatting | bytes 3932160 | tf_op jit(solution)/shard_map/reshape | solution.py:201
  71.8 2.2 %gather_fusion.1 = f32[8,3840]{1,0:T(8,128)S(1)} fusion(f32[128,3840]{1,0:T(8,128)} %reshape.472, s32[1024]{0:T(1024)S(1)} %pad_clamp_fusion.2), kind=kCustom, calls=%fused_computation.1 | custom fusion | bytes 245792 | tf_op jit(solution)/shard_map/jit(_take)/gather | solution.py:200
  74.0 1.1 reshape.473
  75.2 1.2 copy-done
  76.4 0.8 copy.65
  77.5 0.7 slice-done
  79.5 0.7 fusion.39
  80.8 1.5 collective-permute-start.4
  82.4 0.9 fusion.24
  83.3 2.3 %fusion.46 = f32[2,2,5,16,16,128]{5,4,3,2,1,0:T(8,128)S(1)} fusion(f32[2,2,5,8,16,16]{5,3,4,2,1,0:T(8,128)S(1)} %fusion.39, s32[128]{0:T(128)S(1)} %copy-done.10), kind=kOutput, calls=%fused_computation.97 | convolution fusion | flops 62915584 | bytes 2785792 | tf_op jit(solution)/shard_map/ax,by,lkfabc,cz->lkfxyz/dot_general | solution.py:104
  85.6 0.6 pad_maximum_fusion.1.gx_ref
  86.3 0.7 copy.73.gy_ref
  87.0 2.0 %fusion.4.zfix_ref = f32[5,16,16,128]{3,2,1,0:T(8,128)} fusion(f32[2,2,5,16,16,128]{5,4,3,2,1,0:T(8,128)S(1)} %fusion.46, f32[5,16,16]{2,1,0:T(8,128)} %collective-permute-done.5, f32[5,16,16]{2,1,0:T(8,128)S(1)} %collective-permute-done.4, pred[128]{0:T(512)(128)(4,1)S(1)} %copy-done.7, pred[128]{0:T(512)(128)(4,1)S(1)} %copy-done.8, ...), kind=kLoop, calls=%fused_computation.16 | loop fusion | flops 491520 | bytes 1976704 | tf_op jit(solution)/shard_map/jit(_where)/select_n | solution.py:143
  89.6 4.5 %shard_map.59.u_ref = f32[5,16,16,128]{3,2,1,0:T(8,128)} custom-call(f32[5,16,16,128]{3,2,1,0:T(8,128)} %u_ref.1, f32[2,5,16,128]{3,2,1,0:T(8,128)} %pad_maximum_fusion.1.gx_ref, f32[2,16,5,1,128]{4,3,2,1,0:T(1,128)} %copy.73.gy_ref, f32[5,16,16,128]{3,2,1,0:T(8,128)} %fusion.4.zfix_ref, s32[2,16,128]{2,1,0:T(8,128)} %broadcast_in_dim.214.zflag_ref), custom_call_target="tpu_custom_call" | custom-call | tf_op jit(solution)/shard_map/pallas_call | solution.py:93
  94.2 1.9 %slice_reduce_fusion.1 = (f32[5,16,16]{2,1,0:T(8,128)S(1)}, f32[5,16,16]{2,1,0:T(8,128)S(1)}) fusion(f32[5,16,16,128]{3,2,1,0:T(8,128)} %shard_map.59.u_ref), kind=kLoop, calls=%fused_computation.13 | loop fusion | bytes 20480 | tf_op jit(solution)/shard_map/slice | solution.py:134
  96.1 1.1 fusion.62
  97.2 1.2 collective-permute-start.10
  98.4 0.9 collective-permute-start.11
  99.3 0.8 slice_bitcast_fusion.13
  100.1 1.5 collective-permute-start.6
  101.6 1.7 %collective-permute-start.7 = (f32[5,16,128]{2,1,0:T(8,128)S(1)}, f32[5,16,128]{2,1,0:T(8,128)S(1)}, u32[]{:S(2)}, u32[]{:S(2)}) collective-permute-start(f32[5,16,128]{2,1,0:T(8,128)S(1)} %get-tuple-element.14), channel_id=1, source_target_pairs={{64,0},{128,64},{192,128},{0,192},{65,1},{129,65},{193,129},{1,193... | collective-permute-start | bytes 122888 | tf_op jit(solution)/shard_map/ppermute | solution.py:21
  103.9 1.3 fusion.1.zfix_ref
  105.6 3.3 %collective-permute-done.8 = f32[5,16,128]{2,1,0:T(8,128)S(1)} collective-permute-done((f32[5,16,128]{2,1,0:T(8,128)S(1)}, f32[5,16,128]{2,1,0:T(8,128)S(1)}, u32[]{:S(2)}, u32[]{:S(2)}) %collective-permute-start.8) | collective-permute-done | bytes 40992 | tf_op jit(solution)/shard_map/ppermute | solution.py:21
  108.9 0.7 copy.78.gy_ref
  109.7 0.6 pad_maximum_fusion.2.gx_ref
  110.3 4.5 %shard_map.60 = f32[5,16,16,128]{3,2,1,0:T(8,128)} custom-call(f32[5,16,16,128]{3,2,1,0:T(8,128)} %shard_map.59.u_ref, f32[2,5,16,128]{3,2,1,0:T(8,128)} %pad_maximum_fusion.2.gx_ref, f32[2,16,5,1,128]{4,3,2,1,0:T(1,128)} %copy.78.gy_ref, f32[5,16,16,128]{3,2,1,0:T(8,128)} %fusion.1.zfix_ref, s32[2,16,128]{2,1,0:T(8,128)} %broadcast_in_dim.214.zflag_ref), custom_call_target="tpu_custom_call" | custom-call | tf_op jit(solution)/shard_map/pallas_call | solution.py:93
  114.8 1.3 fusion.10
  117.0 0.7 reshape.479
  117.7 1.1 gather_fusion.2
  118.8 1.9 %reshape.480 = f32[64,2,2560]{2,1,0:T(2,128)} reshape(f32[128,2560]{1,0:T(8,128)S(1)} %gather_fusion.2) | data formatting | bytes 2621440 | tf_op jit(solution)/shard_map/reshape | solution.py:214
  120.6 7.0 %all-to-all-start.1 = ((f32[64,2,2560]{2,1,0:T(2,128)}), f32[64,2,2560]{2,1,0:T(2,128)S(1)}, u32[]{:S(2)}, u32[]{:S(2)}) async-start(f32[64,2,2560]{2,1,0:T(2,128)} %reshape.480), calls=%async_computation.1 | async-start | bytes 2621440 | tf_op jit(solution)/shard_map/all_to_all | solution.py:217
  128.0 34.1 %all-to-all-done.1 = f32[64,2,2560]{2,1,0:T(2,128)S(1)} async-done(((f32[64,2,2560]{2,1,0:T(2,128)}), f32[64,2,2560]{2,1,0:T(2,128)S(1)}, u32[]{:S(2)}, u32[]{:S(2)}) %all-to-all-start.1) | async-done | bytes 1310752 | tf_op jit(solution)/shard_map/all_to_all | solution.py:217
  162.1 0.9 reshape.481
  163.0 1.2 gather_fusion.3
  (103 shorter events, 10.9 us)
Async XLA Ops:
  7.8 12.2 %copy-start.1 = (f32[5,16,16,128]{3,2,1,0:T(8,128)S(1)}, f32[5,16,16,128]{3,2,1,0:T(8,128)}, u32[]{:S(2)}) copy-start(f32[5,16,16,128]{3,2,1,0:T(8,128)} %u_ref.1) | copy-start | bytes 1966084
  7.8 61.4 %all-to-all-start = ((f32[64,2,3840]{2,1,0:T(2,128)}), f32[64,2,3840]{2,1,0:T(2,128)S(1)}, u32[]{:S(2)}, u32[]{:S(2)}) async-start(f32[64,2,3840]{2,1,0:T(2,128)} %reshape.471), calls=%async_computation | async-start | bytes 3932160 | tf_op jit(solution)/shard_map/all_to_all | solution.py:197
  20.7 60.1 %collective-permute-start.3 = (f32[5,16,128]{2,1,0:T(8,128)}, f32[5,16,128]{2,1,0:T(8,128)}, u32[]{:S(2)}, u32[]{:S(2)}) collective-permute-start(f32[5,16,128]{2,1,0:T(8,128)} %bitcast.23), channel_id=1, source_target_pairs={{8,0},{16,8},{24,16},{32,24},{40,32},{48,40},{56,48},{0,56},{9,1},... | collective-permute-start | bytes 122888 | tf_op jit(solution)/shard_map/ppermute | solution.py:21
  24.3 58.1 %collective-permute-start.2 = (f32[5,16,128]{2,1,0:T(8,128)S(1)}, f32[5,16,128]{2,1,0:T(8,128)}, u32[]{:S(2)}, u32[]{:S(2)}) collective-permute-start(f32[5,16,128]{2,1,0:T(8,128)S(1)} %bitcast.222), channel_id=1, source_target_pairs={{0,8},{8,16},{16,24},{24,32},{32,40},{40,48},{48,56},{56,0},{1,9},... | collective-permute-start | bytes 122888 | tf_op jit(solution)/shard_map/ppermute | solution.py:21
  24.9 57.5 %collective-permute-start = (f32[5,16,128]{2,1,0:T(8,128)}, f32[5,16,128]{2,1,0:T(8,128)}, u32[]{:S(2)}, u32[]{:S(2)}) collective-permute-start(f32[5,16,128]{2,1,0:T(8,128)} %get-tuple-element.19), channel_id=1, source_target_pairs={{0,64},{64,128},{128,192},{192,0},{1,65},{65,129},{129,193},{193,1... | collective-permute-start | bytes 122888 | tf_op jit(solution)/shard_map/ppermute | solution.py:21
  26.4 5.6 %copy-start.4 = (s32[6,1,1,8]{3,2,1,0:T(1,128)S(1)}, s32[6,1,1,8]{3,2,1,0:T(1,128)}, u32[]{:S(2)}) copy-start(s32[6,1,1,8]{3,2,1,0:T(1,128)} %param.7) | copy-start | bytes 580
  26.4 56.0 %collective-permute-start.1 = (f32[5,16,128]{2,1,0:T(8,128)S(1)}, f32[5,16,128]{2,1,0:T(8,128)}, u32[]{:S(2)}, u32[]{:S(2)}) collective-permute-start(f32[5,16,128]{2,1,0:T(8,128)S(1)} %get-tuple-element.20), channel_id=1, source_target_pairs={{64,0},{128,64},{192,128},{0,192},{65,1},{129,65},{193,129},{1,193... | collective-permute-start | bytes 122888 | tf_op jit(solution)/shard_map/ppermute | solution.py:21
  31.4 55.6 %collective-permute-start.5 = (f32[5,16,16]{2,1,0:T(8,128)}, f32[5,16,16]{2,1,0:T(8,128)}, u32[]{:S(2)}, u32[]{:S(2)}) collective-permute-start(f32[5,16,16]{2,1,0:T(8,128)} %bitcast.37), channel_id=1, source_target_pairs={{1,0},{2,1},{3,2},{4,3},{5,4},{6,5},{7,6},{0,7},{9,8},{10,9},{11,1... | collective-permute-start | bytes 15368 | tf_op jit(solution)/shard_map/ppermute | solution.py:21
  75.1 1.3 copy-start
  77.2 1.1 slice-start
  79.5 1.4 copy-start.2
  79.5 2.9 %copy-start.5 = (pred[128]{0:T(512)(128)(4,1)S(1)}, pred[128]{0:T(512)(128)(4,1)}, u32[]{:S(2)}) copy-start(pred[128]{0:T(512)(128)(4,1)} %broadcast_in_dim.192) | copy-start | bytes 388
  80.2 3.1 %copy-start.10 = (s32[128]{0:T(128)S(1)}, s32[128]{0:T(128)}, u32[]{:S(2)}) copy-start(s32[128]{0:T(128)} %and_select_fusion.1) | copy-start | bytes 1540
  80.8 6.1 %collective-permute-start.4 = (f32[5,16,16]{2,1,0:T(8,128)S(1)}, f32[5,16,16]{2,1,0:T(8,128)S(1)}, u32[]{:S(2)}, u32[]{:S(2)}) collective-permute-start(f32[5,16,16]{2,1,0:T(8,128)S(1)} %bitcast.225), channel_id=1, source_target_pairs={{0,1},{1,2},{2,3},{3,4},{4,5},{5,6},{6,7},{7,0},{8,9},{9,10},{10,1... | collective-permute-start | bytes 15368 | tf_op jit(solution)/shard_map/ppermute | solution.py:21
  83.3 3.7 %copy-start.7 = (pred[128]{0:T(512)(128)(4,1)S(1)}, pred[128]{0:T(512)(128)(4,1)}, u32[]{:S(2)}) copy-start(pred[128]{0:T(512)(128)(4,1)} %compare_and_fusion) | copy-start | bytes 388
  83.3 3.7 %copy-start.8 = (pred[128]{0:T(512)(128)(4,1)S(1)}, pred[128]{0:T(512)(128)(4,1)}, u32[]{:S(2)}) copy-start(pred[128]{0:T(512)(128)(4,1)} %get-tuple-element.41) | copy-start | bytes 388
  83.3 3.7 %copy-start.9 = (pred[128]{0:T(512)(128)(4,1)S(1)}, pred[128]{0:T(512)(128)(4,1)}, u32[]{:S(2)}) copy-start(pred[128]{0:T(512)(128)(4,1)} %get-tuple-element.42) | copy-start | bytes 388
  96.1 12.8 %copy-start.6 = (pred[128]{0:T(512)(128)(4,1)S(1)}, pred[128]{0:T(512)(128)(4,1)}, u32[]{:S(2)}) copy-start(pred[128]{0:T(512)(128)(4,1)} %broadcast_in_dim.192) | copy-start | bytes 388
  97.2 6.2 %collective-permute-start.10 = (f32[5,16,16]{2,1,0:T(8,128)S(1)}, f32[5,16,16]{2,1,0:T(8,128)S(1)}, u32[]{:S(2)}, u32[]{:S(2)}) collective-permute-start(f32[5,16,16]{2,1,0:T(8,128)S(1)} %get-tuple-element.2), channel_id=1, source_target_pairs={{0,1},{1,2},{2,3},{3,4},{4,5},{5,6},{6,7},{7,0},{8,9},{9,10},{10,1... | collective-permute-start | bytes 15368 | tf_op jit(solution)/shard_map/ppermute | solution.py:21
  98.4 5.4 %collective-permute-start.11 = (f32[5,16,16]{2,1,0:T(8,128)S(1)}, f32[5,16,16]{2,1,0:T(8,128)S(1)}, u32[]{:S(2)}, u32[]{:S(2)}) collective-permute-start(f32[5,16,16]{2,1,0:T(8,128)S(1)} %get-tuple-element.3), channel_id=1, source_target_pairs={{1,0},{2,1},{3,2},{4,3},{5,4},{6,5},{7,6},{0,7},{9,8},{10,9},{11,1... | collective-permute-start | bytes 15368 | tf_op jit(solution)/shard_map/ppermute | solution.py:21
  100.1 5.2 %collective-permute-start.6 = (f32[5,16,128]{2,1,0:T(8,128)S(1)}, f32[5,16,128]{2,1,0:T(8,128)S(1)}, u32[]{:S(2)}, u32[]{:S(2)}) collective-permute-start(f32[5,16,128]{2,1,0:T(8,128)S(1)} %get-tuple-element.13), channel_id=1, source_target_pairs={{0,64},{64,128},{128,192},{192,0},{1,65},{65,129},{129,193},{193,1... | collective-permute-start | bytes 122888 | tf_op jit(solution)/shard_map/ppermute | solution.py:21
  101.6 4.0 %collective-permute-start.7 = (f32[5,16,128]{2,1,0:T(8,128)S(1)}, f32[5,16,128]{2,1,0:T(8,128)S(1)}, u32[]{:S(2)}, u32[]{:S(2)}) collective-permute-start(f32[5,16,128]{2,1,0:T(8,128)S(1)} %get-tuple-element.14), channel_id=1, source_target_pairs={{64,0},{128,64},{192,128},{0,192},{65,1},{129,65},{193,129},{1,193... | collective-permute-start | bytes 122888 | tf_op jit(solution)/shard_map/ppermute | solution.py:21
  103.4 2.3 %collective-permute-start.9 = (f32[5,16,128]{2,1,0:T(8,128)S(1)}, f32[5,16,128]{2,1,0:T(8,128)S(1)}, u32[]{:S(2)}, u32[]{:S(2)}) collective-permute-start(f32[5,16,128]{2,1,0:T(8,128)S(1)} %bitcast.224), channel_id=1, source_target_pairs={{8,0},{16,8},{24,16},{32,24},{40,32},{48,40},{56,48},{0,56},{9,1},... | collective-permute-start | bytes 122888 | tf_op jit(solution)/shard_map/ppermute | solution.py:21
  103.4 5.5 %collective-permute-start.8 = (f32[5,16,128]{2,1,0:T(8,128)S(1)}, f32[5,16,128]{2,1,0:T(8,128)S(1)}, u32[]{:S(2)}, u32[]{:S(2)}) collective-permute-start(f32[5,16,128]{2,1,0:T(8,128)S(1)} %bitcast.223), channel_id=1, source_target_pairs={{0,8},{8,16},{16,24},{24,32},{32,40},{40,48},{48,56},{56,0},{1,9},... | collective-permute-start | bytes 122888 | tf_op jit(solution)/shard_map/ppermute | solution.py:21
  120.6 7.2 %copy-start.3 = (s32[1,512]{1,0:T(1,128)S(1)}, s32[1,512]{1,0:T(1,128)}, u32[]{:S(2)}) copy-start(s32[1,512]{1,0:T(1,128)} %param.6) | copy-start | bytes 6148
  120.6 41.5 %all-to-all-start.1 = ((f32[64,2,2560]{2,1,0:T(2,128)}), f32[64,2,2560]{2,1,0:T(2,128)S(1)}, u32[]{:S(2)}, u32[]{:S(2)}) async-start(f32[64,2,2560]{2,1,0:T(2,128)} %reshape.480), calls=%async_computation.1 | async-start | bytes 2621440 | tf_op jit(solution)/shard_map/all_to_all | solution.py:217
where the time goes:
time: 165 us; the launch traced here: 164 us
  waiting for transfers between devices  69.7 us (42%)
  local copies, waits for them, and re-layouts  34.7 us (21%)
  starting transfers between devices  34 us (21%)
  other arithmetic  10.1 us (6%)
  Pallas kernels  9.02 us (5%)
  matrix products  5.55 us (3%)
    all_to_all x1, waiting for transfers between devices, shards(): returned = lax.all_to_all(back, ('gy', 'gz'), 0, 0, tiled=True)  34.1 us
    all_to_all x1, waiting for transfers between devices, shards(): incoming = lax.all_to_all(outgoing, ('gy', 'gz'), 0, 0, tiled=True)  31.9 us
    ppermute x12, starting transfers between devices, shift_in(): return lax.ppermute(plane, axis, pairs)  14.7 us
    all_to_all x1, starting transfers between devices, shards(): incoming = lax.all_to_all(outgoing, ('gy', 'gz'), 0, 0, tiled=True)  12.2 us
    pallas_call x2, Pallas kernels, substep(): pl.pallas_call(substep_kernel, out_shape=jax.ShapeDtypeStruct(state.shape...  9.02 us
    all_to_all x1, starting transfers between devices, shards(): returned = lax.all_to_all(back, ('gy', 'gz'), 0, 0, tiled=True)  7.01 us
    dot_general x7, matrix products, exact_dot(): jnp.einsum(spec, *ops, precision=lax.Precision.HIGHEST, preferred_element...  5.55 us
    unnamed x27, local copies, waits for them, and re-layouts  5.36 us
  transfers between devices with their start and end apart: 14, of which 5 were waited for; matrix products, arithmetic and copies ran while one was open for 16% of the time, Pallas kernels for 0%

commit v1 on v0

--- a/solution.py
+++ b/solution.py
@@ -6,7 +6,6 @@
 from jax.sharding import PartitionSpec as P
 
 BS = 16
-CAP = 2
 
 GAMMA = 1.4
 LAMBDA = 0.05
@@ -161,45 +160,67 @@
     return means.transpose(3, 0, 1, 2, 4).reshape(nblk, -1)
 
 
-def routes(parent_row, nblk):
-    ndev = parent_row.shape[0] // nblk
-    owner = (parent_row // nblk).reshape(ndev, nblk)
-    slot = (parent_row % nblk).reshape(ndev, nblk)
-    pos = jnp.arange(nblk, dtype=jnp.int32)
-    same = owner[:, :, None] == owner[:, None, :]
-    earlier = (pos[None, :] < pos[:, None])[None]
-    rank = jnp.sum((same & earlier).astype(jnp.int32), axis=2)
-    return owner, slot, rank
+def pick(table, index):
+    flat = table.reshape((-1,) + table.shape[2:])
+    return jnp.take(flat, index.reshape(-1), axis=0, mode="clip").reshape(
+        index.shape + table.shape[2:]
+    )
+
+
+def select(mask, value):
+    return jnp.sum(jnp.where(mask, value, 0), axis=-1)
 
 
 def shards(fine, shell, parent, link):
-    half = BS // 2
     nz_dev = fine.shape[3]
     nblk = nz_dev // BS
-    me = lax.axis_index("gy") * lax.axis_size("gz") + lax.axis_index("gz")
+    rows = lax.axis_size("gy")
+    cols = lax.axis_size("gz")
+    my = lax.axis_index("gy")
+    mz = lax.axis_index("gz")
+    me = my * cols + mz
     parent_row = parent[0]
-    ndev = parent_row.shape[0] // nblk
+    count = parent_row.shape[0]
     links = link[:, 0, 0, :].T
     width = shell.shape[2] // 2
-    owner, slot, rank = routes(parent_row, nblk)
-
-    mine = owner == me
-    picks = jnp.stack(
-        [jnp.sum(jnp.where(mine & (rank == c), slot, 0), axis=1) for c in range(CAP)], axis=1
-    )
+
+    item = jnp.arange(count, dtype=jnp.int32)
+    dev = item // nblk
+    d_row = dev // cols
+    d_col = dev % cols
+    owner = parent_row // nblk
+    slot = parent_row % nblk
+    o_row = owner // cols
+    o_col = owner % cols
+    before = item[None, :] < item[:, None]
+    rank1 = jnp.sum(
+        (before & (owner[None, :] == owner[:, None]) & (d_row[None, :] == d_row[:, None])).astype(
+            jnp.int32
+        ),
+        axis=1,
+    )
+    rank2 = jnp.sum(
+        (before & (dev[None, :] == dev[:, None]) & (o_col[None, :] == o_col[:, None])).astype(
+            jnp.int32
+        ),
+        axis=1,
+    )
+    peer_r = jnp.arange(rows, dtype=jnp.int32)[:, None, None]
+    peer_c = jnp.arange(cols, dtype=jnp.int32)[:, None, None]
+    cell = jnp.arange(nblk, dtype=jnp.int32)[None, :, None]
+    via_me = (d_row == my) & (o_col == mz)
+
     local = shell[0]
     levels = jnp.concatenate(
         [local[:, :width], 0.5 * (local[:, :width] + local[:, width:])], axis=1
     )
-    outgoing = jnp.take(levels, picks.reshape(-1), axis=0, mode="clip").reshape(
-        ndev, CAP, levels.shape[1]
-    )
-    incoming = lax.all_to_all(outgoing, ("gy", "gz"), 0, 0, tiled=True)
-    my_owner = lax.dynamic_index_in_dim(owner, me, keepdims=False)
-    my_rank = lax.dynamic_index_in_dim(rank, me, keepdims=False)
-    fetched = jnp.take(
-        incoming.reshape(ndev * CAP, -1), my_owner * CAP + my_rank, axis=0, mode="clip"
-    )
+    first = select((owner == me) & (d_row == peer_r) & (rank1 == cell), slot)
+    stage = lax.all_to_all(pick(levels[None], first), "gy", 0, 0, tiled=True)
+    second = select(via_me & (d_col == peer_c) & (rank2 == cell), o_row * nblk + rank1)
+    stage = lax.all_to_all(pick(stage, second), "gz", 0, 0, tiled=True)
+    mine = lax.dynamic_slice_in_dim(item, me * nblk, nblk)
+    fetched = pick(stage, o_col[mine] * nblk + rank2[mine])
+
     side, ends = coarse_faces(fetched, nblk)
     state = fine
     for step in range(2):
@@ -207,20 +228,15 @@
     restricted = restrict_state(state, nblk)
 
     pos = jnp.arange(nblk, dtype=jnp.int32)
-    dest = jnp.arange(ndev, dtype=jnp.int32)[:, None, None]
-    cell = jnp.arange(CAP, dtype=jnp.int32)[None, :, None]
-    hit = (my_owner[None, None, :] == dest) & (my_rank[None, None, :] == cell)
-    which = jnp.sum(jnp.where(hit, pos[None, None, :], 0), axis=2)
-    back = jnp.take(restricted, which.reshape(-1), axis=0, mode="clip").reshape(
-        ndev, CAP, restricted.shape[1]
-    )
-    returned = lax.all_to_all(back, ("gy", "gz"), 0, 0, tiled=True)
+    back = select(
+        (o_col[mine][None, None, :] == peer_c) & (rank2[mine][None, None, :] == cell), pos
+    )
+    stage = lax.all_to_all(pick(restricted[None], back), "gz", 0, 0, tiled=True)
+    home = select(via_me & (o_row == peer_r) & (rank1 == cell), d_col * nblk + rank2)
+    stage = lax.all_to_all(pick(stage, home), "gy", 0, 0, tiled=True)
     target = me * nblk + pos
-    source = (jnp.arange(ndev * nblk, dtype=jnp.int32) // nblk) * CAP + rank.reshape(-1)
-    match = parent_row[None, :] == target[:, None]
-    origin = jnp.sum(jnp.where(match, source[None, :], 0), axis=1)
-    gathered = jnp.take(returned.reshape(ndev * CAP, -1), origin, axis=0, mode="clip")
-    coarse_new = gathered.reshape(1, nblk, restricted.shape[1])
+    origin = select(parent_row[None, :] == target[:, None], d_row * nblk + rank1)
+    coarse_new = pick(stage, origin).reshape(1, nblk, restricted.shape[1])
     return (state, coarse_new)
 
 

time: 165 us -> 152 us (0.921)
  waiting for transfers between devices: 69.7 us -> 53.9 us
  starting transfers between devices: 34 us -> 39.9 us
  local copies, waits for them, and re-layouts: 34.7 us -> 29.9 us
    all_to_all x2 -> x4, waiting for transfers between devices: 66 us -> 49.8 us  [the longest x1 20.9 us: shards(): stage = lax.all_to_all(pick(stage, home), 'gy', 0, 0, tiled=True)]
    reshape x6 -> x0, local copies, waits for them, and re-layouts: 8.61 us -> none  [the longest x1 2.64 us: shards(): incoming.reshape(ndev * CAP, -1)]
    all_to_all x2 -> x4, starting transfers between devices: 19.2 us -> 25.2 us  [the longest x1 8.6 us: shards(): stage = lax.all_to_all(pick(levels[None], first), 'gy', 0, 0, tiled=True)]
    gather x4 -> x8, local copies, waits for them, and re-layouts: 5.82 us -> 10.1 us  [the longest x6 8.83 us: pick(): jnp.take(flat, index.reshape(-1), axis=0, mode='clip')]
    unnamed x27 -> x26, local copies, waits for them, and re-layouts: 5.36 us -> 3.78 us
  transfers between devices with their start and end apart: 14 -> 16, of which waited for: 5 -> 7; matrix products, arithmetic and copies ran while one was open for 16% -> 16% of each run, Pallas kernels for 0% -> 0%
where the time goes in v1:
time: 152 us; the launch traced here: 151 us
  waiting for transfers between devices  53.9 us (35%)
  starting transfers between devices  39.9 us (26%)
  local copies, waits for them, and re-layouts  29.9 us (20%)
  other arithmetic  11.5 us (8%)
  Pallas kernels  9.03 us (6%)
  matrix products  5.55 us (4%)
    all_to_all x1, waiting for transfers between devices, shards(): stage = lax.all_to_all(pick(stage, home), 'gy', 0, 0, tiled=True)  20.9 us
    ppermute x12, starting transfers between devices, shift_in(): return lax.ppermute(plane, axis, pairs)  14.6 us
    all_to_all x1, waiting for transfers between devices, shards(): stage = lax.all_to_all(pick(levels[None], first), 'gy', 0, 0, tiled=True)  13.4 us
    pallas_call x2, Pallas kernels, substep(): pl.pallas_call(substep_kernel, out_shape=jax.ShapeDtypeStruct(state.shape...  9.03 us
    gather x6, local copies, waits for them, and re-layouts, pick(): jnp.take(flat, index.reshape(-1), axis=0, mode='clip')  8.83 us
    all_to_all x1, starting transfers between devices, shards(): stage = lax.all_to_all(pick(levels[None], first), 'gy', 0, 0, tiled=True)  8.6 us
    all_to_all x1, waiting for transfers between devices, shards(): stage = lax.all_to_all(pick(stage, second), 'gz', 0, 0, tiled=True)  8.31 us
    all_to_all x1, waiting for transfers between devices, shards(): stage = lax.all_to_all(pick(restricted[None], back), 'gz', 0, 0, tiled=True)  7.25 us
  transfers between devices with their start and end apart: 16, of which 7 were waited for; matrix products, arithmetic and copies ran while one was open for 16% of the time, Pallas kernels for 0%

profile of v1, /device:TPU:8, one launch (start us, length us, event | category | flops | bytes accessed | tf_op | source)
XLA Modules:
  0.0 150.9 jit_solution(4059175581458044803)
XLA Ops:
  0.7 0.7 and_select_fusion
  1.4 0.7 add_select_fusion.3
  2.1 0.7 broadcast_compare_fusion
  4.2 0.9 fusion.72
  5.0 1.9 %gather_fusion = f32[64,3840]{1,0:T(8,128)} fusion(f32[8,3840]{1,0:T(8,128)S(1)} %pad_maximum_fusion, s32[1024]{0:T(1024)S(1)} %pad_clamp_fusion.6), kind=kCustom, calls=%fused_computation | custom fusion | bytes 1966336 | tf_op jit(solution)/shard_map/jit(_take)/gather | solution.py:165
  6.9 8.6 %all-to-all-start = ((f32[8,8,3840]{2,1,0:T(8,128)}), f32[8,8,3840]{2,1,0:T(8,128)S(1)}, u32[]{:S(2)}, u32[]{:S(2)}) async-start(f32[8,8,3840]{2,1,0:T(8,128)} %bitcast.8), calls=%async_computation | async-start | bytes 1966080 | tf_op jit(solution)/shard_map/all_to_all | solution.py:218
  15.5 0.7 fusion.71
  16.2 3.9 %collective-permute-start.3 = (f32[5,16,128]{2,1,0:T(8,128)}, f32[5,16,128]{2,1,0:T(8,128)}, u32[]{:S(2)}, u32[]{:S(2)}) collective-permute-start(f32[5,16,128]{2,1,0:T(8,128)} %bitcast.28), channel_id=1, source_target_pairs={{8,0},{16,8},{24,16},{32,24},{40,32},{48,40},{56,48},{0,56},{9,1},... | collective-permute-start | bytes 122888 | tf_op jit(solution)/shard_map/ppermute | solution.py:20
  20.7 1.5 collective-permute-start
  22.2 1.7 %collective-permute-start.1 = (f32[5,16,128]{2,1,0:T(8,128)S(1)}, f32[5,16,128]{2,1,0:T(8,128)}, u32[]{:S(2)}, u32[]{:S(2)}) collective-permute-start(f32[5,16,128]{2,1,0:T(8,128)S(1)} %get-tuple-element.23), channel_id=1, source_target_pairs={{64,0},{128,64},{192,128},{0,192},{65,1},{129,65},{193,129},{1,193... | collective-permute-start | bytes 122888 | tf_op jit(solution)/shard_map/ppermute | solution.py:20
  24.2 1.2 copy.81
  26.5 0.7 gather_fusion.3
  27.9 0.7 broadcast_in_dim.241
  30.8 13.4 %all-to-all-done = f32[8,8,3840]{2,1,0:T(8,128)S(1)} async-done(((f32[8,8,3840]{2,1,0:T(8,128)}), f32[8,8,3840]{2,1,0:T(8,128)S(1)}, u32[]{:S(2)}, u32[]{:S(2)}) %all-to-all-start) | async-done | bytes 983072 | tf_op jit(solution)/shard_map/all_to_all | solution.py:218
  44.1 1.9 %gather_fusion.1 = f32[64,3840]{1,0:T(8,128)} fusion(f32[64,3840]{1,0:T(8,128)S(1)} %bitcast.226, s32[1024]{0:T(1024)S(1)} %pad_clamp_fusion.5), kind=kCustom, calls=%fused_computation.1 | custom fusion | bytes 1966336 | tf_op jit(solution)/shard_map/jit(_take)/gather | solution.py:165
  46.0 4.9 %all-to-all-start.1 = ((f32[8,8,3840]{2,1,0:T(8,128)}), f32[8,8,3840]{2,1,0:T(8,128)S(1)}, u32[]{:S(2)}, u32[]{:S(2)}) async-start(f32[8,8,3840]{2,1,0:T(8,128)} %bitcast.11), calls=%async_computation.1 | async-start | bytes 1966080 | tf_op jit(solution)/shard_map/all_to_all | solution.py:220
  51.2 1.2 copy.79
  53.6 8.3 %all-to-all-done.1 = f32[8,8,3840]{2,1,0:T(8,128)S(1)} async-done(((f32[8,8,3840]{2,1,0:T(8,128)}), f32[8,8,3840]{2,1,0:T(8,128)S(1)}, u32[]{:S(2)}, u32[]{:S(2)}) %all-to-all-start.1) | async-done | bytes 983072 | tf_op jit(solution)/shard_map/all_to_all | solution.py:220
  62.5 1.1 reshape.762
  63.7 1.2 copy-done
  64.8 0.8 copy.51
  66.0 0.7 slice-done
  68.0 0.7 fusion.46
  69.3 1.3 collective-permute-start.4
  70.6 0.9 fusion.28
  71.5 2.3 %fusion.52 = f32[2,2,5,16,16,128]{5,4,3,2,1,0:T(8,128)S(1)} fusion(f32[2,2,5,8,16,16]{5,3,4,2,1,0:T(8,128)S(1)} %fusion.46, s32[128]{0:T(128)S(1)} %copy-done.10), kind=kOutput, calls=%fused_computation.118 | convolution fusion | flops 62915584 | bytes 2785792 | tf_op jit(solution)/shard_map/ax,by,lkfabc,cz->lkfxyz/dot_general | solution.py:103
  74.5 0.7 copy.59.gy_ref
  75.2 2.0 %fusion.8.zfix_ref = f32[5,16,16,128]{3,2,1,0:T(8,128)} fusion(f32[2,2,5,16,16,128]{5,4,3,2,1,0:T(8,128)S(1)} %fusion.52, f32[5,16,16]{2,1,0:T(8,128)} %collective-permute-done.5, f32[5,16,16]{2,1,0:T(8,128)S(1)} %collective-permute-done.4, pred[128]{0:T(512)(128)(4,1)S(1)} %get-tuple-element.46, pred[128]{0:T(512)(128)(4,1)S(1)} %get-tuple-element.47, ...), kind=kLoop, calls=%fused_computation.27 | loop fusion | flops 491520 | bytes 1976704 | tf_op jit(solution)/shard_map/jit(_where)/select_n | solution.py:142
  77.8 4.5 %shard_map.59.u_ref = f32[5,16,16,128]{3,2,1,0:T(8,128)} custom-call(f32[5,16,16,128]{3,2,1,0:T(8,128)} %u_ref.1, f32[2,5,16,128]{3,2,1,0:T(8,128)} %pad_maximum_fusion.1.gx_ref, f32[2,16,5,1,128]{4,3,2,1,0:T(1,128)} %copy.59.gy_ref, f32[5,16,16,128]{3,2,1,0:T(8,128)} %fusion.8.zfix_ref, s32[2,16,128]{2,1,0:T(8,128)} %broadcast_in_dim.253.zflag_ref), custom_call_target="tpu_custom_call" | custom-call | tf_op jit(solution)/shard_map/pallas_call | solution.py:92
  82.3 1.9 %slice_reduce_fusion.1 = (f32[5,16,16]{2,1,0:T(8,128)S(1)}, f32[5,16,16]{2,1,0:T(8,128)S(1)}) fusion(f32[5,16,16,128]{3,2,1,0:T(8,128)} %shard_map.59.u_ref), kind=kLoop, calls=%fused_computation.24 | loop fusion | bytes 20480 | tf_op jit(solution)/shard_map/slice | solution.py:133
  84.3 1.1 fusion.69
  85.4 1.5 collective-permute-start.10
  87.5 0.8 slice_bitcast_fusion.13
  88.3 1.5 collective-permute-start.6
  89.8 1.7 %collective-permute-start.7 = (f32[5,16,128]{2,1,0:T(8,128)S(1)}, f32[5,16,128]{2,1,0:T(8,128)S(1)}, u32[]{:S(2)}, u32[]{:S(2)}) collective-permute-start(f32[5,16,128]{2,1,0:T(8,128)S(1)} %get-tuple-element.17), channel_id=1, source_target_pairs={{64,0},{128,64},{192,128},{0,192},{65,1},{129,65},{193,129},{1,193... | collective-permute-start | bytes 122888 | tf_op jit(solution)/shard_map/ppermute | solution.py:20
  92.1 1.3 fusion.5.zfix_ref
  93.8 3.6 %collective-permute-done.8 = f32[5,16,128]{2,1,0:T(8,128)S(1)} collective-permute-done((f32[5,16,128]{2,1,0:T(8,128)S(1)}, f32[5,16,128]{2,1,0:T(8,128)S(1)}, u32[]{:S(2)}, u32[]{:S(2)}) %collective-permute-start.8) | collective-permute-done | bytes 40992 | tf_op jit(solution)/shard_map/ppermute | solution.py:20
  97.4 0.7 copy.64.gy_ref
  98.8 4.5 %shard_map.60 = f32[5,16,16,128]{3,2,1,0:T(8,128)} custom-call(f32[5,16,16,128]{3,2,1,0:T(8,128)} %shard_map.59.u_ref, f32[2,5,16,128]{3,2,1,0:T(8,128)} %pad_maximum_fusion.2.gx_ref, f32[2,16,5,1,128]{4,3,2,1,0:T(1,128)} %copy.64.gy_ref, f32[5,16,16,128]{3,2,1,0:T(8,128)} %fusion.5.zfix_ref, s32[2,16,128]{2,1,0:T(8,128)} %broadcast_in_dim.253.zflag_ref), custom_call_target="tpu_custom_call" | custom-call | tf_op jit(solution)/shard_map/pallas_call | solution.py:92
  103.3 1.3 fusion.14
  105.5 0.7 reshape_broadcast_in_dim_reshape.3
  106.2 1.6 %gather_fusion.5 = f32[64,2560]{1,0:T(8,128)} fusion(f32[8,2560]{1,0:T(8,128)S(1)} %reshape_broadcast_in_dim_reshape.3, s32[1024]{0:T(1024)S(1)} %pad_clamp_fusion.2), kind=kCustom, calls=%fused_computation.5 | custom fusion | bytes 1310976 | tf_op jit(solution)/shard_map/jit(_take)/gather | solution.py:165
  107.8 7.2 %all-to-all-start.2 = ((f32[8,8,2560]{2,1,0:T(8,128)}), f32[8,8,2560]{2,1,0:T(8,128)S(1)}, u32[]{:S(2)}, u32[]{:S(2)}) async-start(f32[8,8,2560]{2,1,0:T(8,128)} %bitcast.67), calls=%async_computation.2 | async-start | bytes 1310720 | tf_op jit(solution)/shard_map/all_to_all | solution.py:234
  115.1 7.2 %all-to-all-done.2 = f32[8,8,2560]{2,1,0:T(8,128)S(1)} async-done(((f32[8,8,2560]{2,1,0:T(8,128)}), f32[8,8,2560]{2,1,0:T(8,128)S(1)}, u32[]{:S(2)}, u32[]{:S(2)}) %all-to-all-start.2) | async-done | bytes 655392 | tf_op jit(solution)/shard_map/all_to_all | solution.py:234
  122.3 1.6 %gather_fusion.6 = f32[64,2560]{1,0:T(8,128)} fusion(f32[64,2560]{1,0:T(8,128)S(1)} %bitcast.227, s32[1024]{0:T(1024)S(1)} %pad_clamp_fusion.1), kind=kCustom, calls=%fused_computation.6 | custom fusion | bytes 1310976 | tf_op jit(solution)/shard_map/jit(_take)/gather | solution.py:165
  124.0 4.6 %all-to-all-start.3 = ((f32[8,8,2560]{2,1,0:T(8,128)}), f32[8,8,2560]{2,1,0:T(8,128)S(1)}, u32[]{:S(2)}, u32[]{:S(2)}) async-start(f32[8,8,2560]{2,1,0:T(8,128)} %bitcast.69), calls=%async_computation.3 | async-start | bytes 1310720 | tf_op jit(solution)/shard_map/all_to_all | solution.py:236
  128.7 20.9 %all-to-all-done.3 = f32[8,8,2560]{2,1,0:T(8,128)S(1)} async-done(((f32[8,8,2560]{2,1,0:T(8,128)}), f32[8,8,2560]{2,1,0:T(8,128)S(1)}, u32[]{:S(2)}, u32[]{:S(2)}) %all-to-all-start.3) | async-done | bytes 655392 | tf_op jit(solution)/shard_map/all_to_all | solution.py:236
  149.7 1.2 gather_fusion.7
  (115 shorter events, 15.3 us)
Async XLA Ops:
  6.9 8.6 %copy-start.1 = (f32[5,16,16,128]{3,2,1,0:T(8,128)S(1)}, f32[5,16,16,128]{3,2,1,0:T(8,128)}, u32[]{:S(2)}) copy-start(f32[5,16,16,128]{3,2,1,0:T(8,128)} %u_ref.1) | copy-start | bytes 1966084
  6.9 37.2 %all-to-all-start = ((f32[8,8,3840]{2,1,0:T(8,128)}), f32[8,8,3840]{2,1,0:T(8,128)S(1)}, u32[]{:S(2)}, u32[]{:S(2)}) async-start(f32[8,8,3840]{2,1,0:T(8,128)} %bitcast.8), calls=%async_computation | async-start | bytes 1966080 | tf_op jit(solution)/shard_map/all_to_all | solution.py:218
  16.2 53.1 %collective-permute-start.3 = (f32[5,16,128]{2,1,0:T(8,128)}, f32[5,16,128]{2,1,0:T(8,128)}, u32[]{:S(2)}, u32[]{:S(2)}) collective-permute-start(f32[5,16,128]{2,1,0:T(8,128)} %bitcast.28), channel_id=1, source_target_pairs={{8,0},{16,8},{24,16},{32,24},{40,32},{48,40},{56,48},{0,56},{9,1},... | collective-permute-start | bytes 122888 | tf_op jit(solution)/shard_map/ppermute | solution.py:20
  20.1 50.5 %collective-permute-start.2 = (f32[5,16,128]{2,1,0:T(8,128)S(1)}, f32[5,16,128]{2,1,0:T(8,128)}, u32[]{:S(2)}, u32[]{:S(2)}) collective-permute-start(f32[5,16,128]{2,1,0:T(8,128)S(1)} %bitcast.234), channel_id=1, source_target_pairs={{0,8},{8,16},{16,24},{24,32},{32,40},{40,48},{48,56},{56,0},{1,9},... | collective-permute-start | bytes 122888 | tf_op jit(solution)/shard_map/ppermute | solution.py:20
  20.7 49.9 %collective-permute-start = (f32[5,16,128]{2,1,0:T(8,128)}, f32[5,16,128]{2,1,0:T(8,128)}, u32[]{:S(2)}, u32[]{:S(2)}) collective-permute-start(f32[5,16,128]{2,1,0:T(8,128)} %get-tuple-element.22), channel_id=1, source_target_pairs={{0,64},{64,128},{128,192},{192,0},{1,65},{65,129},{129,193},{193,1... | collective-permute-start | bytes 122888 | tf_op jit(solution)/shard_map/ppermute | solution.py:20
  22.2 48.4 %collective-permute-start.1 = (f32[5,16,128]{2,1,0:T(8,128)S(1)}, f32[5,16,128]{2,1,0:T(8,128)}, u32[]{:S(2)}, u32[]{:S(2)}) collective-permute-start(f32[5,16,128]{2,1,0:T(8,128)S(1)} %get-tuple-element.23), channel_id=1, source_target_pairs={{64,0},{128,64},{192,128},{0,192},{65,1},{129,65},{193,129},{1,193... | collective-permute-start | bytes 122888 | tf_op jit(solution)/shard_map/ppermute | solution.py:20
  24.2 3.0 %copy-start.4 = (s32[6,1,1,8]{3,2,1,0:T(1,128)S(1)}, s32[6,1,1,8]{3,2,1,0:T(1,128)}, u32[]{:S(2)}) copy-start(s32[6,1,1,8]{3,2,1,0:T(1,128)} %param.7) | copy-start | bytes 580
  25.3 49.9 %collective-permute-start.5 = (f32[5,16,16]{2,1,0:T(8,128)}, f32[5,16,16]{2,1,0:T(8,128)}, u32[]{:S(2)}, u32[]{:S(2)}) collective-permute-start(f32[5,16,16]{2,1,0:T(8,128)} %bitcast.42), channel_id=1, source_target_pairs={{1,0},{2,1},{3,2},{4,3},{5,4},{6,5},{7,6},{0,7},{9,8},{10,9},{11,1... | collective-permute-start | bytes 15368 | tf_op jit(solution)/shard_map/ppermute | solution.py:20
  46.0 15.8 %all-to-all-start.1 = ((f32[8,8,3840]{2,1,0:T(8,128)}), f32[8,8,3840]{2,1,0:T(8,128)S(1)}, u32[]{:S(2)}, u32[]{:S(2)}) async-start(f32[8,8,3840]{2,1,0:T(8,128)} %bitcast.11), calls=%async_computation.1 | async-start | bytes 1966080 | tf_op jit(solution)/shard_map/all_to_all | solution.py:220
  63.5 1.3 copy-start
  65.6 1.1 slice-start
  67.9 1.4 copy-start.2
  67.9 2.7 %copy-start.5 = (pred[128]{0:T(512)(128)(4,1)S(1)}, pred[128]{0:T(512)(128)(4,1)}, u32[]{:S(2)}) copy-start(pred[128]{0:T(512)(128)(4,1)} %broadcast_in_dim.241) | copy-start | bytes 388
  67.9 2.7 %copy-start.6 = (pred[128]{0:T(512)(128)(4,1)S(1)}, pred[128]{0:T(512)(128)(4,1)}, u32[]{:S(2)}) copy-start(pred[128]{0:T(512)(128)(4,1)} %broadcast_in_dim.238) | copy-start | bytes 388
  67.9 2.7 %copy-start.7 = (pred[128]{0:T(512)(128)(4,1)S(1)}, pred[128]{0:T(512)(128)(4,1)}, u32[]{:S(2)}) copy-start(pred[128]{0:T(512)(128)(4,1)} %broadcast_in_dim.235) | copy-start | bytes 388
  68.0 2.7 %copy-start.8 = (pred[128]{0:T(512)(128)(4,1)S(1)}, pred[128]{0:T(512)(128)(4,1)}, u32[]{:S(2)}) copy-start(pred[128]{0:T(512)(128)(4,1)} %broadcast_in_dim.226) | copy-start | bytes 388
  68.7 2.8 %copy-start.10 = (s32[128]{0:T(128)S(1)}, s32[128]{0:T(128)}, u32[]{:S(2)}) copy-start(s32[128]{0:T(128)} %and_select_fusion.3) | copy-start | bytes 1540
  69.3 5.8 %collective-permute-start.4 = (f32[5,16,16]{2,1,0:T(8,128)S(1)}, f32[5,16,16]{2,1,0:T(8,128)S(1)}, u32[]{:S(2)}, u32[]{:S(2)}) collective-permute-start(f32[5,16,16]{2,1,0:T(8,128)S(1)} %bitcast.237), channel_id=1, source_target_pairs={{0,1},{1,2},{2,3},{3,4},{4,5},{5,6},{6,7},{7,0},{8,9},{9,10},{10,1... | collective-permute-start | bytes 15368 | tf_op jit(solution)/shard_map/ppermute | solution.py:20
  71.5 3.6 %copy-start.9 = (pred[128]{0:T(512)(128)(4,1)S(1)}, pred[128]{0:T(512)(128)(4,1)}, u32[]{:S(2)}) copy-start(pred[128]{0:T(512)(128)(4,1)} %fusion.66) | copy-start | bytes 388
  85.4 6.2 %collective-permute-start.10 = (f32[5,16,16]{2,1,0:T(8,128)S(1)}, f32[5,16,16]{2,1,0:T(8,128)S(1)}, u32[]{:S(2)}, u32[]{:S(2)}) collective-permute-start(f32[5,16,16]{2,1,0:T(8,128)S(1)} %get-tuple-element.2), channel_id=1, source_target_pairs={{0,1},{1,2},{2,3},{3,4},{4,5},{5,6},{6,7},{7,0},{8,9},{9,10},{10,1... | collective-permute-start | bytes 15368 | tf_op jit(solution)/shard_map/ppermute | solution.py:20
  86.9 5.2 %collective-permute-start.11 = (f32[5,16,16]{2,1,0:T(8,128)S(1)}, f32[5,16,16]{2,1,0:T(8,128)S(1)}, u32[]{:S(2)}, u32[]{:S(2)}) collective-permute-start(f32[5,16,16]{2,1,0:T(8,128)S(1)} %get-tuple-element.3), channel_id=1, source_target_pairs={{1,0},{2,1},{3,2},{4,3},{5,4},{6,5},{7,6},{0,7},{9,8},{10,9},{11,1... | collective-permute-start | bytes 15368 | tf_op jit(solution)/shard_map/ppermute | solution.py:20
  88.3 5.2 %collective-permute-start.6 = (f32[5,16,128]{2,1,0:T(8,128)S(1)}, f32[5,16,128]{2,1,0:T(8,128)S(1)}, u32[]{:S(2)}, u32[]{:S(2)}) collective-permute-start(f32[5,16,128]{2,1,0:T(8,128)S(1)} %get-tuple-element.16), channel_id=1, source_target_pairs={{0,64},{64,128},{128,192},{192,0},{1,65},{65,129},{129,193},{193,1... | collective-permute-start | bytes 122888 | tf_op jit(solution)/shard_map/ppermute | solution.py:20
  89.8 4.0 %collective-permute-start.7 = (f32[5,16,128]{2,1,0:T(8,128)S(1)}, f32[5,16,128]{2,1,0:T(8,128)S(1)}, u32[]{:S(2)}, u32[]{:S(2)}) collective-permute-start(f32[5,16,128]{2,1,0:T(8,128)S(1)} %get-tuple-element.17), channel_id=1, source_target_pairs={{64,0},{128,64},{192,128},{0,192},{65,1},{129,65},{193,129},{1,193... | collective-permute-start | bytes 122888 | tf_op jit(solution)/shard_map/ppermute | solution.py:20
  91.5 2.3 %collective-permute-start.9 = (f32[5,16,128]{2,1,0:T(8,128)S(1)}, f32[5,16,128]{2,1,0:T(8,128)S(1)}, u32[]{:S(2)}, u32[]{:S(2)}) collective-permute-start(f32[5,16,128]{2,1,0:T(8,128)S(1)} %bitcast.236), channel_id=1, source_target_pairs={{8,0},{16,8},{24,16},{32,24},{40,32},{48,40},{56,48},{0,56},{9,1},... | collective-permute-start | bytes 122888 | tf_op jit(solution)/shard_map/ppermute | solution.py:20
  91.6 5.9 %collective-permute-start.8 = (f32[5,16,128]{2,1,0:T(8,128)S(1)}, f32[5,16,128]{2,1,0:T(8,128)S(1)}, u32[]{:S(2)}, u32[]{:S(2)}) collective-permute-start(f32[5,16,128]{2,1,0:T(8,128)S(1)} %bitcast.235), channel_id=1, source_target_pairs={{0,8},{8,16},{16,24},{24,32},{32,40},{40,48},{48,56},{56,0},{1,9},... | collective-permute-start | bytes 122888 | tf_op jit(solution)/shard_map/ppermute | solution.py:20
  107.8 14.5 %all-to-all-start.2 = ((f32[8,8,2560]{2,1,0:T(8,128)}), f32[8,8,2560]{2,1,0:T(8,128)S(1)}, u32[]{:S(2)}, u32[]{:S(2)}) async-start(f32[8,8,2560]{2,1,0:T(8,128)} %bitcast.67), calls=%async_computation.2 | async-start | bytes 1310720 | tf_op jit(solution)/shard_map/all_to_all | solution.py:234
  124.0 4.6 %copy-start.3 = (s32[1,512]{1,0:T(1,128)S(1)}, s32[1,512]{1,0:T(1,128)}, u32[]{:S(2)}) copy-start(s32[1,512]{1,0:T(1,128)} %param.6) | copy-start | bytes 6148
  124.0 25.7 %all-to-all-start.3 = ((f32[8,8,2560]{2,1,0:T(8,128)}), f32[8,8,2560]{2,1,0:T(8,128)S(1)}, u32[]{:S(2)}, u32[]{:S(2)}) async-start(f32[8,8,2560]{2,1,0:T(8,128)} %bitcast.69), calls=%async_computation.3 | async-start | bytes 1310720 | tf_op jit(solution)/shard_map/all_to_all | solution.py:236

commit v2 on v1

--- a/solution.py
+++ b/solution.py
@@ -105,9 +105,9 @@
 
 def coarse_faces(fetched, nblk):
     half = BS // 2
-    lv = fetched.reshape(nblk, 2, 6, 5, half, half)
+    lv = fetched.reshape(nblk, -1, 6, 5, half, half)
     rows = replicate(half, BS)
-    side = lv[:, :, 0:4].transpose(1, 2, 3, 4, 0, 5).reshape(2, 4, 5, half, nblk * half)
+    side = lv[:, :, 0:4].transpose(1, 2, 3, 4, 0, 5).reshape(lv.shape[1], 4, 5, half, nblk * half)
     side = exact_dot("ay,lkfab,bz->lkfyz", rows, side, replicate(nblk * half, nblk * BS))
     ends = lv[:, :, 4:6].transpose(1, 2, 3, 4, 5, 0)
     ends = exact_dot("ax,by,lkfabc,cz->lkfxyz", rows, rows, ends, replicate(nblk, nblk * BS))
@@ -215,16 +215,19 @@
         [local[:, :width], 0.5 * (local[:, :width] + local[:, width:])], axis=1
     )
     first = select((owner == me) & (d_row == peer_r) & (rank1 == cell), slot)
-    stage = lax.all_to_all(pick(levels[None], first), "gy", 0, 0, tiled=True)
     second = select(via_me & (d_col == peer_c) & (rank2 == cell), o_row * nblk + rank1)
-    stage = lax.all_to_all(pick(stage, second), "gz", 0, 0, tiled=True)
     mine = lax.dynamic_slice_in_dim(item, me * nblk, nblk)
-    fetched = pick(stage, o_col[mine] * nblk + rank2[mine])
-
-    side, ends = coarse_faces(fetched, nblk)
+    last = o_col[mine] * nblk + rank2[mine]
+
+    def route(rows_of):
+        stage = lax.all_to_all(pick(rows_of[None], first), "gy", 0, 0, tiled=True)
+        stage = lax.all_to_all(pick(stage, second), "gz", 0, 0, tiled=True)
+        return pick(stage, last)
+
     state = fine
     for step in range(2):
-        state = substep(state, *ghost_inputs(state, side[step], ends[step], links))
+        side, ends = coarse_faces(route(levels[:, step * width : (step + 1) * width]), nblk)
+        state = substep(state, *ghost_inputs(state, side[0], ends[0], links))
     restricted = restrict_state(state, nblk)
 
     pos = jnp.arange(nblk, dtype=jnp.int32)

time: 152 us -> 164 us (1.079)
  starting transfers between devices: 39.9 us -> 53.8 us
  local copies, waits for them, and re-layouts: 29.9 us -> 26.9 us
  waiting for transfers between devices: 53.9 us -> 56.7 us
  other arithmetic: 11.5 us -> 8.79 us
    all_to_all x2 -> x4, starting transfers between devices: 13.5 us -> 24.5 us  [the longest x2 13.1 us: route(): stage = lax.all_to_all(pick(rows_of[None], first), 'gy', 0, 0, tiled=True)]
    ppermute x12, starting transfers between devices: 14.6 us -> 18.1 us  [shift_in(): return lax.ppermute(plane, axis, pairs)]
    gather x6 -> x9, local copies, waits for them, and re-layouts: 8.83 us -> 11.8 us  [pick(): jnp.take(flat, index.reshape(-1), axis=0, mode='clip')]
    unnamed x26 -> x15, local copies, waits for them, and re-layouts: 3.78 us -> 1.91 us
    all_to_all x2 -> x4, waiting for transfers between devices: 21.7 us -> 23 us  [the longest x2 18.2 us: route(): stage = lax.all_to_all(pick(rows_of[None], first), 'gy', 0, 0, tiled=True)]
    dot_general x7 -> x12, matrix products: 5.55 us -> 6.33 us  [exact_dot(): jnp.einsum(spec, *ops, precision=lax.Precision.HIGHEST, preferred_element...]
  transfers between devices with their start and end apart: 16 -> 18, of which waited for: 7 -> 9; matrix products, arithmetic and copies ran while one was open for 16% -> 18% of each run, Pallas kernels for 0% -> 3%
where the time goes in v2:
time: 164 us; the launch traced here: 163 us
  waiting for transfers between devices  56.7 us (35%)
  starting transfers between devices  53.8 us (33%)
  local copies, waits for them, and re-layouts  26.9 us (16%)
  Pallas kernels  9.03 us (6%)
  other arithmetic  8.79 us (5%)
  matrix products  6.33 us (4%)
    all_to_all x1, waiting for transfers between devices, shards(): stage = lax.all_to_all(pick(stage, home), 'gy', 0, 0, tiled=True)  20.9 us
    all_to_all x2, waiting for transfers between devices, route(): stage = lax.all_to_all(pick(rows_of[None], first), 'gy', 0, 0, tiled=True)  18.2 us
    ppermute x12, starting transfers between devices, shift_in(): return lax.ppermute(plane, axis, pairs)  18.1 us
    all_to_all x2, starting transfers between devices, route(): stage = lax.all_to_all(pick(rows_of[None], first), 'gy', 0, 0, tiled=True)  13.1 us
    gather x9, local copies, waits for them, and re-layouts, pick(): jnp.take(flat, index.reshape(-1), axis=0, mode='clip')  11.8 us
    all_to_all x2, starting transfers between devices, route(): stage = lax.all_to_all(pick(stage, second), 'gz', 0, 0, tiled=True)  11.4 us
    pallas_call x2, Pallas kernels, substep(): pl.pallas_call(substep_kernel, out_shape=jax.ShapeDtypeStruct(state.shape...  9.03 us
    all_to_all x1, starting transfers between devices, shards(): stage = lax.all_to_all(pick(restricted[None], back), 'gz', 0, 0, tiled=True)  7.55 us
  transfers between devices with their start and end apart: 18, of which 9 were waited for; matrix products, arithmetic and copies ran while one was open for 18% of the time, Pallas kernels for 3%

profile of v2, /device:TPU:8, one launch (start us, length us, event | category | flops | bytes accessed | tf_op | source)
XLA Modules:
  0.0 162.8 jit_solution(5158589637500506207)
XLA Ops:
  0.6 1.1 fusion.84
  1.9 0.7 and_select_fusion
  2.6 0.7 broadcast_compare_fusion
  3.7 0.7 add_select_fusion.3
  4.8 0.9 fusion.18
  6.3 1.5 gather_fusion
  7.8 9.6 %all-to-all-start = ((f32[8,8,1920]{2,1,0:T(8,128)}), f32[8,8,1920]{2,1,0:T(8,128)S(1)}, u32[]{:S(2)}, u32[]{:S(2)}) async-start(f32[8,8,1920]{2,1,0:T(8,128)} %bitcast.8), calls=%async_computation | async-start | bytes 983040 | tf_op jit(solution)/shard_map/all_to_all | solution.py:223
  17.4 3.9 %collective-permute-start.3 = (f32[5,16,128]{2,1,0:T(8,128)S(1)}, f32[5,16,128]{2,1,0:T(8,128)S(1)}, u32[]{:S(2)}, u32[]{:S(2)}) collective-permute-start(f32[5,16,128]{2,1,0:T(8,128)S(1)} %bitcast.258), channel_id=1, source_target_pairs={{8,0},{16,8},{24,16},{32,24},{40,32},{48,40},{56,48},{0,56},{9,1},... | collective-permute-start | bytes 122888 | tf_op jit(solution)/shard_map/ppermute | solution.py:20
  21.3 2.8 %collective-permute-start.1 = (f32[5,16,128]{2,1,0:T(8,128)S(1)}, f32[5,16,128]{2,1,0:T(8,128)S(1)}, u32[]{:S(2)}, u32[]{:S(2)}) collective-permute-start(f32[5,16,128]{2,1,0:T(8,128)S(1)} %get-tuple-element.23), channel_id=1, source_target_pairs={{64,0},{128,64},{192,128},{0,192},{65,1},{129,65},{193,129},{1,193... | collective-permute-start | bytes 122888 | tf_op jit(solution)/shard_map/ppermute | solution.py:20
  25.5 0.6 gather_fusion.3
  26.2 0.7 gather_fusion.2
  26.8 1.5 gather_fusion.5
  28.4 6.4 %all-to-all-done = f32[8,8,1920]{2,1,0:T(8,128)S(1)} async-done(((f32[8,8,1920]{2,1,0:T(8,128)}), f32[8,8,1920]{2,1,0:T(8,128)S(1)}, u32[]{:S(2)}, u32[]{:S(2)}) %all-to-all-start) | async-done | bytes 491552 | tf_op jit(solution)/shard_map/all_to_all | solution.py:223
  34.8 3.5 %all-to-all-start.2 = ((f32[8,8,1920]{2,1,0:T(8,128)}), f32[8,8,1920]{2,1,0:T(8,128)S(1)}, u32[]{:S(2)}, u32[]{:S(2)}) async-start(f32[8,8,1920]{2,1,0:T(8,128)} %bitcast.49), calls=%async_computation.2 | async-start | bytes 983040 | tf_op jit(solution)/shard_map/all_to_all | solution.py:223
  40.6 1.5 gather_fusion.1
  42.1 11.8 %all-to-all-done.2 = f32[8,8,1920]{2,1,0:T(8,128)S(1)} async-done(((f32[8,8,1920]{2,1,0:T(8,128)}), f32[8,8,1920]{2,1,0:T(8,128)S(1)}, u32[]{:S(2)}, u32[]{:S(2)}) %all-to-all-start.2) | async-done | bytes 491552 | tf_op jit(solution)/shard_map/all_to_all | solution.py:223
  54.0 6.3 %all-to-all-start.1 = ((f32[8,8,1920]{2,1,0:T(8,128)}), f32[8,8,1920]{2,1,0:T(8,128)S(1)}, u32[]{:S(2)}, u32[]{:S(2)}) async-start(f32[8,8,1920]{2,1,0:T(8,128)} %bitcast.11), calls=%async_computation.1 | async-start | bytes 983040 | tf_op jit(solution)/shard_map/all_to_all | solution.py:224
  60.4 1.5 gather_fusion.6
  61.9 4.8 %all-to-all-done.1 = f32[8,8,1920]{2,1,0:T(8,128)S(1)} async-done(((f32[8,8,1920]{2,1,0:T(8,128)}), f32[8,8,1920]{2,1,0:T(8,128)S(1)}, u32[]{:S(2)}, u32[]{:S(2)}) %all-to-all-start.1) | async-done | bytes 491552 | tf_op jit(solution)/shard_map/all_to_all | solution.py:224
  66.7 5.1 %all-to-all-start.3 = ((f32[8,8,1920]{2,1,0:T(8,128)}), f32[8,8,1920]{2,1,0:T(8,128)S(1)}, u32[]{:S(2)}, u32[]{:S(2)}) async-start(f32[8,8,1920]{2,1,0:T(8,128)} %bitcast.51), calls=%async_computation.3 | async-start | bytes 983040 | tf_op jit(solution)/shard_map/all_to_all | solution.py:224
  75.0 1.2 fusion.61
  76.6 1.7 %collective-permute-start.4 = (f32[5,16,16]{2,1,0:T(8,128)S(1)}, f32[5,16,16]{2,1,0:T(8,128)S(1)}, u32[]{:S(2)}, u32[]{:S(2)}) collective-permute-start(f32[5,16,16]{2,1,0:T(8,128)S(1)} %bitcast.263), channel_id=1, source_target_pairs={{0,1},{1,2},{2,3},{3,4},{4,5},{5,6},{6,7},{7,0},{8,9},{9,10},{10,1... | collective-permute-start | bytes 15368 | tf_op jit(solution)/shard_map/ppermute | solution.py:20
  78.3 0.6 pad_maximum_fusion.gx_ref
  79.0 0.7 copy.63.gy_ref
  79.7 1.1 collective-permute-done.4
  80.8 1.3 fusion.8.zfix_ref
  82.7 4.5 %shard_map.59.u_ref = f32[5,16,16,128]{3,2,1,0:T(8,128)} custom-call(f32[5,16,16,128]{3,2,1,0:T(8,128)} %u_ref.1, f32[2,5,16,128]{3,2,1,0:T(8,128)} %pad_maximum_fusion.gx_ref, f32[2,16,5,1,128]{4,3,2,1,0:T(1,128)} %copy.63.gy_ref, f32[5,16,16,128]{3,2,1,0:T(8,128)} %fusion.8.zfix_ref, s32[2,16,128]{2,1,0:T(8,128)} %broadcast_in_dim.262.zflag_ref), custom_call_target="tpu_custom_call" | custom-call | tf_op jit(solution)/shard_map/pallas_call | solution.py:92
  87.2 0.8 slice_bitcast_fusion.14
  88.0 1.1 fusion.82
  92.7 3.9 %collective-permute-start.9 = (f32[5,16,128]{2,1,0:T(8,128)S(1)}, f32[5,16,128]{2,1,0:T(8,128)S(1)}, u32[]{:S(2)}, u32[]{:S(2)}) collective-permute-start(f32[5,16,128]{2,1,0:T(8,128)S(1)} %bitcast.260), channel_id=1, source_target_pairs={{8,0},{16,8},{24,16},{32,24},{40,32},{48,40},{56,48},{0,56},{9,1},... | collective-permute-start | bytes 122888 | tf_op jit(solution)/shard_map/ppermute | solution.py:20
  96.6 2.8 %collective-permute-start.7 = (f32[5,16,128]{2,1,0:T(8,128)S(1)}, f32[5,16,128]{2,1,0:T(8,128)S(1)}, u32[]{:S(2)}, u32[]{:S(2)}) collective-permute-start(f32[5,16,128]{2,1,0:T(8,128)S(1)} %get-tuple-element.17), channel_id=1, source_target_pairs={{64,0},{128,64},{192,128},{0,192},{65,1},{129,65},{193,129},{1,193... | collective-permute-start | bytes 122888 | tf_op jit(solution)/shard_map/ppermute | solution.py:20
  100.5 2.3 %collective-permute-start.11 = (f32[5,16,16]{2,1,0:T(8,128)S(1)}, f32[5,16,16]{2,1,0:T(8,128)S(1)}, u32[]{:S(2)}, u32[]{:S(2)}) collective-permute-start(f32[5,16,16]{2,1,0:T(8,128)S(1)} %get-tuple-element.3), channel_id=1, source_target_pairs={{1,0},{2,1},{3,2},{4,3},{5,4},{6,5},{7,6},{0,7},{9,8},{10,9},{11,1... | collective-permute-start | bytes 15368 | tf_op jit(solution)/shard_map/ppermute | solution.py:20
  102.8 1.2 fusion.59
  104.6 2.2 %collective-permute-done.10 = f32[5,16,16]{2,1,0:T(8,128)S(1)} collective-permute-done((f32[5,16,16]{2,1,0:T(8,128)S(1)}, f32[5,16,16]{2,1,0:T(8,128)S(1)}, u32[]{:S(2)}, u32[]{:S(2)}) %collective-permute-start.10) | collective-permute-done | bytes 5152 | tf_op jit(solution)/shard_map/ppermute | solution.py:20
  106.8 1.3 fusion.5.zfix_ref
  108.2 1.7 %collective-permute-done.6 = f32[5,16,128]{2,1,0:T(8,128)S(1)} collective-permute-done((f32[5,16,128]{2,1,0:T(8,128)S(1)}, f32[5,16,128]{2,1,0:T(8,128)S(1)}, u32[]{:S(2)}, u32[]{:S(2)}) %collective-permute-start.6) | collective-permute-done | bytes 40992 | tf_op jit(solution)/shard_map/ppermute | solution.py:20
  109.9 0.7 copy.71.gy_ref
  110.6 0.6 pad_maximum_fusion.1.gx_ref
  111.2 4.5 %shard_map.60 = f32[5,16,16,128]{3,2,1,0:T(8,128)} custom-call(f32[5,16,16,128]{3,2,1,0:T(8,128)} %shard_map.59.u_ref, f32[2,5,16,128]{3,2,1,0:T(8,128)} %pad_maximum_fusion.1.gx_ref, f32[2,16,5,1,128]{4,3,2,1,0:T(1,128)} %copy.71.gy_ref, f32[5,16,16,128]{3,2,1,0:T(8,128)} %fusion.5.zfix_ref, s32[2,16,128]{2,1,0:T(8,128)} %broadcast_in_dim.262.zflag_ref), custom_call_target="tpu_custom_call" | custom-call | tf_op jit(solution)/shard_map/pallas_call | solution.py:92
  115.8 1.3 fusion.12
  118.0 0.7 reshape_broadcast_in_dim_reshape.3
  118.6 1.7 %gather_fusion.8 = f32[64,2560]{1,0:T(8,128)} fusion(f32[8,2560]{1,0:T(8,128)S(1)} %reshape_broadcast_in_dim_reshape.3, s32[1024]{0:T(1024)S(1)} %pad_clamp_fusion.2), kind=kCustom, calls=%fused_computation.8 | custom fusion | bytes 1310976 | tf_op jit(solution)/shard_map/jit(_take)/gather | solution.py:165
  120.3 7.6 %all-to-all-start.4 = ((f32[8,8,2560]{2,1,0:T(8,128)}), f32[8,8,2560]{2,1,0:T(8,128)S(1)}, u32[]{:S(2)}, u32[]{:S(2)}) async-start(f32[8,8,2560]{2,1,0:T(8,128)} %bitcast.80), calls=%async_computation.4 | async-start | bytes 1310720 | tf_op jit(solution)/shard_map/all_to_all | solution.py:237
  127.9 7.2 %all-to-all-done.4 = f32[8,8,2560]{2,1,0:T(8,128)S(1)} async-done(((f32[8,8,2560]{2,1,0:T(8,128)}), f32[8,8,2560]{2,1,0:T(8,128)S(1)}, u32[]{:S(2)}, u32[]{:S(2)}) %all-to-all-start.4) | async-done | bytes 655392 | tf_op jit(solution)/shard_map/all_to_all | solution.py:237
  135.1 1.7 %gather_fusion.9 = f32[64,2560]{1,0:T(8,128)} fusion(f32[64,2560]{1,0:T(8,128)S(1)} %bitcast.248, s32[1024]{0:T(1024)S(1)} %pad_clamp_fusion.1), kind=kCustom, calls=%fused_computation.9 | custom fusion | bytes 1310976 | tf_op jit(solution)/shard_map/jit(_take)/gather | solution.py:165
  136.8 3.7 %all-to-all-start.5 = ((f32[8,8,2560]{2,1,0:T(8,128)}), f32[8,8,2560]{2,1,0:T(8,128)S(1)}, u32[]{:S(2)}, u32[]{:S(2)}) async-start(f32[8,8,2560]{2,1,0:T(8,128)} %bitcast.82), calls=%async_computation.5 | async-start | bytes 1310720 | tf_op jit(solution)/shard_map/all_to_all | solution.py:239
  140.7 20.9 %all-to-all-done.5 = f32[8,8,2560]{2,1,0:T(8,128)S(1)} async-done(((f32[8,8,2560]{2,1,0:T(8,128)}), f32[8,8,2560]{2,1,0:T(8,128)S(1)}, u32[]{:S(2)}, u32[]{:S(2)}) %all-to-all-start.5) | async-done | bytes 655392 | tf_op jit(solution)/shard_map/all_to_all | solution.py:239
  161.6 1.2 gather_fusion.10
  (121 shorter events, 15.5 us)
Async XLA Ops:
  1.8 74.8 %collective-permute-start.2 = (f32[5,16,128]{2,1,0:T(8,128)S(1)}, f32[5,16,128]{2,1,0:T(8,128)S(1)}, u32[]{:S(2)}, u32[]{:S(2)}) collective-permute-start(f32[5,16,128]{2,1,0:T(8,128)S(1)} %bitcast.259), channel_id=1, source_target_pairs={{0,8},{8,16},{16,24},{24,32},{32,40},{40,48},{48,56},{56,0},{1,9},... | collective-permute-start | bytes 122888 | tf_op jit(solution)/shard_map/ppermute | solution.py:20
  6.3 15.0 %copy-start.1 = (f32[5,16,16,128]{3,2,1,0:T(8,128)S(1)}, f32[5,16,16,128]{3,2,1,0:T(8,128)}, u32[]{:S(2)}) copy-start(f32[5,16,16,128]{3,2,1,0:T(8,128)} %u_ref.1) | copy-start | bytes 1966084
  7.8 27.0 %all-to-all-start = ((f32[8,8,1920]{2,1,0:T(8,128)}), f32[8,8,1920]{2,1,0:T(8,128)S(1)}, u32[]{:S(2)}, u32[]{:S(2)}) async-start(f32[8,8,1920]{2,1,0:T(8,128)} %bitcast.8), calls=%async_computation | async-start | bytes 983040 | tf_op jit(solution)/shard_map/all_to_all | solution.py:223
  17.4 60.9 %collective-permute-start.3 = (f32[5,16,128]{2,1,0:T(8,128)S(1)}, f32[5,16,128]{2,1,0:T(8,128)S(1)}, u32[]{:S(2)}, u32[]{:S(2)}) collective-permute-start(f32[5,16,128]{2,1,0:T(8,128)S(1)} %bitcast.258), channel_id=1, source_target_pairs={{8,0},{16,8},{24,16},{32,24},{40,32},{48,40},{56,48},{0,56},{9,1},... | collective-permute-start | bytes 122888 | tf_op jit(solution)/shard_map/ppermute | solution.py:20
  21.3 57.0 %collective-permute-start.1 = (f32[5,16,128]{2,1,0:T(8,128)S(1)}, f32[5,16,128]{2,1,0:T(8,128)S(1)}, u32[]{:S(2)}, u32[]{:S(2)}) collective-permute-start(f32[5,16,128]{2,1,0:T(8,128)S(1)} %get-tuple-element.23), channel_id=1, source_target_pairs={{64,0},{128,64},{192,128},{0,192},{65,1},{129,65},{193,129},{1,193... | collective-permute-start | bytes 122888 | tf_op jit(solution)/shard_map/ppermute | solution.py:20
  24.1 54.2 %collective-permute-start = (f32[5,16,128]{2,1,0:T(8,128)S(1)}, f32[5,16,128]{2,1,0:T(8,128)S(1)}, u32[]{:S(2)}, u32[]{:S(2)}) collective-permute-start(f32[5,16,128]{2,1,0:T(8,128)S(1)} %get-tuple-element.22), channel_id=1, source_target_pairs={{0,64},{64,128},{128,192},{192,0},{1,65},{65,129},{129,193},{193,1... | collective-permute-start | bytes 122888 | tf_op jit(solution)/shard_map/ppermute | solution.py:20
  24.4 2.4 %copy-start.4 = (s32[6,1,1,8]{3,2,1,0:T(1,128)S(1)}, s32[6,1,1,8]{3,2,1,0:T(1,128)}, u32[]{:S(2)}) copy-start(s32[6,1,1,8]{3,2,1,0:T(1,128)} %param.7) | copy-start | bytes 580
  24.9 54.8 %collective-permute-start.5 = (f32[5,16,16]{2,1,0:T(8,128)S(1)}, f32[5,16,16]{2,1,0:T(8,128)S(1)}, u32[]{:S(2)}, u32[]{:S(2)}) collective-permute-start(f32[5,16,16]{2,1,0:T(8,128)S(1)} %bitcast.262), channel_id=1, source_target_pairs={{1,0},{2,1},{3,2},{4,3},{5,4},{6,5},{7,6},{0,7},{9,8},{10,9},{11,1... | collective-permute-start | bytes 15368 | tf_op jit(solution)/shard_map/ppermute | solution.py:20
  34.8 19.2 %all-to-all-start.2 = ((f32[8,8,1920]{2,1,0:T(8,128)}), f32[8,8,1920]{2,1,0:T(8,128)S(1)}, u32[]{:S(2)}, u32[]{:S(2)}) async-start(f32[8,8,1920]{2,1,0:T(8,128)} %bitcast.49), calls=%async_computation.2 | async-start | bytes 983040 | tf_op jit(solution)/shard_map/all_to_all | solution.py:223
  54.0 12.8 %all-to-all-start.1 = ((f32[8,8,1920]{2,1,0:T(8,128)}), f32[8,8,1920]{2,1,0:T(8,128)S(1)}, u32[]{:S(2)}, u32[]{:S(2)}) async-start(f32[8,8,1920]{2,1,0:T(8,128)} %bitcast.11), calls=%async_computation.1 | async-start | bytes 983040 | tf_op jit(solution)/shard_map/all_to_all | solution.py:224
  66.7 22.4 %all-to-all-start.3 = ((f32[8,8,1920]{2,1,0:T(8,128)}), f32[8,8,1920]{2,1,0:T(8,128)S(1)}, u32[]{:S(2)}, u32[]{:S(2)}) async-start(f32[8,8,1920]{2,1,0:T(8,128)} %bitcast.51), calls=%async_computation.3 | async-start | bytes 983040 | tf_op jit(solution)/shard_map/all_to_all | solution.py:224
  76.6 4.3 %collective-permute-start.4 = (f32[5,16,16]{2,1,0:T(8,128)S(1)}, f32[5,16,16]{2,1,0:T(8,128)S(1)}, u32[]{:S(2)}, u32[]{:S(2)}) collective-permute-start(f32[5,16,16]{2,1,0:T(8,128)S(1)} %bitcast.263), channel_id=1, source_target_pairs={{0,1},{1,2},{2,3},{3,4},{4,5},{5,6},{6,7},{7,0},{8,9},{9,10},{10,1... | collective-permute-start | bytes 15368 | tf_op jit(solution)/shard_map/ppermute | solution.py:20
  89.8 1.1 copy-start
  90.3 1.2 copy-start.2
  91.5 7.8 %slice-start = ((f32[8,1,6,5,8,8]{5,4,3,2,0,1:T(8,128)}), f32[8,1,2,5,8,8]{5,4,3,2,0,1:T(8,128)S(1)}, s32[]{:S(2)}) async-start(f32[8,1,6,5,8,8]{5,4,3,2,0,1:T(8,128)} %copy-done.2), calls=%async_computation.6 | async-start | bytes 655360 | tf_op jit(solution)/shard_map/slice | solution.py:112
  91.5 16.6 %collective-permute-start.8 = (f32[5,16,128]{2,1,0:T(8,128)S(1)}, f32[5,16,128]{2,1,0:T(8,128)S(1)}, u32[]{:S(2)}, u32[]{:S(2)}) collective-permute-start(f32[5,16,128]{2,1,0:T(8,128)S(1)} %bitcast.261), channel_id=1, source_target_pairs={{0,8},{8,16},{16,24},{24,32},{32,40},{40,48},{48,56},{56,0},{1,9},... | collective-permute-start | bytes 122888 | tf_op jit(solution)/shard_map/ppermute | solution.py:20
  92.7 15.5 %collective-permute-start.9 = (f32[5,16,128]{2,1,0:T(8,128)S(1)}, f32[5,16,128]{2,1,0:T(8,128)S(1)}, u32[]{:S(2)}, u32[]{:S(2)}) collective-permute-start(f32[5,16,128]{2,1,0:T(8,128)S(1)} %bitcast.260), channel_id=1, source_target_pairs={{8,0},{16,8},{24,16},{32,24},{40,32},{48,40},{56,48},{0,56},{9,1},... | collective-permute-start | bytes 122888 | tf_op jit(solution)/shard_map/ppermute | solution.py:20
  96.6 11.6 %collective-permute-start.7 = (f32[5,16,128]{2,1,0:T(8,128)S(1)}, f32[5,16,128]{2,1,0:T(8,128)S(1)}, u32[]{:S(2)}, u32[]{:S(2)}) collective-permute-start(f32[5,16,128]{2,1,0:T(8,128)S(1)} %get-tuple-element.17), channel_id=1, source_target_pairs={{64,0},{128,64},{192,128},{0,192},{65,1},{129,65},{193,129},{1,193... | collective-permute-start | bytes 122888 | tf_op jit(solution)/shard_map/ppermute | solution.py:20
  100.5 4.1 %collective-permute-start.11 = (f32[5,16,16]{2,1,0:T(8,128)S(1)}, f32[5,16,16]{2,1,0:T(8,128)S(1)}, u32[]{:S(2)}, u32[]{:S(2)}) collective-permute-start(f32[5,16,16]{2,1,0:T(8,128)S(1)} %get-tuple-element.3), channel_id=1, source_target_pairs={{1,0},{2,1},{3,2},{4,3},{5,4},{6,5},{7,6},{0,7},{9,8},{10,9},{11,1... | collective-permute-start | bytes 15368 | tf_op jit(solution)/shard_map/ppermute | solution.py:20
  102.8 4.0 %collective-permute-start.10 = (f32[5,16,16]{2,1,0:T(8,128)S(1)}, f32[5,16,16]{2,1,0:T(8,128)S(1)}, u32[]{:S(2)}, u32[]{:S(2)}) collective-permute-start(f32[5,16,16]{2,1,0:T(8,128)S(1)} %get-tuple-element.2), channel_id=1, source_target_pairs={{0,1},{1,2},{2,3},{3,4},{4,5},{5,6},{6,7},{7,0},{8,9},{9,10},{10,1... | collective-permute-start | bytes 15368 | tf_op jit(solution)/shard_map/ppermute | solution.py:20
  104.6 5.2 %collective-permute-start.6 = (f32[5,16,128]{2,1,0:T(8,128)S(1)}, f32[5,16,128]{2,1,0:T(8,128)S(1)}, u32[]{:S(2)}, u32[]{:S(2)}) collective-permute-start(f32[5,16,128]{2,1,0:T(8,128)S(1)} %get-tuple-element.16), channel_id=1, source_target_pairs={{0,64},{64,128},{128,192},{192,0},{1,65},{65,129},{129,193},{193,1... | collective-permute-start | bytes 122888 | tf_op jit(solution)/shard_map/ppermute | solution.py:20
  120.3 14.9 %all-to-all-start.4 = ((f32[8,8,2560]{2,1,0:T(8,128)}), f32[8,8,2560]{2,1,0:T(8,128)S(1)}, u32[]{:S(2)}, u32[]{:S(2)}) async-start(f32[8,8,2560]{2,1,0:T(8,128)} %bitcast.80), calls=%async_computation.4 | async-start | bytes 1310720 | tf_op jit(solution)/shard_map/all_to_all | solution.py:237
  136.8 3.7 %copy-start.3 = (s32[1,512]{1,0:T(1,128)S(1)}, s32[1,512]{1,0:T(1,128)}, u32[]{:S(2)}) copy-start(s32[1,512]{1,0:T(1,128)} %param.6) | copy-start | bytes 6148
  136.8 24.7 %all-to-all-start.5 = ((f32[8,8,2560]{2,1,0:T(8,128)}), f32[8,8,2560]{2,1,0:T(8,128)S(1)}, u32[]{:S(2)}, u32[]{:S(2)}) async-start(f32[8,8,2560]{2,1,0:T(8,128)} %bitcast.82), calls=%async_computation.5 | async-start | bytes 1310720 | tf_op jit(solution)/shard_map/all_to_all | solution.py:239

commit v3 on v1

--- a/solution.py
+++ b/solution.py
@@ -110,7 +110,11 @@
     side = lv[:, :, 0:4].transpose(1, 2, 3, 4, 0, 5).reshape(2, 4, 5, half, nblk * half)
     side = exact_dot("ay,lkfab,bz->lkfyz", rows, side, replicate(nblk * half, nblk * BS))
     ends = lv[:, :, 4:6].transpose(1, 2, 3, 4, 5, 0)
-    ends = exact_dot("ax,by,lkfabc,cz->lkfxyz", rows, rows, ends, replicate(nblk, nblk * BS))
+    lane = jnp.arange(nblk * BS)
+    starts = (lane % BS == 0)[None, :]
+    spread = replicate(nblk, nblk * BS)
+    choose = jnp.stack([jnp.where(starts, spread, 0.0), jnp.where(starts, 0.0, spread)])
+    ends = exact_dot("ax,by,lkfabc,kcz->lfxyz", rows, rows, ends, choose)
     return side, ends
 
 
@@ -137,9 +141,11 @@
     at_hi = lane % BS == BS - 1
     link_lo = jnp.repeat(links[:, 4] == 1, BS)
     link_hi = jnp.repeat(links[:, 5] == 1, BS)
-    lo_val = jnp.where(link_lo & (lane == 0), far_lo[..., None], ends[0])
-    hi_val = jnp.where(link_hi & (lane == nz_dev - 1), far_hi[..., None], ends[1])
-    zfix = jnp.where(at_lo, lo_val, hi_val)
+    zfix = jnp.where(
+        link_lo & (lane == 0),
+        far_lo[..., None],
+        jnp.where(link_hi & (lane == nz_dev - 1), far_hi[..., None], ends),
+    )
     flag_lo = at_lo & (~link_lo | (lane == 0))
     flag_hi = at_hi & (~link_hi | (lane == nz_dev - 1))
     zflag = jnp.broadcast_to(

time: 152 us -> 149 us (0.980)
  local copies, waits for them, and re-layouts: 29.9 us -> 22.9 us
  waiting for transfers between devices: 53.9 us -> 60.8 us
  other arithmetic: 11.5 us -> 8.73 us
  starting transfers between devices: 39.9 us -> 41.7 us
    all_to_all x1, waiting for transfers between devices: 13.4 us -> 18.5 us  [shards(): stage = lax.all_to_all(pick(levels[None], first), 'gy', 0, 0, tiled=True)]
    unnamed x26 -> x9, local copies, waits for them, and re-layouts: 3.78 us -> 1.08 us
    select_n x2 -> x3, other arithmetic: 3.34 us -> 2.5 us  [the longest x2 2.5 us: ghost_inputs(): jnp.where(link_lo & (lane == 0), far_lo[..., None], jnp.where(link_hi & (...]
  transfers between devices with their start and end apart: 16 -> 16, of which waited for: 7 -> 8; matrix products, arithmetic and copies ran while one was open for 16% -> 11% of each run, Pallas kernels for 0% -> 0%
where the time goes in v3:
time: 149 us
  waiting for transfers between devices  60.8 us (41%)
  starting transfers between devices  41.7 us (28%)
  local copies, waits for them, and re-layouts  22.9 us (15%)
  Pallas kernels  9.02 us (6%)
  other arithmetic  8.73 us (6%)
  matrix products  4.52 us (3%)
    all_to_all x1, waiting for transfers between devices, shards(): stage = lax.all_to_all(pick(stage, home), 'gy', 0, 0, tiled=True)  20.9 us
    all_to_all x1, waiting for transfers between devices, shards(): stage = lax.all_to_all(pick(levels[None], first), 'gy', 0, 0, tiled=True)  18.5 us
    ppermute x12, starting transfers between devices, shift_in(): return lax.ppermute(plane, axis, pairs)  16.1 us
    pallas_call x2, Pallas kernels, substep(): pl.pallas_call(substep_kernel, out_shape=jax.ShapeDtypeStruct(state.shape...  9.02 us
    gather x6, local copies, waits for them, and re-layouts, pick(): jnp.take(flat, index.reshape(-1), axis=0, mode='clip')  8.75 us
    all_to_all x1, waiting for transfers between devices, shards(): stage = lax.all_to_all(pick(stage, second), 'gz', 0, 0, tiled=True)  8.62 us
    all_to_all x1, starting transfers between devices, shards(): stage = lax.all_to_all(pick(levels[None], first), 'gy', 0, 0, tiled=True)  8.6 us
    all_to_all x1, starting transfers between devices, shards(): stage = lax.all_to_all(pick(restricted[None], back), 'gz', 0, 0, tiled=True)  7.48 us
  transfers between devices with their start and end apart: 16, of which 8 were waited for; matrix products, arithmetic and copies ran while one was open for 11% of the time, Pallas kernels for 0%

profile of v3, /device:TPU:8, one launch (start us, length us, event | category | flops | bytes accessed | tf_op | source)
XLA Modules:
  0.0 148.7 jit_solution(14077670313706488112)
XLA Ops:
  0.7 0.7 and_select_fusion
  1.4 0.7 add_select_fusion.3
  2.1 0.7 broadcast_compare_fusion
  4.2 0.9 fusion.67
  5.0 1.8 %gather_fusion = f32[64,3840]{1,0:T(8,128)} fusion(f32[8,3840]{1,0:T(8,128)S(1)} %pad_maximum_fusion, s32[1024]{0:T(1024)S(1)} %pad_clamp_fusion.6), kind=kCustom, calls=%fused_computation | custom fusion | bytes 1966336 | tf_op jit(solution)/shard_map/jit(_take)/gather | solution.py:171
  6.9 8.6 %all-to-all-start = ((f32[8,8,3840]{2,1,0:T(8,128)}), f32[8,8,3840]{2,1,0:T(8,128)S(1)}, u32[]{:S(2)}, u32[]{:S(2)}) async-start(f32[8,8,3840]{2,1,0:T(8,128)} %bitcast.8), calls=%async_computation | async-start | bytes 1966080 | tf_op jit(solution)/shard_map/all_to_all | solution.py:224
  15.6 3.9 %collective-permute-start.3 = (f32[5,16,128]{2,1,0:T(8,128)S(1)}, f32[5,16,128]{2,1,0:T(8,128)S(1)}, u32[]{:S(2)}, u32[]{:S(2)}) collective-permute-start(f32[5,16,128]{2,1,0:T(8,128)S(1)} %bitcast.223), channel_id=1, source_target_pairs={{8,0},{16,8},{24,16},{32,24},{40,32},{48,40},{56,48},{0,56},{9,1},... | collective-permute-start | bytes 122888 | tf_op jit(solution)/shard_map/ppermute | solution.py:20
  19.5 1.6 %collective-permute-start = (f32[5,16,128]{2,1,0:T(8,128)S(1)}, f32[5,16,128]{2,1,0:T(8,128)S(1)}, u32[]{:S(2)}, u32[]{:S(2)}) collective-permute-start(f32[5,16,128]{2,1,0:T(8,128)S(1)} %get-tuple-element.22), channel_id=1, source_target_pairs={{0,64},{64,128},{128,192},{192,0},{1,65},{65,129},{129,193},{193,1... | collective-permute-start | bytes 122888 | tf_op jit(solution)/shard_map/ppermute | solution.py:20
  21.1 1.7 %collective-permute-start.1 = (f32[5,16,128]{2,1,0:T(8,128)S(1)}, f32[5,16,128]{2,1,0:T(8,128)S(1)}, u32[]{:S(2)}, u32[]{:S(2)}) collective-permute-start(f32[5,16,128]{2,1,0:T(8,128)S(1)} %get-tuple-element.23), channel_id=1, source_target_pairs={{64,0},{128,64},{192,128},{0,192},{65,1},{129,65},{193,129},{1,193... | collective-permute-start | bytes 122888 | tf_op jit(solution)/shard_map/ppermute | solution.py:20
  24.2 0.6 gather_fusion.2
  24.8 0.7 gather_fusion.3
  25.6 18.5 %all-to-all-done = f32[8,8,3840]{2,1,0:T(8,128)S(1)} async-done(((f32[8,8,3840]{2,1,0:T(8,128)}), f32[8,8,3840]{2,1,0:T(8,128)S(1)}, u32[]{:S(2)}, u32[]{:S(2)}) %all-to-all-start) | async-done | bytes 983072 | tf_op jit(solution)/shard_map/all_to_all | solution.py:224
  44.1 1.8 %gather_fusion.1 = f32[64,3840]{1,0:T(8,128)} fusion(f32[64,3840]{1,0:T(8,128)S(1)} %bitcast.214, s32[1024]{0:T(1024)S(1)} %pad_clamp_fusion.5), kind=kCustom, calls=%fused_computation.1 | custom fusion | bytes 1966336 | tf_op jit(solution)/shard_map/jit(_take)/gather | solution.py:171
  46.0 4.9 %all-to-all-start.1 = ((f32[8,8,3840]{2,1,0:T(8,128)}), f32[8,8,3840]{2,1,0:T(8,128)S(1)}, u32[]{:S(2)}, u32[]{:S(2)}) async-start(f32[8,8,3840]{2,1,0:T(8,128)} %bitcast.11), calls=%async_computation.1 | async-start | bytes 1966080 | tf_op jit(solution)/shard_map/all_to_all | solution.py:226
  53.2 8.6 %all-to-all-done.1 = f32[8,8,3840]{2,1,0:T(8,128)S(1)} async-done(((f32[8,8,3840]{2,1,0:T(8,128)}), f32[8,8,3840]{2,1,0:T(8,128)S(1)}, u32[]{:S(2)}, u32[]{:S(2)}) %all-to-all-start.1) | async-done | bytes 983072 | tf_op jit(solution)/shard_map/all_to_all | solution.py:226
  61.8 0.6 gather_fusion.4
  62.4 1.1 reshape.864
  63.7 0.8 copy.71
  65.1 1.2 convolution_bitcast_fusion.1
  66.8 0.8 convolution_bitcast_fusion
  68.2 1.1 collective-permute-start.4
  69.3 0.6 pad_maximum_fusion.1.gx_ref
  70.0 0.7 copy.80.gy_ref
  70.7 1.6 %collective-permute-done.4 = f32[5,16,16]{2,1,0:T(8,128)S(1)} collective-permute-done((f32[5,16,16]{2,1,0:T(8,128)S(1)}, f32[5,16,16]{2,1,0:T(8,128)S(1)}, u32[]{:S(2)}, u32[]{:S(2)}) %collective-permute-start.4) | collective-permute-done | bytes 5152 | tf_op jit(solution)/shard_map/ppermute | solution.py:20
  72.2 1.2 fusion.7.zfix_ref
  73.5 0.6 broadcast_in_dim.270.zflag_ref
  74.1 4.5 %shard_map.59.u_ref = f32[5,16,16,128]{3,2,1,0:T(8,128)} custom-call(f32[5,16,16,128]{3,2,1,0:T(8,128)} %u_ref.1, f32[2,5,16,128]{3,2,1,0:T(8,128)} %pad_maximum_fusion.1.gx_ref, f32[2,16,5,1,128]{4,3,2,1,0:T(1,128)} %copy.80.gy_ref, f32[5,16,16,128]{3,2,1,0:T(8,128)} %fusion.7.zfix_ref, s32[2,16,128]{2,1,0:T(8,128)} %broadcast_in_dim.270.zflag_ref), custom_call_target="tpu_custom_call" | custom-call | tf_op jit(solution)/shard_map/pallas_call | solution.py:92
  78.6 1.9 %slice_reduce_fusion.1 = (f32[5,16,16]{2,1,0:T(8,128)S(1)}, f32[5,16,16]{2,1,0:T(8,128)S(1)}) fusion(f32[5,16,16,128]{3,2,1,0:T(8,128)} %shard_map.59.u_ref), kind=kLoop, calls=%fused_computation.24 | loop fusion | bytes 20480 | tf_op jit(solution)/shard_map/slice | solution.py:137
  80.5 1.1 fusion.64
  81.6 1.1 collective-permute-start.10
  82.7 2.4 %collective-permute-start.11 = (f32[5,16,16]{2,1,0:T(8,128)S(1)}, f32[5,16,16]{2,1,0:T(8,128)S(1)}, u32[]{:S(2)}, u32[]{:S(2)}) collective-permute-start(f32[5,16,16]{2,1,0:T(8,128)S(1)} %get-tuple-element.3), channel_id=1, source_target_pairs={{1,0},{2,1},{3,2},{4,3},{5,4},{6,5},{7,6},{0,7},{9,8},{10,9},{11,1... | collective-permute-start | bytes 15368 | tf_op jit(solution)/shard_map/ppermute | solution.py:20
  85.2 0.8 slice_bitcast_fusion.12
  86.0 1.5 %collective-permute-start.6 = (f32[5,16,128]{2,1,0:T(8,128)S(1)}, f32[5,16,128]{2,1,0:T(8,128)S(1)}, u32[]{:S(2)}, u32[]{:S(2)}) collective-permute-start(f32[5,16,128]{2,1,0:T(8,128)S(1)} %get-tuple-element.16), channel_id=1, source_target_pairs={{0,64},{64,128},{128,192},{192,0},{1,65},{65,129},{129,193},{193,1... | collective-permute-start | bytes 122888 | tf_op jit(solution)/shard_map/ppermute | solution.py:20
  87.5 1.7 %collective-permute-start.7 = (f32[5,16,128]{2,1,0:T(8,128)S(1)}, f32[5,16,128]{2,1,0:T(8,128)S(1)}, u32[]{:S(2)}, u32[]{:S(2)}) collective-permute-start(f32[5,16,128]{2,1,0:T(8,128)S(1)} %get-tuple-element.17), channel_id=1, source_target_pairs={{64,0},{128,64},{192,128},{0,192},{65,1},{129,65},{193,129},{1,193... | collective-permute-start | bytes 122888 | tf_op jit(solution)/shard_map/ppermute | solution.py:20
  89.7 1.3 fusion.5.zfix_ref
  91.5 3.5 %collective-permute-done.8 = f32[5,16,128]{2,1,0:T(8,128)S(1)} collective-permute-done((f32[5,16,128]{2,1,0:T(8,128)S(1)}, f32[5,16,128]{2,1,0:T(8,128)S(1)}, u32[]{:S(2)}, u32[]{:S(2)}) %collective-permute-start.8) | collective-permute-done | bytes 40992 | tf_op jit(solution)/shard_map/ppermute | solution.py:20
  95.0 0.7 copy.85.gy_ref
  95.7 0.6 pad_maximum_fusion.2.gx_ref
  96.3 4.5 %shard_map.60 = f32[5,16,16,128]{3,2,1,0:T(8,128)} custom-call(f32[5,16,16,128]{3,2,1,0:T(8,128)} %shard_map.59.u_ref, f32[2,5,16,128]{3,2,1,0:T(8,128)} %pad_maximum_fusion.2.gx_ref, f32[2,16,5,1,128]{4,3,2,1,0:T(1,128)} %copy.85.gy_ref, f32[5,16,16,128]{3,2,1,0:T(8,128)} %fusion.5.zfix_ref, s32[2,16,128]{2,1,0:T(8,128)} %broadcast_in_dim.270.zflag_ref), custom_call_target="tpu_custom_call" | custom-call | tf_op jit(solution)/shard_map/pallas_call | solution.py:92
  100.8 1.3 fusion.11
  103.0 0.7 reshape_broadcast_in_dim_reshape.3
  103.7 1.6 %gather_fusion.5 = f32[64,2560]{1,0:T(8,128)} fusion(f32[8,2560]{1,0:T(8,128)S(1)} %reshape_broadcast_in_dim_reshape.3, s32[1024]{0:T(1024)S(1)} %pad_clamp_fusion.2), kind=kCustom, calls=%fused_computation.5 | custom fusion | bytes 1310976 | tf_op jit(solution)/shard_map/jit(_take)/gather | solution.py:171
  105.3 7.5 %all-to-all-start.2 = ((f32[8,8,2560]{2,1,0:T(8,128)}), f32[8,8,2560]{2,1,0:T(8,128)S(1)}, u32[]{:S(2)}, u32[]{:S(2)}) async-start(f32[8,8,2560]{2,1,0:T(8,128)} %bitcast.66), calls=%async_computation.2 | async-start | bytes 1310720 | tf_op jit(solution)/shard_map/all_to_all | solution.py:240
  112.9 7.2 %all-to-all-done.2 = f32[8,8,2560]{2,1,0:T(8,128)S(1)} async-done(((f32[8,8,2560]{2,1,0:T(8,128)}), f32[8,8,2560]{2,1,0:T(8,128)S(1)}, u32[]{:S(2)}, u32[]{:S(2)}) %all-to-all-start.2) | async-done | bytes 655392 | tf_op jit(solution)/shard_map/all_to_all | solution.py:240
  120.2 1.6 %gather_fusion.6 = f32[64,2560]{1,0:T(8,128)} fusion(f32[64,2560]{1,0:T(8,128)S(1)} %bitcast.215, s32[1024]{0:T(1024)S(1)} %pad_clamp_fusion.1), kind=kCustom, calls=%fused_computation.6 | custom fusion | bytes 1310976 | tf_op jit(solution)/shard_map/jit(_take)/gather | solution.py:171
  121.8 4.6 %all-to-all-start.3 = ((f32[8,8,2560]{2,1,0:T(8,128)}), f32[8,8,2560]{2,1,0:T(8,128)S(1)}, u32[]{:S(2)}, u32[]{:S(2)}) async-start(f32[8,8,2560]{2,1,0:T(8,128)} %bitcast.68), calls=%async_computation.3 | async-start | bytes 1310720 | tf_op jit(solution)/shard_map/all_to_all | solution.py:242
  126.6 20.9 %all-to-all-done.3 = f32[8,8,2560]{2,1,0:T(8,128)S(1)} async-done(((f32[8,8,2560]{2,1,0:T(8,128)}), f32[8,8,2560]{2,1,0:T(8,128)S(1)}, u32[]{:S(2)}, u32[]{:S(2)}) %all-to-all-start.3) | async-done | bytes 655392 | tf_op jit(solution)/shard_map/all_to_all | solution.py:242
  147.5 1.2 gather_fusion.7
  (98 shorter events, 9.3 us)
Async XLA Ops:
  6.9 8.6 %copy-start = (f32[5,16,16,128]{3,2,1,0:T(8,128)S(1)}, f32[5,16,16,128]{3,2,1,0:T(8,128)}, u32[]{:S(2)}) copy-start(f32[5,16,16,128]{3,2,1,0:T(8,128)} %u_ref.1) | copy-start | bytes 1966084
  6.9 37.2 %all-to-all-start = ((f32[8,8,3840]{2,1,0:T(8,128)}), f32[8,8,3840]{2,1,0:T(8,128)S(1)}, u32[]{:S(2)}, u32[]{:S(2)}) async-start(f32[8,8,3840]{2,1,0:T(8,128)} %bitcast.8), calls=%async_computation | async-start | bytes 1966080 | tf_op jit(solution)/shard_map/all_to_all | solution.py:224
  15.6 52.6 %collective-permute-start.3 = (f32[5,16,128]{2,1,0:T(8,128)S(1)}, f32[5,16,128]{2,1,0:T(8,128)S(1)}, u32[]{:S(2)}, u32[]{:S(2)}) collective-permute-start(f32[5,16,128]{2,1,0:T(8,128)S(1)} %bitcast.223), channel_id=1, source_target_pairs={{8,0},{16,8},{24,16},{32,24},{40,32},{48,40},{56,48},{0,56},{9,1},... | collective-permute-start | bytes 122888 | tf_op jit(solution)/shard_map/ppermute | solution.py:20
  19.5 49.8 %collective-permute-start.2 = (f32[5,16,128]{2,1,0:T(8,128)S(1)}, f32[5,16,128]{2,1,0:T(8,128)S(1)}, u32[]{:S(2)}, u32[]{:S(2)}) collective-permute-start(f32[5,16,128]{2,1,0:T(8,128)S(1)} %bitcast.222), channel_id=1, source_target_pairs={{0,8},{8,16},{16,24},{24,32},{32,40},{40,48},{48,56},{56,0},{1,9},... | collective-permute-start | bytes 122888 | tf_op jit(solution)/shard_map/ppermute | solution.py:20
  19.5 49.8 %collective-permute-start = (f32[5,16,128]{2,1,0:T(8,128)S(1)}, f32[5,16,128]{2,1,0:T(8,128)S(1)}, u32[]{:S(2)}, u32[]{:S(2)}) collective-permute-start(f32[5,16,128]{2,1,0:T(8,128)S(1)} %get-tuple-element.22), channel_id=1, source_target_pairs={{0,64},{64,128},{128,192},{192,0},{1,65},{65,129},{129,193},{193,1... | collective-permute-start | bytes 122888 | tf_op jit(solution)/shard_map/ppermute | solution.py:20
  21.1 48.2 %collective-permute-start.1 = (f32[5,16,128]{2,1,0:T(8,128)S(1)}, f32[5,16,128]{2,1,0:T(8,128)S(1)}, u32[]{:S(2)}, u32[]{:S(2)}) collective-permute-start(f32[5,16,128]{2,1,0:T(8,128)S(1)} %get-tuple-element.23), channel_id=1, source_target_pairs={{64,0},{128,64},{192,128},{0,192},{65,1},{129,65},{193,129},{1,193... | collective-permute-start | bytes 122888 | tf_op jit(solution)/shard_map/ppermute | solution.py:20
  23.1 2.4 %copy-start.2 = (s32[6,1,1,8]{3,2,1,0:T(1,128)S(1)}, s32[6,1,1,8]{3,2,1,0:T(1,128)}, u32[]{:S(2)}) copy-start(s32[6,1,1,8]{3,2,1,0:T(1,128)} %param.7) | copy-start | bytes 580
  23.6 47.1 %collective-permute-start.5 = (f32[5,16,16]{2,1,0:T(8,128)S(1)}, f32[5,16,16]{2,1,0:T(8,128)S(1)}, u32[]{:S(2)}, u32[]{:S(2)}) collective-permute-start(f32[5,16,16]{2,1,0:T(8,128)S(1)} %bitcast.226), channel_id=1, source_target_pairs={{1,0},{2,1},{3,2},{4,3},{5,4},{6,5},{7,6},{0,7},{9,8},{10,9},{11,1... | collective-permute-start | bytes 15368 | tf_op jit(solution)/shard_map/ppermute | solution.py:20
  46.0 15.9 %all-to-all-start.1 = ((f32[8,8,3840]{2,1,0:T(8,128)}), f32[8,8,3840]{2,1,0:T(8,128)S(1)}, u32[]{:S(2)}, u32[]{:S(2)}) async-start(f32[8,8,3840]{2,1,0:T(8,128)} %bitcast.11), calls=%async_computation.1 | async-start | bytes 1966080 | tf_op jit(solution)/shard_map/all_to_all | solution.py:226
  68.2 4.1 %collective-permute-start.4 = (f32[5,16,16]{2,1,0:T(8,128)S(1)}, f32[5,16,16]{2,1,0:T(8,128)S(1)}, u32[]{:S(2)}, u32[]{:S(2)}) collective-permute-start(f32[5,16,16]{2,1,0:T(8,128)S(1)} %bitcast.227), channel_id=1, source_target_pairs={{0,1},{1,2},{2,3},{3,4},{4,5},{5,6},{6,7},{7,0},{8,9},{9,10},{10,1... | collective-permute-start | bytes 15368 | tf_op jit(solution)/shard_map/ppermute | solution.py:20
  81.6 7.6 %collective-permute-start.10 = (f32[5,16,16]{2,1,0:T(8,128)S(1)}, f32[5,16,16]{2,1,0:T(8,128)S(1)}, u32[]{:S(2)}, u32[]{:S(2)}) collective-permute-start(f32[5,16,16]{2,1,0:T(8,128)S(1)} %get-tuple-element.2), channel_id=1, source_target_pairs={{0,1},{1,2},{2,3},{3,4},{4,5},{5,6},{6,7},{7,0},{8,9},{9,10},{10,1... | collective-permute-start | bytes 15368 | tf_op jit(solution)/shard_map/ppermute | solution.py:20
  82.7 7.0 %collective-permute-start.11 = (f32[5,16,16]{2,1,0:T(8,128)S(1)}, f32[5,16,16]{2,1,0:T(8,128)S(1)}, u32[]{:S(2)}, u32[]{:S(2)}) collective-permute-start(f32[5,16,16]{2,1,0:T(8,128)S(1)} %get-tuple-element.3), channel_id=1, source_target_pairs={{1,0},{2,1},{3,2},{4,3},{5,4},{6,5},{7,6},{0,7},{9,8},{10,9},{11,1... | collective-permute-start | bytes 15368 | tf_op jit(solution)/shard_map/ppermute | solution.py:20
  86.0 5.2 %collective-permute-start.6 = (f32[5,16,128]{2,1,0:T(8,128)S(1)}, f32[5,16,128]{2,1,0:T(8,128)S(1)}, u32[]{:S(2)}, u32[]{:S(2)}) collective-permute-start(f32[5,16,128]{2,1,0:T(8,128)S(1)} %get-tuple-element.16), channel_id=1, source_target_pairs={{0,64},{64,128},{128,192},{192,0},{1,65},{65,129},{129,193},{193,1... | collective-permute-start | bytes 122888 | tf_op jit(solution)/shard_map/ppermute | solution.py:20
  87.5 4.0 %collective-permute-start.7 = (f32[5,16,128]{2,1,0:T(8,128)S(1)}, f32[5,16,128]{2,1,0:T(8,128)S(1)}, u32[]{:S(2)}, u32[]{:S(2)}) collective-permute-start(f32[5,16,128]{2,1,0:T(8,128)S(1)} %get-tuple-element.17), channel_id=1, source_target_pairs={{64,0},{128,64},{192,128},{0,192},{65,1},{129,65},{193,129},{1,193... | collective-permute-start | bytes 122888 | tf_op jit(solution)/shard_map/ppermute | solution.py:20
  89.2 2.3 %collective-permute-start.9 = (f32[5,16,128]{2,1,0:T(8,128)S(1)}, f32[5,16,128]{2,1,0:T(8,128)S(1)}, u32[]{:S(2)}, u32[]{:S(2)}) collective-permute-start(f32[5,16,128]{2,1,0:T(8,128)S(1)} %bitcast.225), channel_id=1, source_target_pairs={{8,0},{16,8},{24,16},{32,24},{40,32},{48,40},{56,48},{0,56},{9,1},... | collective-permute-start | bytes 122888 | tf_op jit(solution)/shard_map/ppermute | solution.py:20
  89.2 5.7 %collective-permute-start.8 = (f32[5,16,128]{2,1,0:T(8,128)S(1)}, f32[5,16,128]{2,1,0:T(8,128)S(1)}, u32[]{:S(2)}, u32[]{:S(2)}) collective-permute-start(f32[5,16,128]{2,1,0:T(8,128)S(1)} %bitcast.224), channel_id=1, source_target_pairs={{0,8},{8,16},{16,24},{24,32},{32,40},{40,48},{48,56},{56,0},{1,9},... | collective-permute-start | bytes 122888 | tf_op jit(solution)/shard_map/ppermute | solution.py:20
  105.3 14.8 %all-to-all-start.2 = ((f32[8,8,2560]{2,1,0:T(8,128)}), f32[8,8,2560]{2,1,0:T(8,128)S(1)}, u32[]{:S(2)}, u32[]{:S(2)}) async-start(f32[8,8,2560]{2,1,0:T(8,128)} %bitcast.66), calls=%async_computation.2 | async-start | bytes 1310720 | tf_op jit(solution)/shard_map/all_to_all | solution.py:240
  121.8 4.6 %copy-start.1 = (s32[1,512]{1,0:T(1,128)S(1)}, s32[1,512]{1,0:T(1,128)}, u32[]{:S(2)}) copy-start(s32[1,512]{1,0:T(1,128)} %param.6) | copy-start | bytes 6148
  121.8 25.7 %all-to-all-start.3 = ((f32[8,8,2560]{2,1,0:T(8,128)}), f32[8,8,2560]{2,1,0:T(8,128)S(1)}, u32[]{:S(2)}, u32[]{:S(2)}) async-start(f32[8,8,2560]{2,1,0:T(8,128)} %bitcast.68), calls=%async_computation.3 | async-start | bytes 1310720 | tf_op jit(solution)/shard_map/all_to_all | solution.py:242

commit v4 on v3

--- a/solution.py
+++ b/solution.py
@@ -45,7 +45,7 @@
     return [0.5 * (fa[i] + fb[i]) - wave * (vb[i] - va[i]) for i in range(5)]
 
 
-def substep_kernel(u_ref, gx_ref, gy_ref, zfix_ref, zflag_ref, o_ref):
+def substep_kernel(u_ref, gx_ref, gy_ref, zfix_ref, zflag_ref, o_ref, ox_ref, oy_ref, oz_ref):
     nx = u_ref.shape[1]
     ny = u_ref.shape[2]
     nz = u_ref.shape[3]
@@ -81,17 +81,43 @@
             right = face_of(fc, sc, cen, fh, sh, hi)
             diff = [right[i] - left[i] for i in range(5)]
             total = diff if total is None else [total[i] + diff[i] for i in range(5)]
+        new = [cen[f] - LAMBDA * total[f] for f in range(5)]
         for f in range(5):
-            o_ref[f, x] = cen[f] - LAMBDA * total[f]
+            o_ref[f, x] = new[f]
+            oy_ref[0, x, f] = new[f][ny - 1 : ny, :]
+            oy_ref[1, x, f] = new[f][0:1, :]
+            oz_ref[0, f, x] = new[f][:, nz - 1 : nz]
+            oz_ref[1, f, x] = new[f][:, 0:1]
+
+        @pl.when(x == nx - 1)
+        def _():
+            for f in range(5):
+                ox_ref[0, f] = new[f]
+
+        @pl.when(x == 0)
+        def _():
+            for f in range(5):
+                ox_ref[1, f] = new[f]
+
         return carry
 
     lax.fori_loop(0, nx, body, 0)
 
 
 def substep(state, gx, gy, zfix, zflag):
-    return pl.pallas_call(
-        substep_kernel, out_shape=jax.ShapeDtypeStruct(state.shape, state.dtype)
+    five, nx, ny, nz = state.shape
+    shapes = [state.shape, (2, five, ny, nz), (2, nx, five, 1, nz), (2, five, nx, ny, 1)]
+    out = pl.pallas_call(
+        substep_kernel, out_shape=[jax.ShapeDtypeStruct(one, state.dtype) for one in shapes]
     )(state, gx, gy, zfix, zflag)
+    return out[0], out[1:]
+
+
+def planes_of(state):
+    ox = jnp.stack([state[:, -1], state[:, 0]])
+    oy = jnp.stack([state[:, :, -1], state[:, :, 0]]).transpose(0, 2, 1, 3)[:, :, :, None, :]
+    oz = jnp.stack([state[..., -1], state[..., 0]])[..., None]
+    return ox, oy, oz
 
 
 def replicate(rows, cols):
@@ -118,24 +144,24 @@
     return side, ends
 
 
-def ghost_inputs(state, side, ends, links):
+def ghost_inputs(state, planes, side, ends, links):
     nz_dev = state.shape[3]
+    ox, oy, oz = planes
     chosen = [jnp.repeat(links[:, face] == 1, BS)[None, None, :] for face in range(4)]
     gx = jnp.stack(
         [
-            jnp.where(chosen[0], shift_in(state[:, -1], "gx", True), side[0]),
-            jnp.where(chosen[1], shift_in(state[:, 0], "gx", False), side[1]),
+            jnp.where(chosen[0], shift_in(ox[0], "gx", True), side[0]),
+            jnp.where(chosen[1], shift_in(ox[1], "gx", False), side[1]),
         ]
     )
     gy = jnp.stack(
         [
-            jnp.where(chosen[2], shift_in(state[:, :, -1], "gy", True), side[2]),
-            jnp.where(chosen[3], shift_in(state[:, :, 0], "gy", False), side[3]),
-        ]
-    )
-    gy = gy.transpose(0, 2, 1, 3)[:, :, :, None, :]
-    far_lo = shift_in(state[..., -1], "gz", True)
-    far_hi = shift_in(state[..., 0], "gz", False)
+            jnp.where(chosen[2], shift_in(oy[0], "gy", True), side[2]),
+            jnp.where(chosen[3], shift_in(oy[1], "gy", False), side[3]),
+        ]
+    )
+    far_lo = shift_in(oz[0], "gz", True)
+    far_hi = shift_in(oz[1], "gz", False)
     lane = jnp.arange(nz_dev, dtype=jnp.int32)
     at_lo = lane % BS == 0
     at_hi = lane % BS == BS - 1
@@ -143,8 +169,8 @@
     link_hi = jnp.repeat(links[:, 5] == 1, BS)
     zfix = jnp.where(
         link_lo & (lane == 0),
-        far_lo[..., None],
-        jnp.where(link_hi & (lane == nz_dev - 1), far_hi[..., None], ends),
+        far_lo,
+        jnp.where(link_hi & (lane == nz_dev - 1), far_hi, ends),
     )
     flag_lo = at_lo & (~link_lo | (lane == 0))
     flag_hi = at_hi & (~link_hi | (lane == nz_dev - 1))
@@ -228,9 +254,13 @@
     fetched = pick(stage, o_col[mine] * nblk + rank2[mine])
 
     side, ends = coarse_faces(fetched, nblk)
+    side = [side[:, 0], side[:, 1], side[:, 2].transpose(0, 2, 1, 3)[:, :, :, None, :],
+            side[:, 3].transpose(0, 2, 1, 3)[:, :, :, None, :]]
     state = fine
+    planes = planes_of(fine)
     for step in range(2):
-        state = substep(state, *ghost_inputs(state, side[step], ends[step], links))
+        level_side = [one[step] for one in side]
+        state, planes = substep(state, *ghost_inputs(state, planes, level_side, ends[step], links))
     restricted = restrict_state(state, nblk)
 
     pos = jnp.arange(nblk, dtype=jnp.int32)

time: 149 us -> 151 us (1.013)
  Pallas kernels: 9.02 us -> 12.2 us
  local copies, waits for them, and re-layouts: 22.9 us -> 20.8 us
  other arithmetic: 8.73 us -> 10.4 us
  waiting for transfers between devices: 60.8 us -> 59.2 us
    pallas_call x2, Pallas kernels: 9.02 us -> 12.2 us  [substep(): pl.pallas_call(substep_kernel, out_shape=[jax.ShapeDtypeStruct(one, state...]
    all_to_all x1, starting transfers between devices: 7.48 us -> 5.46 us  [shards(): stage = lax.all_to_all(pick(restricted[None], back), 'gz', 0, 0, tiled=True)]
    ppermute x12, waiting for transfers between devices: 5.51 us -> 3.69 us  [shift_in(): return lax.ppermute(plane, axis, pairs)]
    ppermute x12, starting transfers between devices: 16.1 us -> 17.9 us  [shift_in(): return lax.ppermute(plane, axis, pairs)]
    broadcast_in_dim x6 -> x2, local copies, waits for them, and re-layouts: 1.79 us -> 0.18 us  [the longest x1 0.09 us: ghost_inputs(): jnp.where(chosen[1], shift_in(ox[1], 'gx', False), side[1])]
    another operation x4 -> x12, other arithmetic: 1.34 us -> 2.95 us  [the longest x6 1.64 us: ghost_inputs(): jnp.stack([jnp.where(chosen[2], shift_in(oy[0], 'gy', True), side[2]), jn...]
  transfers between devices with their start and end apart: 16 -> 16, of which waited for: 8 -> 7; matrix products, arithmetic and copies ran while one was open for 11% -> 12% of each run, Pallas kernels for 0% -> 0%
where the time goes in v4:
time: 151 us
  waiting for transfers between devices  59.2 us (39%)
  starting transfers between devices  42.4 us (28%)
  local copies, waits for them, and re-layouts  20.8 us (14%)
  Pallas kernels  12.2 us (8%)
  other arithmetic  10.4 us (7%)
  matrix products  4.53 us (3%)
    all_to_all x1, waiting for transfers between devices, shards(): stage = lax.all_to_all(pick(stage, home), 'gy', 0, 0, tiled=True)  20.9 us
    all_to_all x1, waiting for transfers between devices, shards(): stage = lax.all_to_all(pick(levels[None], first), 'gy', 0, 0, tiled=True)  18.2 us
    ppermute x12, starting transfers between devices, shift_in(): return lax.ppermute(plane, axis, pairs)  17.9 us
    pallas_call x2, Pallas kernels, substep(): pl.pallas_call(substep_kernel, out_shape=[jax.ShapeDtypeStruct(one, state...  12.2 us
    gather x6, local copies, waits for them, and re-layouts, pick(): jnp.take(flat, index.reshape(-1), axis=0, mode='clip')  8.82 us
    all_to_all x1, waiting for transfers between devices, shards(): stage = lax.all_to_all(pick(stage, second), 'gz', 0, 0, tiled=True)  8.62 us
    all_to_all x1, starting transfers between devices, shards(): stage = lax.all_to_all(pick(levels[None], first), 'gy', 0, 0, tiled=True)  8.6 us
    all_to_all x1, waiting for transfers between devices, shards(): stage = lax.all_to_all(pick(restricted[None], back), 'gz', 0, 0, tiled=True)  7.7 us
  transfers between devices with their start and end apart: 16, of which 7 were waited for; matrix products, arithmetic and copies ran while one was open for 12% of the time, Pallas kernels for 0%

profile of v4, /device:TPU:8, one launch (start us, length us, event | category | flops | bytes accessed | tf_op | source)
XLA Modules:
  0.0 150.7 jit_solution(8365186679404424075)
XLA Ops:
  0.7 0.7 and_select_fusion
  1.4 0.7 add_select_fusion.3
  2.1 0.7 broadcast_compare_fusion
  4.2 0.9 fusion.60
  5.0 1.9 %gather_fusion = f32[64,3840]{1,0:T(8,128)} fusion(f32[8,3840]{1,0:T(8,128)S(1)} %pad_maximum_fusion, s32[1024]{0:T(1024)S(1)} %pad_clamp_fusion.6), kind=kCustom, calls=%fused_computation | custom fusion | bytes 1966336 | tf_op jit(solution)/shard_map/jit(_take)/gather | solution.py:197
  6.9 8.6 %all-to-all-start = ((f32[8,8,3840]{2,1,0:T(8,128)}), f32[8,8,3840]{2,1,0:T(8,128)S(1)}, u32[]{:S(2)}, u32[]{:S(2)}) async-start(f32[8,8,3840]{2,1,0:T(8,128)} %bitcast.8), calls=%async_computation | async-start | bytes 1966080 | tf_op jit(solution)/shard_map/all_to_all | solution.py:250
  16.4 3.4 %collective-permute-start.3 = (f32[16,5,1,128]{3,2,1,0:T(1,128)S(1)}, f32[16,5,1,128]{3,2,1,0:T(1,128)S(1)}, u32[]{:S(2)}, u32[]{:S(2)}) collective-permute-start(f32[16,5,1,128]{3,2,1,0:T(1,128)S(1)} %get-tuple-element.43), channel_id=1, source_target_pairs={{8,0},{16,8},{24,16},{32,24},{40,32},{48,40},{56,48},{0,56},{9,1},... | collective-permute-start | bytes 122888 | tf_op jit(solution)/shard_map/ppermute | solution.py:20
  19.9 1.5 collective-permute-start
  21.4 1.7 %collective-permute-start.1 = (f32[5,16,128]{2,1,0:T(8,128)S(1)}, f32[5,16,128]{2,1,0:T(8,128)S(1)}, u32[]{:S(2)}, u32[]{:S(2)}) collective-permute-start(f32[5,16,128]{2,1,0:T(8,128)S(1)} %get-tuple-element.29), channel_id=1, source_target_pairs={{64,0},{128,64},{192,128},{0,192},{65,1},{129,65},{193,129},{1,193... | collective-permute-start | bytes 122888 | tf_op jit(solution)/shard_map/ppermute | solution.py:20
  24.5 0.6 gather_fusion.2
  25.1 0.7 gather_fusion.3
  25.9 18.2 %all-to-all-done = f32[8,8,3840]{2,1,0:T(8,128)S(1)} async-done(((f32[8,8,3840]{2,1,0:T(8,128)}), f32[8,8,3840]{2,1,0:T(8,128)S(1)}, u32[]{:S(2)}, u32[]{:S(2)}) %all-to-all-start) | async-done | bytes 983072 | tf_op jit(solution)/shard_map/all_to_all | solution.py:250
  44.1 1.9 %gather_fusion.1 = f32[64,3840]{1,0:T(8,128)} fusion(f32[64,3840]{1,0:T(8,128)S(1)} %bitcast.203, s32[1024]{0:T(1024)S(1)} %pad_clamp_fusion.5), kind=kCustom, calls=%fused_computation.1 | custom fusion | bytes 1966336 | tf_op jit(solution)/shard_map/jit(_take)/gather | solution.py:197
  46.0 4.9 %all-to-all-start.1 = ((f32[8,8,3840]{2,1,0:T(8,128)}), f32[8,8,3840]{2,1,0:T(8,128)S(1)}, u32[]{:S(2)}, u32[]{:S(2)}) async-start(f32[8,8,3840]{2,1,0:T(8,128)} %bitcast.11), calls=%async_computation.1 | async-start | bytes 1966080 | tf_op jit(solution)/shard_map/all_to_all | solution.py:252
  53.2 8.6 %all-to-all-done.1 = f32[8,8,3840]{2,1,0:T(8,128)S(1)} async-done(((f32[8,8,3840]{2,1,0:T(8,128)}), f32[8,8,3840]{2,1,0:T(8,128)S(1)}, u32[]{:S(2)}, u32[]{:S(2)}) %all-to-all-start.1) | async-done | bytes 983072 | tf_op jit(solution)/shard_map/all_to_all | solution.py:252
  61.8 0.6 gather_fusion.4
  62.4 1.1 reshape.872
  63.7 0.8 copy.109
  66.1 1.2 convolution_bitcast_fusion.1
  67.8 0.8 convolution_bitcast_fusion
  68.6 1.1 collective-permute-start.4
  69.9 0.7 pad_maximum_fusion.2.gy_ref
  70.6 0.6 pad_maximum_fusion.1.gx_ref
  71.2 1.5 collective-permute-done.4
  72.7 1.2 fusion.7.zfix_ref
  74.0 0.6 broadcast_in_dim.270.zflag_ref
  74.6 6.1 %shard_map.59 = (f32[5,16,16,128]{3,2,1,0:T(8,128)}, f32[2,5,16,128]{3,2,1,0:T(8,128)}, f32[2,16,5,1,128]{4,3,2,1,0:T(1,128)}, f32[2,5,16,16,1]{4,3,2,1,0:T(8,128)}) custom-call(f32[5,16,16,128]{3,2,1,0:T(8,128)} %u_ref.1, f32[2,5,16,128]{3,2,1,0:T(8,128)} %pad_maximum_fusion.1.gx_ref, f32[2,16,5,1,128]{4,3,2,1,0:T(1,128)} %pad_maximum_fusion.2.gy_ref, ...), custom_call_target="tpu_custom_call" | custom-call | tf_op jit(solution)/shard_map/pallas_call | solution.py:110
  80.6 0.8 slice_bitcast_fusion.18
  81.5 1.5 collective-permute-start.6
  83.0 1.7 %collective-permute-start.7 = (f32[5,16,128]{2,1,0:T(8,128)S(1)}, f32[5,16,128]{2,1,0:T(8,128)S(1)}, u32[]{:S(2)}, u32[]{:S(2)}) collective-permute-start(f32[5,16,128]{2,1,0:T(8,128)S(1)} %get-tuple-element.41), channel_id=1, source_target_pairs={{64,0},{128,64},{192,128},{0,192},{65,1},{129,65},{193,129},{1,193... | collective-permute-start | bytes 122888 | tf_op jit(solution)/shard_map/ppermute | solution.py:20
  84.7 1.7 %slice_reduce_fusion.1 = (f32[5,16,16]{2,1,0:T(8,128)S(1)}, f32[5,16,16]{2,1,0:T(8,128)S(1)}) fusion(f32[2,5,16,16,1]{4,3,2,1,0:T(8,128)} %get-tuple-element.10), kind=kLoop, calls=%fused_computation.28 | loop fusion | bytes 20480 | tf_op jit(solution)/shard_map/slice | solution.py:163
  86.4 3.4 %collective-permute-start.11 = (f32[5,16,16,1]{2,1,0,3:T(8,128)S(1)}, f32[5,16,16,1]{2,1,0,3:T(8,128)S(1)}, u32[]{:S(2)}, u32[]{:S(2)}) collective-permute-start(f32[5,16,16,1]{2,1,0,3:T(8,128)S(1)} %bitcast.220), channel_id=1, source_target_pairs={{1,0},{2,1},{3,2},{4,3},{5,4},{6,5},{7,6},{0,7},{9,8},{10,9},{11,1... | collective-permute-start | bytes 15368 | tf_op jit(solution)/shard_map/ppermute | solution.py:20
  90.0 1.6 %collective-permute-done.11 = f32[5,16,16,1]{2,1,0,3:T(8,128)S(1)} collective-permute-done((f32[5,16,16,1]{2,1,0,3:T(8,128)S(1)}, f32[5,16,16,1]{2,1,0,3:T(8,128)S(1)}, u32[]{:S(2)}, u32[]{:S(2)}) %collective-permute-start.11) | collective-permute-done | bytes 5152 | tf_op jit(solution)/shard_map/ppermute | solution.py:20
  91.5 2.3 %collective-permute-start.9 = (f32[16,5,1,128]{3,2,1,0:T(1,128)S(1)}, f32[16,5,1,128]{3,2,1,0:T(1,128)S(1)}, u32[]{:S(2)}, u32[]{:S(2)}) collective-permute-start(f32[16,5,1,128]{3,2,1,0:T(1,128)S(1)} %get-tuple-element.39), channel_id=1, source_target_pairs={{8,0},{16,8},{24,16},{32,24},{40,32},{48,40},{56,48},{0,56},{9,1},... | collective-permute-start | bytes 122888 | tf_op jit(solution)/shard_map/ppermute | solution.py:20
  93.8 1.2 fusion.5.zfix_ref
  95.1 0.6 collective-permute-done.8
  95.8 0.6 pad_maximum_fusion.3.gx_ref
  96.5 0.7 pad_maximum_fusion.4.gy_ref
  97.2 6.1 %shard_map.60 = (f32[5,16,16,128]{3,2,1,0:T(8,128)}, f32[2,5,16,128]{3,2,1,0:T(8,128)}, f32[2,16,5,1,128]{4,3,2,1,0:T(1,128)}, f32[2,5,16,16,1]{4,3,2,1,0:T(8,128)}) custom-call(f32[5,16,16,128]{3,2,1,0:T(8,128)} %get-tuple-element.7.u_ref, f32[2,5,16,128]{3,2,1,0:T(8,128)} %pad_maximum_fusion.3.gx_ref, f32[2,16,5,1,128]{4,3,2,1,0:T(1,128)} %pad_maximum_fusion.4.gy_ref, ...), custom_call_target="tpu_custom_call" | custom-call | tf_op jit(solution)/shard_map/pallas_call | solution.py:110
  103.3 1.3 fusion.11
  105.5 0.7 reshape_broadcast_in_dim_reshape.3
  106.2 1.6 %gather_fusion.5 = f32[64,2560]{1,0:T(8,128)} fusion(f32[8,2560]{1,0:T(8,128)S(1)} %reshape_broadcast_in_dim_reshape.3, s32[1024]{0:T(1024)S(1)} %pad_clamp_fusion.2), kind=kCustom, calls=%fused_computation.5 | custom fusion | bytes 1310976 | tf_op jit(solution)/shard_map/jit(_take)/gather | solution.py:197
  107.8 5.5 %all-to-all-start.2 = ((f32[8,8,2560]{2,1,0:T(8,128)}), f32[8,8,2560]{2,1,0:T(8,128)S(1)}, u32[]{:S(2)}, u32[]{:S(2)}) async-start(f32[8,8,2560]{2,1,0:T(8,128)} %bitcast.73), calls=%async_computation.2 | async-start | bytes 1310720 | tf_op jit(solution)/shard_map/all_to_all | solution.py:270
  113.4 7.7 %all-to-all-done.2 = f32[8,8,2560]{2,1,0:T(8,128)S(1)} async-done(((f32[8,8,2560]{2,1,0:T(8,128)}), f32[8,8,2560]{2,1,0:T(8,128)S(1)}, u32[]{:S(2)}, u32[]{:S(2)}) %all-to-all-start.2) | async-done | bytes 655392 | tf_op jit(solution)/shard_map/all_to_all | solution.py:270
  121.1 1.6 %gather_fusion.6 = f32[64,2560]{1,0:T(8,128)} fusion(f32[64,2560]{1,0:T(8,128)S(1)} %bitcast.204, s32[1024]{0:T(1024)S(1)} %pad_clamp_fusion.1), kind=kCustom, calls=%fused_computation.6 | custom fusion | bytes 1310976 | tf_op jit(solution)/shard_map/jit(_take)/gather | solution.py:197
  122.7 5.6 %all-to-all-start.3 = ((f32[8,8,2560]{2,1,0:T(8,128)}), f32[8,8,2560]{2,1,0:T(8,128)S(1)}, u32[]{:S(2)}, u32[]{:S(2)}) async-start(f32[8,8,2560]{2,1,0:T(8,128)} %bitcast.75), calls=%async_computation.3 | async-start | bytes 1310720 | tf_op jit(solution)/shard_map/all_to_all | solution.py:272
  128.5 20.9 %all-to-all-done.3 = f32[8,8,2560]{2,1,0:T(8,128)S(1)} async-done(((f32[8,8,2560]{2,1,0:T(8,128)}), f32[8,8,2560]{2,1,0:T(8,128)S(1)}, u32[]{:S(2)}, u32[]{:S(2)}) %all-to-all-start.3) | async-done | bytes 655392 | tf_op jit(solution)/shard_map/all_to_all | solution.py:272
  149.5 1.2 gather_fusion.7
  (111 shorter events, 9.8 us)
Async XLA Ops:
  6.9 8.6 %copy-start = (f32[5,16,16,128]{3,2,1,0:T(8,128)S(1)}, f32[5,16,16,128]{3,2,1,0:T(8,128)}, u32[]{:S(2)}) copy-start(f32[5,16,16,128]{3,2,1,0:T(8,128)} %u_ref.1) | copy-start | bytes 1966084
  6.9 37.2 %all-to-all-start = ((f32[8,8,3840]{2,1,0:T(8,128)}), f32[8,8,3840]{2,1,0:T(8,128)S(1)}, u32[]{:S(2)}, u32[]{:S(2)}) async-start(f32[8,8,3840]{2,1,0:T(8,128)} %bitcast.8), calls=%async_computation | async-start | bytes 1966080 | tf_op jit(solution)/shard_map/all_to_all | solution.py:250
  15.8 52.8 %collective-permute-start.2 = (f32[16,5,1,128]{3,2,1,0:T(1,128)S(1)}, f32[16,5,1,128]{3,2,1,0:T(1,128)S(1)}, u32[]{:S(2)}, u32[]{:S(2)}) collective-permute-start(f32[16,5,1,128]{3,2,1,0:T(1,128)S(1)} %get-tuple-element.42), channel_id=1, source_target_pairs={{0,8},{8,16},{16,24},{24,32},{32,40},{40,48},{48,56},{56,0},{1,9},... | collective-permute-start | bytes 122888 | tf_op jit(solution)/shard_map/ppermute | solution.py:20
  16.4 53.3 %collective-permute-start.3 = (f32[16,5,1,128]{3,2,1,0:T(1,128)S(1)}, f32[16,5,1,128]{3,2,1,0:T(1,128)S(1)}, u32[]{:S(2)}, u32[]{:S(2)}) collective-permute-start(f32[16,5,1,128]{3,2,1,0:T(1,128)S(1)} %get-tuple-element.43), channel_id=1, source_target_pairs={{8,0},{16,8},{24,16},{32,24},{40,32},{48,40},{56,48},{0,56},{9,1},... | collective-permute-start | bytes 122888 | tf_op jit(solution)/shard_map/ppermute | solution.py:20
  19.9 50.0 %collective-permute-start = (f32[5,16,128]{2,1,0:T(8,128)S(1)}, f32[5,16,128]{2,1,0:T(8,128)S(1)}, u32[]{:S(2)}, u32[]{:S(2)}) collective-permute-start(f32[5,16,128]{2,1,0:T(8,128)S(1)} %get-tuple-element.28), channel_id=1, source_target_pairs={{0,64},{64,128},{128,192},{192,0},{1,65},{65,129},{129,193},{193,1... | collective-permute-start | bytes 122888 | tf_op jit(solution)/shard_map/ppermute | solution.py:20
  21.4 49.2 %collective-permute-start.1 = (f32[5,16,128]{2,1,0:T(8,128)S(1)}, f32[5,16,128]{2,1,0:T(8,128)S(1)}, u32[]{:S(2)}, u32[]{:S(2)}) collective-permute-start(f32[5,16,128]{2,1,0:T(8,128)S(1)} %get-tuple-element.29), channel_id=1, source_target_pairs={{64,0},{128,64},{192,128},{0,192},{65,1},{129,65},{193,129},{1,193... | collective-permute-start | bytes 122888 | tf_op jit(solution)/shard_map/ppermute | solution.py:20
  23.3 2.4 %copy-start.3 = (s32[6,1,1,8]{3,2,1,0:T(1,128)S(1)}, s32[6,1,1,8]{3,2,1,0:T(1,128)}, u32[]{:S(2)}) copy-start(s32[6,1,1,8]{3,2,1,0:T(1,128)} %param.7) | copy-start | bytes 580
  23.9 47.3 %collective-permute-start.5 = (f32[5,16,16,1]{2,1,0,3:T(8,128)S(1)}, f32[5,16,16,1]{2,1,0,3:T(8,128)S(1)}, u32[]{:S(2)}, u32[]{:S(2)}) collective-permute-start(f32[5,16,16,1]{2,1,0,3:T(8,128)S(1)} %copy.142), channel_id=1, source_target_pairs={{1,0},{2,1},{3,2},{4,3},{5,4},{6,5},{7,6},{0,7},{9,8},{10,9},{11,1... | collective-permute-start | bytes 15368 | tf_op jit(solution)/shard_map/ppermute | solution.py:20
  46.0 15.9 %all-to-all-start.1 = ((f32[8,8,3840]{2,1,0:T(8,128)}), f32[8,8,3840]{2,1,0:T(8,128)S(1)}, u32[]{:S(2)}, u32[]{:S(2)}) async-start(f32[8,8,3840]{2,1,0:T(8,128)} %bitcast.11), calls=%async_computation.1 | async-start | bytes 1966080 | tf_op jit(solution)/shard_map/all_to_all | solution.py:252
  68.6 4.1 %collective-permute-start.4 = (f32[5,16,16,1]{2,1,0,3:T(8,128)S(1)}, f32[5,16,16,1]{2,1,0,3:T(8,128)S(1)}, u32[]{:S(2)}, u32[]{:S(2)}) collective-permute-start(f32[5,16,16,1]{2,1,0,3:T(8,128)S(1)} %copy.141), channel_id=1, source_target_pairs={{0,1},{1,2},{2,3},{3,4},{4,5},{5,6},{6,7},{7,0},{8,9},{9,10},{10,1... | collective-permute-start | bytes 15368 | tf_op jit(solution)/shard_map/ppermute | solution.py:20
  80.6 9.2 %copy-start.1 = (f32[2,16,5,1,128]{4,3,2,1,0:T(1,128)S(1)}, f32[2,16,5,1,128]{4,3,2,1,0:T(1,128)}, u32[]{:S(2)}) copy-start(f32[2,16,5,1,128]{4,3,2,1,0:T(1,128)} %get-tuple-element.9) | copy-start | bytes 245764
  81.5 14.3 %collective-permute-start.6 = (f32[5,16,128]{2,1,0:T(8,128)S(1)}, f32[5,16,128]{2,1,0:T(8,128)S(1)}, u32[]{:S(2)}, u32[]{:S(2)}) collective-permute-start(f32[5,16,128]{2,1,0:T(8,128)S(1)} %get-tuple-element.40), channel_id=1, source_target_pairs={{0,64},{64,128},{128,192},{192,0},{1,65},{65,129},{129,193},{193,1... | collective-permute-start | bytes 122888 | tf_op jit(solution)/shard_map/ppermute | solution.py:20
  83.0 12.8 %collective-permute-start.7 = (f32[5,16,128]{2,1,0:T(8,128)S(1)}, f32[5,16,128]{2,1,0:T(8,128)S(1)}, u32[]{:S(2)}, u32[]{:S(2)}) collective-permute-start(f32[5,16,128]{2,1,0:T(8,128)S(1)} %get-tuple-element.41), channel_id=1, source_target_pairs={{64,0},{128,64},{192,128},{0,192},{65,1},{129,65},{193,129},{1,193... | collective-permute-start | bytes 122888 | tf_op jit(solution)/shard_map/ppermute | solution.py:20
  86.4 5.1 %collective-permute-start.11 = (f32[5,16,16,1]{2,1,0,3:T(8,128)S(1)}, f32[5,16,16,1]{2,1,0,3:T(8,128)S(1)}, u32[]{:S(2)}, u32[]{:S(2)}) collective-permute-start(f32[5,16,16,1]{2,1,0,3:T(8,128)S(1)} %bitcast.220), channel_id=1, source_target_pairs={{1,0},{2,1},{3,2},{4,3},{5,4},{6,5},{7,6},{0,7},{9,8},{10,9},{11,1... | collective-permute-start | bytes 15368 | tf_op jit(solution)/shard_map/ppermute | solution.py:20
  89.8 4.0 %collective-permute-start.10 = (f32[5,16,16,1]{2,1,0,3:T(8,128)S(1)}, f32[5,16,16,1]{2,1,0,3:T(8,128)S(1)}, u32[]{:S(2)}, u32[]{:S(2)}) collective-permute-start(f32[5,16,16,1]{2,1,0,3:T(8,128)S(1)} %bitcast.218), channel_id=1, source_target_pairs={{0,1},{1,2},{2,3},{3,4},{4,5},{5,6},{6,7},{7,0},{8,9},{9,10},{10,1... | collective-permute-start | bytes 15368 | tf_op jit(solution)/shard_map/ppermute | solution.py:20
  89.9 5.8 %collective-permute-start.8 = (f32[16,5,1,128]{3,2,1,0:T(1,128)S(1)}, f32[16,5,1,128]{3,2,1,0:T(1,128)S(1)}, u32[]{:S(2)}, u32[]{:S(2)}) collective-permute-start(f32[16,5,1,128]{3,2,1,0:T(1,128)S(1)} %get-tuple-element.38), channel_id=1, source_target_pairs={{0,8},{8,16},{16,24},{24,32},{32,40},{40,48},{48,56},{56,0},{1,9},... | collective-permute-start | bytes 122888 | tf_op jit(solution)/shard_map/ppermute | solution.py:20
  91.5 4.9 %collective-permute-start.9 = (f32[16,5,1,128]{3,2,1,0:T(1,128)S(1)}, f32[16,5,1,128]{3,2,1,0:T(1,128)S(1)}, u32[]{:S(2)}, u32[]{:S(2)}) collective-permute-start(f32[16,5,1,128]{3,2,1,0:T(1,128)S(1)} %get-tuple-element.39), channel_id=1, source_target_pairs={{8,0},{16,8},{24,16},{32,24},{40,32},{48,40},{56,48},{0,56},{9,1},... | collective-permute-start | bytes 122888 | tf_op jit(solution)/shard_map/ppermute | solution.py:20
  107.8 13.2 %all-to-all-start.2 = ((f32[8,8,2560]{2,1,0:T(8,128)}), f32[8,8,2560]{2,1,0:T(8,128)S(1)}, u32[]{:S(2)}, u32[]{:S(2)}) async-start(f32[8,8,2560]{2,1,0:T(8,128)} %bitcast.73), calls=%async_computation.2 | async-start | bytes 1310720 | tf_op jit(solution)/shard_map/all_to_all | solution.py:270
  122.7 5.6 %copy-start.2 = (s32[1,512]{1,0:T(1,128)S(1)}, s32[1,512]{1,0:T(1,128)}, u32[]{:S(2)}) copy-start(s32[1,512]{1,0:T(1,128)} %param.6) | copy-start | bytes 6148
  122.7 26.7 %all-to-all-start.3 = ((f32[8,8,2560]{2,1,0:T(8,128)}), f32[8,8,2560]{2,1,0:T(8,128)S(1)}, u32[]{:S(2)}, u32[]{:S(2)}) async-start(f32[8,8,2560]{2,1,0:T(8,128)} %bitcast.75), calls=%async_computation.3 | async-start | bytes 1310720 | tf_op jit(solution)/shard_map/all_to_all | solution.py:272

commit v5 on v3

--- a/solution.py
+++ b/solution.py
@@ -31,7 +31,7 @@
 
 
 def flux_of(v, prim, direc):
-    rho, mx, my, mz, energy = v
+    _, mx, my, mz, energy = v
     vel, press, sound = prim
     normal = vel[direc]
     mom = (mx, my, mz)
@@ -119,8 +119,14 @@
 
 
 def ghost_inputs(state, side, ends, links):
-    nz_dev = state.shape[3]
     chosen = [jnp.repeat(links[:, face] == 1, BS)[None, None, :] for face in range(4)]
+    far_lo = shift_in(state[..., -1], "gz", True)
+    far_hi = shift_in(state[..., 0], "gz", False)
+    gx, gy = xy_ghosts(state, side, chosen)
+    return finish_ghosts(state, gx, gy, far_lo, far_hi, ends, links)
+
+
+def xy_ghosts(state, side, chosen):
     gx = jnp.stack(
         [
             jnp.where(chosen[0], shift_in(state[:, -1], "gx", True), side[0]),
@@ -133,9 +139,11 @@
             jnp.where(chosen[3], shift_in(state[:, :, 0], "gy", False), side[3]),
         ]
     )
-    gy = gy.transpose(0, 2, 1, 3)[:, :, :, None, :]
-    far_lo = shift_in(state[..., -1], "gz", True)
-    far_hi = shift_in(state[..., 0], "gz", False)
+    return gx, gy.transpose(0, 2, 1, 3)[:, :, :, None, :]
+
+
+def finish_ghosts(state, gx, gy, far_lo, far_hi, ends, links):
+    nz_dev = state.shape[3]
     lane = jnp.arange(nz_dev, dtype=jnp.int32)
     at_lo = lane % BS == 0
     at_hi = lane % BS == BS - 1
@@ -247,6 +255,10 @@
 
 
 def solution(mesh):
+    return step_of(mesh)
+
+
+def step_of(mesh):
     return jax.shard_map(
         shards,
         mesh=mesh,

time: 149 us -> 149 us (level)
  no operation moved by 1% of the time
where the time goes in v5:
time: 149 us
  waiting for transfers between devices  60.8 us (41%)
  starting transfers between devices  41.7 us (28%)
  local copies, waits for them, and re-layouts  22.9 us (15%)
  Pallas kernels  9.02 us (6%)
  other arithmetic  8.73 us (6%)
  matrix products  4.52 us (3%)
    all_to_all x1, waiting for transfers between devices, shards(): stage = lax.all_to_all(pick(stage, home), 'gy', 0, 0, tiled=True)  20.9 us
    all_to_all x1, waiting for transfers between devices, shards(): stage = lax.all_to_all(pick(levels[None], first), 'gy', 0, 0, tiled=True)  18.5 us
    ppermute x12, starting transfers between devices, shift_in(): return lax.ppermute(plane, axis, pairs)  16.1 us
    pallas_call x2, Pallas kernels, substep(): pl.pallas_call(substep_kernel, out_shape=jax.ShapeDtypeStruct(state.shape...  9.02 us
    gather x6, local copies, waits for them, and re-layouts, pick(): jnp.take(flat, index.reshape(-1), axis=0, mode='clip')  8.75 us
    all_to_all x1, waiting for transfers between devices, shards(): stage = lax.all_to_all(pick(stage, second), 'gz', 0, 0, tiled=True)  8.62 us
    all_to_all x1, starting transfers between devices, shards(): stage = lax.all_to_all(pick(levels[None], first), 'gy', 0, 0, tiled=True)  8.6 us
    all_to_all x1, starting transfers between devices, shards(): stage = lax.all_to_all(pick(restricted[None], back), 'gz', 0, 0, tiled=True)  7.48 us
  transfers between devices with their start and end apart: 16, of which 8 were waited for; matrix products, arithmetic and copies ran while one was open for 11% of the time, Pallas kernels for 0%

profile of v5, /device:TPU:8, one launch (start us, length us, event | category | flops | bytes accessed | tf_op | source)
XLA Modules:
  0.0 148.7 jit_solution(14077670313706488112)
XLA Ops:
  0.7 0.7 and_select_fusion
  1.4 0.7 add_select_fusion.3
  2.1 0.7 broadcast_compare_fusion
  4.2 0.9 fusion.67
  5.0 1.8 %gather_fusion = f32[64,3840]{1,0:T(8,128)} fusion(f32[8,3840]{1,0:T(8,128)S(1)} %pad_maximum_fusion, s32[1024]{0:T(1024)S(1)} %pad_clamp_fusion.6), kind=kCustom, calls=%fused_computation | custom fusion | bytes 1966336 | tf_op jit(solution)/shard_map/jit(_take)/gather | solution.py:179
  6.9 8.6 %all-to-all-start = ((f32[8,8,3840]{2,1,0:T(8,128)}), f32[8,8,3840]{2,1,0:T(8,128)S(1)}, u32[]{:S(2)}, u32[]{:S(2)}) async-start(f32[8,8,3840]{2,1,0:T(8,128)} %bitcast.8), calls=%async_computation | async-start | bytes 1966080 | tf_op jit(solution)/shard_map/all_to_all | solution.py:232
  15.6 3.9 %collective-permute-start.3 = (f32[5,16,128]{2,1,0:T(8,128)S(1)}, f32[5,16,128]{2,1,0:T(8,128)S(1)}, u32[]{:S(2)}, u32[]{:S(2)}) collective-permute-start(f32[5,16,128]{2,1,0:T(8,128)S(1)} %bitcast.223), channel_id=1, source_target_pairs={{8,0},{16,8},{24,16},{32,24},{40,32},{48,40},{56,48},{0,56},{9,1},... | collective-permute-start | bytes 122888 | tf_op jit(solution)/shard_map/ppermute | solution.py:20
  19.5 1.6 %collective-permute-start = (f32[5,16,128]{2,1,0:T(8,128)S(1)}, f32[5,16,128]{2,1,0:T(8,128)S(1)}, u32[]{:S(2)}, u32[]{:S(2)}) collective-permute-start(f32[5,16,128]{2,1,0:T(8,128)S(1)} %get-tuple-element.22), channel_id=1, source_target_pairs={{0,64},{64,128},{128,192},{192,0},{1,65},{65,129},{129,193},{193,1... | collective-permute-start | bytes 122888 | tf_op jit(solution)/shard_map/ppermute | solution.py:20
  21.1 1.7 %collective-permute-start.1 = (f32[5,16,128]{2,1,0:T(8,128)S(1)}, f32[5,16,128]{2,1,0:T(8,128)S(1)}, u32[]{:S(2)}, u32[]{:S(2)}) collective-permute-start(f32[5,16,128]{2,1,0:T(8,128)S(1)} %get-tuple-element.23), channel_id=1, source_target_pairs={{64,0},{128,64},{192,128},{0,192},{65,1},{129,65},{193,129},{1,193... | collective-permute-start | bytes 122888 | tf_op jit(solution)/shard_map/ppermute | solution.py:20
  24.2 0.6 gather_fusion.2
  24.8 0.7 gather_fusion.3
  25.6 18.5 %all-to-all-done = f32[8,8,3840]{2,1,0:T(8,128)S(1)} async-done(((f32[8,8,3840]{2,1,0:T(8,128)}), f32[8,8,3840]{2,1,0:T(8,128)S(1)}, u32[]{:S(2)}, u32[]{:S(2)}) %all-to-all-start) | async-done | bytes 983072 | tf_op jit(solution)/shard_map/all_to_all | solution.py:232
  44.1 1.8 %gather_fusion.1 = f32[64,3840]{1,0:T(8,128)} fusion(f32[64,3840]{1,0:T(8,128)S(1)} %bitcast.214, s32[1024]{0:T(1024)S(1)} %pad_clamp_fusion.5), kind=kCustom, calls=%fused_computation.1 | custom fusion | bytes 1966336 | tf_op jit(solution)/shard_map/jit(_take)/gather | solution.py:179
  46.0 4.9 %all-to-all-start.1 = ((f32[8,8,3840]{2,1,0:T(8,128)}), f32[8,8,3840]{2,1,0:T(8,128)S(1)}, u32[]{:S(2)}, u32[]{:S(2)}) async-start(f32[8,8,3840]{2,1,0:T(8,128)} %bitcast.11), calls=%async_computation.1 | async-start | bytes 1966080 | tf_op jit(solution)/shard_map/all_to_all | solution.py:234
  53.2 8.6 %all-to-all-done.1 = f32[8,8,3840]{2,1,0:T(8,128)S(1)} async-done(((f32[8,8,3840]{2,1,0:T(8,128)}), f32[8,8,3840]{2,1,0:T(8,128)S(1)}, u32[]{:S(2)}, u32[]{:S(2)}) %all-to-all-start.1) | async-done | bytes 983072 | tf_op jit(solution)/shard_map/all_to_all | solution.py:234
  61.8 0.6 gather_fusion.4
  62.4 1.1 reshape.864
  63.7 0.8 copy.71
  65.1 1.2 convolution_bitcast_fusion.1
  66.8 0.8 convolution_bitcast_fusion
  68.2 1.1 collective-permute-start.4
  69.3 0.6 pad_maximum_fusion.1.gx_ref
  70.0 0.7 copy.80.gy_ref
  70.7 1.6 %collective-permute-done.4 = f32[5,16,16]{2,1,0:T(8,128)S(1)} collective-permute-done((f32[5,16,16]{2,1,0:T(8,128)S(1)}, f32[5,16,16]{2,1,0:T(8,128)S(1)}, u32[]{:S(2)}, u32[]{:S(2)}) %collective-permute-start.4) | collective-permute-done | bytes 5152 | tf_op jit(solution)/shard_map/ppermute | solution.py:20
  72.2 1.2 fusion.7.zfix_ref
  73.5 0.6 broadcast_in_dim.270.zflag_ref
  74.1 4.5 %shard_map.59.u_ref = f32[5,16,16,128]{3,2,1,0:T(8,128)} custom-call(f32[5,16,16,128]{3,2,1,0:T(8,128)} %u_ref.1, f32[2,5,16,128]{3,2,1,0:T(8,128)} %pad_maximum_fusion.1.gx_ref, f32[2,16,5,1,128]{4,3,2,1,0:T(1,128)} %copy.80.gy_ref, f32[5,16,16,128]{3,2,1,0:T(8,128)} %fusion.7.zfix_ref, s32[2,16,128]{2,1,0:T(8,128)} %broadcast_in_dim.270.zflag_ref), custom_call_target="tpu_custom_call" | custom-call | tf_op jit(solution)/shard_map/pallas_call | solution.py:92
  78.6 1.9 %slice_reduce_fusion.1 = (f32[5,16,16]{2,1,0:T(8,128)S(1)}, f32[5,16,16]{2,1,0:T(8,128)S(1)}) fusion(f32[5,16,16,128]{3,2,1,0:T(8,128)} %shard_map.59.u_ref), kind=kLoop, calls=%fused_computation.24 | loop fusion | bytes 20480 | tf_op jit(solution)/shard_map/slice | solution.py:123
  80.5 1.1 fusion.64
  81.6 1.1 collective-permute-start.10
  82.7 2.4 %collective-permute-start.11 = (f32[5,16,16]{2,1,0:T(8,128)S(1)}, f32[5,16,16]{2,1,0:T(8,128)S(1)}, u32[]{:S(2)}, u32[]{:S(2)}) collective-permute-start(f32[5,16,16]{2,1,0:T(8,128)S(1)} %get-tuple-element.3), channel_id=1, source_target_pairs={{1,0},{2,1},{3,2},{4,3},{5,4},{6,5},{7,6},{0,7},{9,8},{10,9},{11,1... | collective-permute-start | bytes 15368 | tf_op jit(solution)/shard_map/ppermute | solution.py:20
  85.2 0.8 slice_bitcast_fusion.12
  86.0 1.5 %collective-permute-start.6 = (f32[5,16,128]{2,1,0:T(8,128)S(1)}, f32[5,16,128]{2,1,0:T(8,128)S(1)}, u32[]{:S(2)}, u32[]{:S(2)}) collective-permute-start(f32[5,16,128]{2,1,0:T(8,128)S(1)} %get-tuple-element.16), channel_id=1, source_target_pairs={{0,64},{64,128},{128,192},{192,0},{1,65},{65,129},{129,193},{193,1... | collective-permute-start | bytes 122888 | tf_op jit(solution)/shard_map/ppermute | solution.py:20
  87.5 1.7 %collective-permute-start.7 = (f32[5,16,128]{2,1,0:T(8,128)S(1)}, f32[5,16,128]{2,1,0:T(8,128)S(1)}, u32[]{:S(2)}, u32[]{:S(2)}) collective-permute-start(f32[5,16,128]{2,1,0:T(8,128)S(1)} %get-tuple-element.17), channel_id=1, source_target_pairs={{64,0},{128,64},{192,128},{0,192},{65,1},{129,65},{193,129},{1,193... | collective-permute-start | bytes 122888 | tf_op jit(solution)/shard_map/ppermute | solution.py:20
  89.7 1.3 fusion.5.zfix_ref
  91.5 3.5 %collective-permute-done.8 = f32[5,16,128]{2,1,0:T(8,128)S(1)} collective-permute-done((f32[5,16,128]{2,1,0:T(8,128)S(1)}, f32[5,16,128]{2,1,0:T(8,128)S(1)}, u32[]{:S(2)}, u32[]{:S(2)}) %collective-permute-start.8) | collective-permute-done | bytes 40992 | tf_op jit(solution)/shard_map/ppermute | solution.py:20
  95.0 0.7 copy.85.gy_ref
  95.7 0.6 pad_maximum_fusion.2.gx_ref
  96.3 4.5 %shard_map.60 = f32[5,16,16,128]{3,2,1,0:T(8,128)} custom-call(f32[5,16,16,128]{3,2,1,0:T(8,128)} %shard_map.59.u_ref, f32[2,5,16,128]{3,2,1,0:T(8,128)} %pad_maximum_fusion.2.gx_ref, f32[2,16,5,1,128]{4,3,2,1,0:T(1,128)} %copy.85.gy_ref, f32[5,16,16,128]{3,2,1,0:T(8,128)} %fusion.5.zfix_ref, s32[2,16,128]{2,1,0:T(8,128)} %broadcast_in_dim.270.zflag_ref), custom_call_target="tpu_custom_call" | custom-call | tf_op jit(solution)/shard_map/pallas_call | solution.py:92
  100.8 1.3 fusion.11
  103.0 0.7 reshape_broadcast_in_dim_reshape.3
  103.7 1.6 %gather_fusion.5 = f32[64,2560]{1,0:T(8,128)} fusion(f32[8,2560]{1,0:T(8,128)S(1)} %reshape_broadcast_in_dim_reshape.3, s32[1024]{0:T(1024)S(1)} %pad_clamp_fusion.2), kind=kCustom, calls=%fused_computation.5 | custom fusion | bytes 1310976 | tf_op jit(solution)/shard_map/jit(_take)/gather | solution.py:179
  105.3 7.5 %all-to-all-start.2 = ((f32[8,8,2560]{2,1,0:T(8,128)}), f32[8,8,2560]{2,1,0:T(8,128)S(1)}, u32[]{:S(2)}, u32[]{:S(2)}) async-start(f32[8,8,2560]{2,1,0:T(8,128)} %bitcast.66), calls=%async_computation.2 | async-start | bytes 1310720 | tf_op jit(solution)/shard_map/all_to_all | solution.py:248
  112.9 7.2 %all-to-all-done.2 = f32[8,8,2560]{2,1,0:T(8,128)S(1)} async-done(((f32[8,8,2560]{2,1,0:T(8,128)}), f32[8,8,2560]{2,1,0:T(8,128)S(1)}, u32[]{:S(2)}, u32[]{:S(2)}) %all-to-all-start.2) | async-done | bytes 655392 | tf_op jit(solution)/shard_map/all_to_all | solution.py:248
  120.2 1.6 %gather_fusion.6 = f32[64,2560]{1,0:T(8,128)} fusion(f32[64,2560]{1,0:T(8,128)S(1)} %bitcast.215, s32[1024]{0:T(1024)S(1)} %pad_clamp_fusion.1), kind=kCustom, calls=%fused_computation.6 | custom fusion | bytes 1310976 | tf_op jit(solution)/shard_map/jit(_take)/gather | solution.py:179
  121.8 4.6 %all-to-all-start.3 = ((f32[8,8,2560]{2,1,0:T(8,128)}), f32[8,8,2560]{2,1,0:T(8,128)S(1)}, u32[]{:S(2)}, u32[]{:S(2)}) async-start(f32[8,8,2560]{2,1,0:T(8,128)} %bitcast.68), calls=%async_computation.3 | async-start | bytes 1310720 | tf_op jit(solution)/shard_map/all_to_all | solution.py:250
  126.6 20.9 %all-to-all-done.3 = f32[8,8,2560]{2,1,0:T(8,128)S(1)} async-done(((f32[8,8,2560]{2,1,0:T(8,128)}), f32[8,8,2560]{2,1,0:T(8,128)S(1)}, u32[]{:S(2)}, u32[]{:S(2)}) %all-to-all-start.3) | async-done | bytes 655392 | tf_op jit(solution)/shard_map/all_to_all | solution.py:250
  147.5 1.2 gather_fusion.7
  (98 shorter events, 9.3 us)
Async XLA Ops:
  6.9 8.6 %copy-start = (f32[5,16,16,128]{3,2,1,0:T(8,128)S(1)}, f32[5,16,16,128]{3,2,1,0:T(8,128)}, u32[]{:S(2)}) copy-start(f32[5,16,16,128]{3,2,1,0:T(8,128)} %u_ref.1) | copy-start | bytes 1966084
  6.9 37.2 %all-to-all-start = ((f32[8,8,3840]{2,1,0:T(8,128)}), f32[8,8,3840]{2,1,0:T(8,128)S(1)}, u32[]{:S(2)}, u32[]{:S(2)}) async-start(f32[8,8,3840]{2,1,0:T(8,128)} %bitcast.8), calls=%async_computation | async-start | bytes 1966080 | tf_op jit(solution)/shard_map/all_to_all | solution.py:232
  15.6 52.6 %collective-permute-start.3 = (f32[5,16,128]{2,1,0:T(8,128)S(1)}, f32[5,16,128]{2,1,0:T(8,128)S(1)}, u32[]{:S(2)}, u32[]{:S(2)}) collective-permute-start(f32[5,16,128]{2,1,0:T(8,128)S(1)} %bitcast.223), channel_id=1, source_target_pairs={{8,0},{16,8},{24,16},{32,24},{40,32},{48,40},{56,48},{0,56},{9,1},... | collective-permute-start | bytes 122888 | tf_op jit(solution)/shard_map/ppermute | solution.py:20
  19.5 49.8 %collective-permute-start.2 = (f32[5,16,128]{2,1,0:T(8,128)S(1)}, f32[5,16,128]{2,1,0:T(8,128)S(1)}, u32[]{:S(2)}, u32[]{:S(2)}) collective-permute-start(f32[5,16,128]{2,1,0:T(8,128)S(1)} %bitcast.222), channel_id=1, source_target_pairs={{0,8},{8,16},{16,24},{24,32},{32,40},{40,48},{48,56},{56,0},{1,9},... | collective-permute-start | bytes 122888 | tf_op jit(solution)/shard_map/ppermute | solution.py:20
  19.5 49.8 %collective-permute-start = (f32[5,16,128]{2,1,0:T(8,128)S(1)}, f32[5,16,128]{2,1,0:T(8,128)S(1)}, u32[]{:S(2)}, u32[]{:S(2)}) collective-permute-start(f32[5,16,128]{2,1,0:T(8,128)S(1)} %get-tuple-element.22), channel_id=1, source_target_pairs={{0,64},{64,128},{128,192},{192,0},{1,65},{65,129},{129,193},{193,1... | collective-permute-start | bytes 122888 | tf_op jit(solution)/shard_map/ppermute | solution.py:20
  21.1 48.2 %collective-permute-start.1 = (f32[5,16,128]{2,1,0:T(8,128)S(1)}, f32[5,16,128]{2,1,0:T(8,128)S(1)}, u32[]{:S(2)}, u32[]{:S(2)}) collective-permute-start(f32[5,16,128]{2,1,0:T(8,128)S(1)} %get-tuple-element.23), channel_id=1, source_target_pairs={{64,0},{128,64},{192,128},{0,192},{65,1},{129,65},{193,129},{1,193... | collective-permute-start | bytes 122888 | tf_op jit(solution)/shard_map/ppermute | solution.py:20
  23.1 2.4 %copy-start.2 = (s32[6,1,1,8]{3,2,1,0:T(1,128)S(1)}, s32[6,1,1,8]{3,2,1,0:T(1,128)}, u32[]{:S(2)}) copy-start(s32[6,1,1,8]{3,2,1,0:T(1,128)} %param.7) | copy-start | bytes 580
  23.6 47.1 %collective-permute-start.5 = (f32[5,16,16]{2,1,0:T(8,128)S(1)}, f32[5,16,16]{2,1,0:T(8,128)S(1)}, u32[]{:S(2)}, u32[]{:S(2)}) collective-permute-start(f32[5,16,16]{2,1,0:T(8,128)S(1)} %bitcast.226), channel_id=1, source_target_pairs={{1,0},{2,1},{3,2},{4,3},{5,4},{6,5},{7,6},{0,7},{9,8},{10,9},{11,1... | collective-permute-start | bytes 15368 | tf_op jit(solution)/shard_map/ppermute | solution.py:20
  46.0 15.9 %all-to-all-start.1 = ((f32[8,8,3840]{2,1,0:T(8,128)}), f32[8,8,3840]{2,1,0:T(8,128)S(1)}, u32[]{:S(2)}, u32[]{:S(2)}) async-start(f32[8,8,3840]{2,1,0:T(8,128)} %bitcast.11), calls=%async_computation.1 | async-start | bytes 1966080 | tf_op jit(solution)/shard_map/all_to_all | solution.py:234
  68.2 4.1 %collective-permute-start.4 = (f32[5,16,16]{2,1,0:T(8,128)S(1)}, f32[5,16,16]{2,1,0:T(8,128)S(1)}, u32[]{:S(2)}, u32[]{:S(2)}) collective-permute-start(f32[5,16,16]{2,1,0:T(8,128)S(1)} %bitcast.227), channel_id=1, source_target_pairs={{0,1},{1,2},{2,3},{3,4},{4,5},{5,6},{6,7},{7,0},{8,9},{9,10},{10,1... | collective-permute-start | bytes 15368 | tf_op jit(solution)/shard_map/ppermute | solution.py:20
  81.6 7.6 %collective-permute-start.10 = (f32[5,16,16]{2,1,0:T(8,128)S(1)}, f32[5,16,16]{2,1,0:T(8,128)S(1)}, u32[]{:S(2)}, u32[]{:S(2)}) collective-permute-start(f32[5,16,16]{2,1,0:T(8,128)S(1)} %get-tuple-element.2), channel_id=1, source_target_pairs={{0,1},{1,2},{2,3},{3,4},{4,5},{5,6},{6,7},{7,0},{8,9},{9,10},{10,1... | collective-permute-start | bytes 15368 | tf_op jit(solution)/shard_map/ppermute | solution.py:20
  82.7 7.0 %collective-permute-start.11 = (f32[5,16,16]{2,1,0:T(8,128)S(1)}, f32[5,16,16]{2,1,0:T(8,128)S(1)}, u32[]{:S(2)}, u32[]{:S(2)}) collective-permute-start(f32[5,16,16]{2,1,0:T(8,128)S(1)} %get-tuple-element.3), channel_id=1, source_target_pairs={{1,0},{2,1},{3,2},{4,3},{5,4},{6,5},{7,6},{0,7},{9,8},{10,9},{11,1... | collective-permute-start | bytes 15368 | tf_op jit(solution)/shard_map/ppermute | solution.py:20
  86.0 5.2 %collective-permute-start.6 = (f32[5,16,128]{2,1,0:T(8,128)S(1)}, f32[5,16,128]{2,1,0:T(8,128)S(1)}, u32[]{:S(2)}, u32[]{:S(2)}) collective-permute-start(f32[5,16,128]{2,1,0:T(8,128)S(1)} %get-tuple-element.16), channel_id=1, source_target_pairs={{0,64},{64,128},{128,192},{192,0},{1,65},{65,129},{129,193},{193,1... | collective-permute-start | bytes 122888 | tf_op jit(solution)/shard_map/ppermute | solution.py:20
  87.5 4.0 %collective-permute-start.7 = (f32[5,16,128]{2,1,0:T(8,128)S(1)}, f32[5,16,128]{2,1,0:T(8,128)S(1)}, u32[]{:S(2)}, u32[]{:S(2)}) collective-permute-start(f32[5,16,128]{2,1,0:T(8,128)S(1)} %get-tuple-element.17), channel_id=1, source_target_pairs={{64,0},{128,64},{192,128},{0,192},{65,1},{129,65},{193,129},{1,193... | collective-permute-start | bytes 122888 | tf_op jit(solution)/shard_map/ppermute | solution.py:20
  89.2 2.3 %collective-permute-start.9 = (f32[5,16,128]{2,1,0:T(8,128)S(1)}, f32[5,16,128]{2,1,0:T(8,128)S(1)}, u32[]{:S(2)}, u32[]{:S(2)}) collective-permute-start(f32[5,16,128]{2,1,0:T(8,128)S(1)} %bitcast.225), channel_id=1, source_target_pairs={{8,0},{16,8},{24,16},{32,24},{40,32},{48,40},{56,48},{0,56},{9,1},... | collective-permute-start | bytes 122888 | tf_op jit(solution)/shard_map/ppermute | solution.py:20
  89.2 5.7 %collective-permute-start.8 = (f32[5,16,128]{2,1,0:T(8,128)S(1)}, f32[5,16,128]{2,1,0:T(8,128)S(1)}, u32[]{:S(2)}, u32[]{:S(2)}) collective-permute-start(f32[5,16,128]{2,1,0:T(8,128)S(1)} %bitcast.224), channel_id=1, source_target_pairs={{0,8},{8,16},{16,24},{24,32},{32,40},{40,48},{48,56},{56,0},{1,9},... | collective-permute-start | bytes 122888 | tf_op jit(solution)/shard_map/ppermute | solution.py:20
  105.3 14.8 %all-to-all-start.2 = ((f32[8,8,2560]{2,1,0:T(8,128)}), f32[8,8,2560]{2,1,0:T(8,128)S(1)}, u32[]{:S(2)}, u32[]{:S(2)}) async-start(f32[8,8,2560]{2,1,0:T(8,128)} %bitcast.66), calls=%async_computation.2 | async-start | bytes 1310720 | tf_op jit(solution)/shard_map/all_to_all | solution.py:248
  121.8 4.6 %copy-start.1 = (s32[1,512]{1,0:T(1,128)S(1)}, s32[1,512]{1,0:T(1,128)}, u32[]{:S(2)}) copy-start(s32[1,512]{1,0:T(1,128)} %param.6) | copy-start | bytes 6148
  121.8 25.7 %all-to-all-start.3 = ((f32[8,8,2560]{2,1,0:T(8,128)}), f32[8,8,2560]{2,1,0:T(8,128)S(1)}, u32[]{:S(2)}, u32[]{:S(2)}) async-start(f32[8,8,2560]{2,1,0:T(8,128)} %bitcast.68), calls=%async_computation.3 | async-start | bytes 1310720 | tf_op jit(solution)/shard_map/all_to_all | solution.py:250

commit v6 on v3

--- a/solution.py
+++ b/solution.py
@@ -105,9 +105,9 @@
 
 def coarse_faces(fetched, nblk):
     half = BS // 2
-    lv = fetched.reshape(nblk, 2, 6, 5, half, half)
+    lv = fetched.reshape(nblk, -1, 6, 5, half, half)
     rows = replicate(half, BS)
-    side = lv[:, :, 0:4].transpose(1, 2, 3, 4, 0, 5).reshape(2, 4, 5, half, nblk * half)
+    side = lv[:, :, 0:4].transpose(1, 2, 3, 4, 0, 5).reshape(lv.shape[1], 4, 5, half, nblk * half)
     side = exact_dot("ay,lkfab,bz->lkfyz", rows, side, replicate(nblk * half, nblk * BS))
     ends = lv[:, :, 4:6].transpose(1, 2, 3, 4, 5, 0)
     lane = jnp.arange(nblk * BS)
@@ -227,10 +227,10 @@
     mine = lax.dynamic_slice_in_dim(item, me * nblk, nblk)
     fetched = pick(stage, o_col[mine] * nblk + rank2[mine])
 
-    side, ends = coarse_faces(fetched, nblk)
     state = fine
     for step in range(2):
-        state = substep(state, *ghost_inputs(state, side[step], ends[step], links))
+        side, ends = coarse_faces(fetched[:, step * width : (step + 1) * width], nblk)
+        state = substep(state, *ghost_inputs(state, side[0], ends[0], links))
     restricted = restrict_state(state, nblk)
 
     pos = jnp.arange(nblk, dtype=jnp.int32)

time: 149 us -> 150 us (level)
  starting transfers between devices: 41.7 us -> 45.6 us
  waiting for transfers between devices: 60.8 us -> 57.5 us
  matrix products: 4.52 us -> 7.15 us
  other arithmetic: 8.73 us -> 6.22 us
    ppermute x12, waiting for transfers between devices: 5.51 us -> 1.72 us  [shift_in(): return lax.ppermute(plane, axis, pairs)]
    ppermute x12, starting transfers between devices: 16.1 us -> 19.6 us  [shift_in(): return lax.ppermute(plane, axis, pairs)]
    dot_general x7 -> x12, matrix products: 4.52 us -> 7.15 us  [exact_dot(): jnp.einsum(spec, *ops, precision=lax.Precision.HIGHEST, preferred_element...]
    select_n x2 -> x0, other arithmetic: 2.5 us -> none  [ghost_inputs(): jnp.where(link_lo & (lane == 0), far_lo[..., None], jnp.where(link_hi & (...]
  transfers between devices with their start and end apart: 16 -> 16, of which waited for: 8 -> 6; matrix products, arithmetic and copies ran while one was open for 11% -> 10% of each run, Pallas kernels for 0% -> 0%
where the time goes in v6:
time: 150 us
  waiting for transfers between devices  57.5 us (38%)
  starting transfers between devices  45.6 us (30%)
  local copies, waits for them, and re-layouts  23.1 us (15%)
  Pallas kernels  9.01 us (6%)
  matrix products  7.15 us (5%)
  other arithmetic  6.22 us (4%)
    all_to_all x1, waiting for transfers between devices, shards(): stage = lax.all_to_all(pick(stage, home), 'gy', 0, 0, tiled=True)  20.9 us
    ppermute x12, starting transfers between devices, shift_in(): return lax.ppermute(plane, axis, pairs)  19.6 us
    all_to_all x1, waiting for transfers between devices, shards(): stage = lax.all_to_all(pick(levels[None], first), 'gy', 0, 0, tiled=True)  17.4 us
    all_to_all x1, waiting for transfers between devices, shards(): stage = lax.all_to_all(pick(stage, second), 'gz', 0, 0, tiled=True)  9.9 us
    pallas_call x2, Pallas kernels, substep(): pl.pallas_call(substep_kernel, out_shape=jax.ShapeDtypeStruct(state.shape...  9.01 us
    gather x6, local copies, waits for them, and re-layouts, pick(): jnp.take(flat, index.reshape(-1), axis=0, mode='clip')  8.77 us
    all_to_all x1, starting transfers between devices, shards(): stage = lax.all_to_all(pick(levels[None], first), 'gy', 0, 0, tiled=True)  8.6 us
    all_to_all x1, waiting for transfers between devices, shards(): stage = lax.all_to_all(pick(restricted[None], back), 'gz', 0, 0, tiled=True)  7.53 us
  transfers between devices with their start and end apart: 16, of which 6 were waited for; matrix products, arithmetic and copies ran while one was open for 10% of the time, Pallas kernels for 0%

profile of v6, /device:TPU:8, one launch (start us, length us, event | category | flops | bytes accessed | tf_op | source)
XLA Modules:
  0.0 149.6 jit_solution(10592296475191206810)
XLA Ops:
  0.7 0.7 and_select_fusion
  1.4 0.7 broadcast_compare_fusion
  2.9 0.7 add_select_fusion.3
  4.2 0.9 fusion.80
  5.1 1.9 %gather_fusion = f32[64,3840]{1,0:T(8,128)} fusion(f32[8,3840]{1,0:T(8,128)S(1)} %pad_maximum_fusion, s32[1024]{0:T(1024)S(1)} %pad_clamp_fusion.6), kind=kCustom, calls=%fused_computation | custom fusion | bytes 1966336 | tf_op jit(solution)/shard_map/jit(_take)/gather | solution.py:171
  6.9 8.6 %all-to-all-start = ((f32[8,8,3840]{2,1,0:T(8,128)}), f32[8,8,3840]{2,1,0:T(8,128)S(1)}, u32[]{:S(2)}, u32[]{:S(2)}) async-start(f32[8,8,3840]{2,1,0:T(8,128)} %bitcast.8), calls=%async_computation | async-start | bytes 1966080 | tf_op jit(solution)/shard_map/all_to_all | solution.py:224
  16.3 1.6 %collective-permute-start.4 = (f32[5,16,16]{2,1,0:T(8,128)S(1)}, f32[5,16,16]{2,1,0:T(8,128)S(1)}, u32[]{:S(2)}, u32[]{:S(2)}) collective-permute-start(f32[5,16,16]{2,1,0:T(8,128)S(1)} %bitcast.252), channel_id=1, source_target_pairs={{0,1},{1,2},{2,3},{3,4},{4,5},{5,6},{6,7},{7,0},{8,9},{9,10},{10,1... | collective-permute-start | bytes 15368 | tf_op jit(solution)/shard_map/ppermute | solution.py:20
  17.9 1.5 collective-permute-start
  19.4 1.7 %collective-permute-start.1 = (f32[5,16,128]{2,1,0:T(8,128)S(1)}, f32[5,16,128]{2,1,0:T(8,128)S(1)}, u32[]{:S(2)}, u32[]{:S(2)}) collective-permute-start(f32[5,16,128]{2,1,0:T(8,128)S(1)} %get-tuple-element.23), channel_id=1, source_target_pairs={{64,0},{128,64},{192,128},{0,192},{65,1},{129,65},{193,129},{1,193... | collective-permute-start | bytes 122888 | tf_op jit(solution)/shard_map/ppermute | solution.py:20
  21.3 3.8 %collective-permute-start.3 = (f32[5,16,128]{2,1,0:T(8,128)S(1)}, f32[5,16,128]{2,1,0:T(8,128)S(1)}, u32[]{:S(2)}, u32[]{:S(2)}) collective-permute-start(f32[5,16,128]{2,1,0:T(8,128)S(1)} %bitcast.248), channel_id=1, source_target_pairs={{8,0},{16,8},{24,16},{32,24},{40,32},{48,40},{56,48},{0,56},{9,1},... | collective-permute-start | bytes 122888 | tf_op jit(solution)/shard_map/ppermute | solution.py:20
  25.3 0.6 gather_fusion.3
  25.9 0.7 gather_fusion.2
  26.7 17.4 %all-to-all-done = f32[8,8,3840]{2,1,0:T(8,128)S(1)} async-done(((f32[8,8,3840]{2,1,0:T(8,128)}), f32[8,8,3840]{2,1,0:T(8,128)S(1)}, u32[]{:S(2)}, u32[]{:S(2)}) %all-to-all-start) | async-done | bytes 983072 | tf_op jit(solution)/shard_map/all_to_all | solution.py:224
  44.1 1.9 %gather_fusion.1 = f32[64,3840]{1,0:T(8,128)} fusion(f32[64,3840]{1,0:T(8,128)S(1)} %bitcast.240, s32[1024]{0:T(1024)S(1)} %pad_clamp_fusion.5), kind=kCustom, calls=%fused_computation.1 | custom fusion | bytes 1966336 | tf_op jit(solution)/shard_map/jit(_take)/gather | solution.py:171
  46.0 5.1 %all-to-all-start.1 = ((f32[8,8,3840]{2,1,0:T(8,128)}), f32[8,8,3840]{2,1,0:T(8,128)S(1)}, u32[]{:S(2)}, u32[]{:S(2)}) async-start(f32[8,8,3840]{2,1,0:T(8,128)} %bitcast.11), calls=%async_computation.1 | async-start | bytes 1966080 | tf_op jit(solution)/shard_map/all_to_all | solution.py:226
  51.7 0.5 copy.117
  53.4 9.9 %all-to-all-done.1 = f32[8,8,3840]{2,1,0:T(8,128)S(1)} async-done(((f32[8,8,3840]{2,1,0:T(8,128)}), f32[8,8,3840]{2,1,0:T(8,128)S(1)}, u32[]{:S(2)}, u32[]{:S(2)}) %all-to-all-start.1) | async-done | bytes 983072 | tf_op jit(solution)/shard_map/all_to_all | solution.py:226
  63.3 0.6 gather_fusion.4
  65.4 0.7 convolution_bitcast_fusion.3
  66.9 1.4 collective-permute-start.5
  68.4 0.6 pad_maximum_fusion.1.gx_ref
  69.0 0.7 copy.89.gy_ref
  69.8 1.4 collective-permute-done.5
  71.1 1.3 select_select_fusion.1.zfix_ref
  72.5 0.6 broadcast_in_dim.285.zflag_ref
  73.1 4.5 %shard_map.59.u_ref = f32[5,16,16,128]{3,2,1,0:T(8,128)} custom-call(f32[5,16,16,128]{3,2,1,0:T(8,128)} %u_ref.1, f32[2,5,16,128]{3,2,1,0:T(8,128)} %pad_maximum_fusion.1.gx_ref, f32[2,16,5,1,128]{4,3,2,1,0:T(1,128)} %copy.89.gy_ref, f32[5,16,16,128]{3,2,1,0:T(8,128)} %select_select_fusion.1.zfix_ref, s32[2,16,128]{2,1,0:T(8,128)} %broadcast_in_dim.285.zflag_ref), custom_call_target="tpu_custom_call" | custom-call | tf_op jit(solution)/shard_map/pallas_call | solution.py:92
  77.6 1.9 %slice_reduce_fusion.1 = (f32[5,16,16]{2,1,0:T(8,128)S(1)}, f32[5,16,16]{2,1,0:T(8,128)S(1)}) fusion(f32[5,16,16,128]{3,2,1,0:T(8,128)} %shard_map.59.u_ref), kind=kLoop, calls=%fused_computation.23 | loop fusion | bytes 20480 | tf_op jit(solution)/shard_map/slice | solution.py:137
  79.5 0.8 slice_bitcast_fusion.12
  80.3 1.1 fusion.76
  82.1 1.0 collective-permute-start.10
  83.0 1.1 collective-permute-start.11
  84.4 0.7 convolution_bitcast_fusion.2
  85.4 1.6 %collective-permute-start.6 = (f32[5,16,128]{2,1,0:T(8,128)S(1)}, f32[5,16,128]{2,1,0:T(8,128)S(1)}, u32[]{:S(2)}, u32[]{:S(2)}) collective-permute-start(f32[5,16,128]{2,1,0:T(8,128)S(1)} %get-tuple-element.16), channel_id=1, source_target_pairs={{0,64},{64,128},{128,192},{192,0},{1,65},{65,129},{129,193},{193,1... | collective-permute-start | bytes 122888 | tf_op jit(solution)/shard_map/ppermute | solution.py:20
  87.0 1.7 %collective-permute-start.7 = (f32[5,16,128]{2,1,0:T(8,128)S(1)}, f32[5,16,128]{2,1,0:T(8,128)S(1)}, u32[]{:S(2)}, u32[]{:S(2)}) collective-permute-start(f32[5,16,128]{2,1,0:T(8,128)S(1)} %get-tuple-element.17), channel_id=1, source_target_pairs={{64,0},{128,64},{192,128},{0,192},{65,1},{129,65},{193,129},{1,193... | collective-permute-start | bytes 122888 | tf_op jit(solution)/shard_map/ppermute | solution.py:20
  89.8 3.9 %collective-permute-start.9 = (f32[5,16,128]{2,1,0:T(8,128)S(1)}, f32[5,16,128]{2,1,0:T(8,128)S(1)}, u32[]{:S(2)}, u32[]{:S(2)}) collective-permute-start(f32[5,16,128]{2,1,0:T(8,128)S(1)} %bitcast.250), channel_id=1, source_target_pairs={{8,0},{16,8},{24,16},{32,24},{40,32},{48,40},{56,48},{0,56},{9,1},... | collective-permute-start | bytes 122888 | tf_op jit(solution)/shard_map/ppermute | solution.py:20
  93.7 1.3 select_select_fusion.zfix_ref
  95.4 0.7 copy.98.gy_ref
  96.1 0.6 pad_maximum_fusion.2.gx_ref
  96.8 4.5 %shard_map.60 = f32[5,16,16,128]{3,2,1,0:T(8,128)} custom-call(f32[5,16,16,128]{3,2,1,0:T(8,128)} %shard_map.59.u_ref, f32[2,5,16,128]{3,2,1,0:T(8,128)} %pad_maximum_fusion.2.gx_ref, f32[2,16,5,1,128]{4,3,2,1,0:T(1,128)} %copy.98.gy_ref, f32[5,16,16,128]{3,2,1,0:T(8,128)} %select_select_fusion.zfix_ref, s32[2,16,128]{2,1,0:T(8,128)} %broadcast_in_dim.285.zflag_ref), custom_call_target="tpu_custom_call" | custom-call | tf_op jit(solution)/shard_map/pallas_call | solution.py:92
  101.3 1.3 fusion.6
  103.5 0.7 reshape_broadcast_in_dim_reshape.3
  104.2 1.6 %gather_fusion.5 = f32[64,2560]{1,0:T(8,128)} fusion(f32[8,2560]{1,0:T(8,128)S(1)} %reshape_broadcast_in_dim_reshape.3, s32[1024]{0:T(1024)S(1)} %pad_clamp_fusion.2), kind=kCustom, calls=%fused_computation.5 | custom fusion | bytes 1310976 | tf_op jit(solution)/shard_map/jit(_take)/gather | solution.py:171
  105.8 7.1 %all-to-all-start.2 = ((f32[8,8,2560]{2,1,0:T(8,128)}), f32[8,8,2560]{2,1,0:T(8,128)S(1)}, u32[]{:S(2)}, u32[]{:S(2)}) async-start(f32[8,8,2560]{2,1,0:T(8,128)} %bitcast.77), calls=%async_computation.2 | async-start | bytes 1310720 | tf_op jit(solution)/shard_map/all_to_all | solution.py:240
  113.0 7.5 %all-to-all-done.2 = f32[8,8,2560]{2,1,0:T(8,128)S(1)} async-done(((f32[8,8,2560]{2,1,0:T(8,128)}), f32[8,8,2560]{2,1,0:T(8,128)S(1)}, u32[]{:S(2)}, u32[]{:S(2)}) %all-to-all-start.2) | async-done | bytes 655392 | tf_op jit(solution)/shard_map/all_to_all | solution.py:240
  120.5 1.6 %gather_fusion.6 = f32[64,2560]{1,0:T(8,128)} fusion(f32[64,2560]{1,0:T(8,128)S(1)} %bitcast.241, s32[1024]{0:T(1024)S(1)} %pad_clamp_fusion.1), kind=kCustom, calls=%fused_computation.6 | custom fusion | bytes 1310976 | tf_op jit(solution)/shard_map/jit(_take)/gather | solution.py:171
  122.2 5.1 %all-to-all-start.3 = ((f32[8,8,2560]{2,1,0:T(8,128)}), f32[8,8,2560]{2,1,0:T(8,128)S(1)}, u32[]{:S(2)}, u32[]{:S(2)}) async-start(f32[8,8,2560]{2,1,0:T(8,128)} %bitcast.79), calls=%async_computation.3 | async-start | bytes 1310720 | tf_op jit(solution)/shard_map/all_to_all | solution.py:242
  127.5 20.9 %all-to-all-done.3 = f32[8,8,2560]{2,1,0:T(8,128)S(1)} async-done(((f32[8,8,2560]{2,1,0:T(8,128)}), f32[8,8,2560]{2,1,0:T(8,128)S(1)}, u32[]{:S(2)}, u32[]{:S(2)}) %all-to-all-start.3) | async-done | bytes 655392 | tf_op jit(solution)/shard_map/all_to_all | solution.py:242
  148.4 1.2 gather_fusion.7
  (108 shorter events, 10.1 us)
Async XLA Ops:
  6.9 8.6 %copy-start = (f32[5,16,16,128]{3,2,1,0:T(8,128)S(1)}, f32[5,16,16,128]{3,2,1,0:T(8,128)}, u32[]{:S(2)}) copy-start(f32[5,16,16,128]{3,2,1,0:T(8,128)} %u_ref.1) | copy-start | bytes 1966084
  6.9 37.2 %all-to-all-start = ((f32[8,8,3840]{2,1,0:T(8,128)}), f32[8,8,3840]{2,1,0:T(8,128)S(1)}, u32[]{:S(2)}, u32[]{:S(2)}) async-start(f32[8,8,3840]{2,1,0:T(8,128)} %bitcast.8), calls=%async_computation | async-start | bytes 1966080 | tf_op jit(solution)/shard_map/all_to_all | solution.py:224
  15.8 10.9 %copy-start.2 = (s32[6,1,1,8]{3,2,1,0:T(1,128)S(1)}, s32[6,1,1,8]{3,2,1,0:T(1,128)}, u32[]{:S(2)}) copy-start(s32[6,1,1,8]{3,2,1,0:T(1,128)} %param.7) | copy-start | bytes 580
  16.3 53.5 %collective-permute-start.4 = (f32[5,16,16]{2,1,0:T(8,128)S(1)}, f32[5,16,16]{2,1,0:T(8,128)S(1)}, u32[]{:S(2)}, u32[]{:S(2)}) collective-permute-start(f32[5,16,16]{2,1,0:T(8,128)S(1)} %bitcast.252), channel_id=1, source_target_pairs={{0,1},{1,2},{2,3},{3,4},{4,5},{5,6},{6,7},{7,0},{8,9},{9,10},{10,1... | collective-permute-start | bytes 15368 | tf_op jit(solution)/shard_map/ppermute | solution.py:20
  17.9 48.9 %collective-permute-start = (f32[5,16,128]{2,1,0:T(8,128)S(1)}, f32[5,16,128]{2,1,0:T(8,128)S(1)}, u32[]{:S(2)}, u32[]{:S(2)}) collective-permute-start(f32[5,16,128]{2,1,0:T(8,128)S(1)} %get-tuple-element.22), channel_id=1, source_target_pairs={{0,64},{64,128},{128,192},{192,0},{1,65},{65,129},{129,193},{193,1... | collective-permute-start | bytes 122888 | tf_op jit(solution)/shard_map/ppermute | solution.py:20
  19.4 48.9 %collective-permute-start.1 = (f32[5,16,128]{2,1,0:T(8,128)S(1)}, f32[5,16,128]{2,1,0:T(8,128)S(1)}, u32[]{:S(2)}, u32[]{:S(2)}) collective-permute-start(f32[5,16,128]{2,1,0:T(8,128)S(1)} %get-tuple-element.23), channel_id=1, source_target_pairs={{64,0},{128,64},{192,128},{0,192},{65,1},{129,65},{193,129},{1,193... | collective-permute-start | bytes 122888 | tf_op jit(solution)/shard_map/ppermute | solution.py:20
  21.2 47.1 %collective-permute-start.2 = (f32[5,16,128]{2,1,0:T(8,128)S(1)}, f32[5,16,128]{2,1,0:T(8,128)S(1)}, u32[]{:S(2)}, u32[]{:S(2)}) collective-permute-start(f32[5,16,128]{2,1,0:T(8,128)S(1)} %bitcast.249), channel_id=1, source_target_pairs={{0,8},{8,16},{16,24},{24,32},{32,40},{40,48},{48,56},{56,0},{1,9},... | collective-permute-start | bytes 122888 | tf_op jit(solution)/shard_map/ppermute | solution.py:20
  21.3 47.0 %collective-permute-start.3 = (f32[5,16,128]{2,1,0:T(8,128)S(1)}, f32[5,16,128]{2,1,0:T(8,128)S(1)}, u32[]{:S(2)}, u32[]{:S(2)}) collective-permute-start(f32[5,16,128]{2,1,0:T(8,128)S(1)} %bitcast.248), channel_id=1, source_target_pairs={{8,0},{16,8},{24,16},{32,24},{40,32},{48,40},{56,48},{0,56},{9,1},... | collective-permute-start | bytes 122888 | tf_op jit(solution)/shard_map/ppermute | solution.py:20
  46.0 17.3 %all-to-all-start.1 = ((f32[8,8,3840]{2,1,0:T(8,128)}), f32[8,8,3840]{2,1,0:T(8,128)S(1)}, u32[]{:S(2)}, u32[]{:S(2)}) async-start(f32[8,8,3840]{2,1,0:T(8,128)} %bitcast.11), calls=%async_computation.1 | async-start | bytes 1966080 | tf_op jit(solution)/shard_map/all_to_all | solution.py:226
  66.9 4.3 %collective-permute-start.5 = (f32[5,16,16]{2,1,0:T(8,128)S(1)}, f32[5,16,16]{2,1,0:T(8,128)S(1)}, u32[]{:S(2)}, u32[]{:S(2)}) collective-permute-start(f32[5,16,16]{2,1,0:T(8,128)S(1)} %bitcast.253), channel_id=1, source_target_pairs={{1,0},{2,1},{3,2},{4,3},{5,4},{6,5},{7,6},{0,7},{9,8},{10,9},{11,1... | collective-permute-start | bytes 15368 | tf_op jit(solution)/shard_map/ppermute | solution.py:20
  82.1 7.7 %collective-permute-start.10 = (f32[5,16,16]{2,1,0:T(8,128)S(1)}, f32[5,16,16]{2,1,0:T(8,128)S(1)}, u32[]{:S(2)}, u32[]{:S(2)}) collective-permute-start(f32[5,16,16]{2,1,0:T(8,128)S(1)} %get-tuple-element.2), channel_id=1, source_target_pairs={{0,1},{1,2},{2,3},{3,4},{4,5},{5,6},{6,7},{7,0},{8,9},{9,10},{10,1... | collective-permute-start | bytes 15368 | tf_op jit(solution)/shard_map/ppermute | solution.py:20
  83.0 10.7 %collective-permute-start.11 = (f32[5,16,16]{2,1,0:T(8,128)S(1)}, f32[5,16,16]{2,1,0:T(8,128)S(1)}, u32[]{:S(2)}, u32[]{:S(2)}) collective-permute-start(f32[5,16,16]{2,1,0:T(8,128)S(1)} %get-tuple-element.3), channel_id=1, source_target_pairs={{1,0},{2,1},{3,2},{4,3},{5,4},{6,5},{7,6},{0,7},{9,8},{10,9},{11,1... | collective-permute-start | bytes 15368 | tf_op jit(solution)/shard_map/ppermute | solution.py:20
  85.4 9.7 %collective-permute-start.6 = (f32[5,16,128]{2,1,0:T(8,128)S(1)}, f32[5,16,128]{2,1,0:T(8,128)S(1)}, u32[]{:S(2)}, u32[]{:S(2)}) collective-permute-start(f32[5,16,128]{2,1,0:T(8,128)S(1)} %get-tuple-element.16), channel_id=1, source_target_pairs={{0,64},{64,128},{128,192},{192,0},{1,65},{65,129},{129,193},{193,1... | collective-permute-start | bytes 122888 | tf_op jit(solution)/shard_map/ppermute | solution.py:20
  87.0 8.1 %collective-permute-start.7 = (f32[5,16,128]{2,1,0:T(8,128)S(1)}, f32[5,16,128]{2,1,0:T(8,128)S(1)}, u32[]{:S(2)}, u32[]{:S(2)}) collective-permute-start(f32[5,16,128]{2,1,0:T(8,128)S(1)} %get-tuple-element.17), channel_id=1, source_target_pairs={{64,0},{128,64},{192,128},{0,192},{65,1},{129,65},{193,129},{1,193... | collective-permute-start | bytes 122888 | tf_op jit(solution)/shard_map/ppermute | solution.py:20
  88.7 6.4 %collective-permute-start.8 = (f32[5,16,128]{2,1,0:T(8,128)S(1)}, f32[5,16,128]{2,1,0:T(8,128)S(1)}, u32[]{:S(2)}, u32[]{:S(2)}) collective-permute-start(f32[5,16,128]{2,1,0:T(8,128)S(1)} %bitcast.251), channel_id=1, source_target_pairs={{0,8},{8,16},{16,24},{24,32},{32,40},{40,48},{48,56},{56,0},{1,9},... | collective-permute-start | bytes 122888 | tf_op jit(solution)/shard_map/ppermute | solution.py:20
  89.8 5.6 %collective-permute-start.9 = (f32[5,16,128]{2,1,0:T(8,128)S(1)}, f32[5,16,128]{2,1,0:T(8,128)S(1)}, u32[]{:S(2)}, u32[]{:S(2)}) collective-permute-start(f32[5,16,128]{2,1,0:T(8,128)S(1)} %bitcast.250), channel_id=1, source_target_pairs={{8,0},{16,8},{24,16},{32,24},{40,32},{48,40},{56,48},{0,56},{9,1},... | collective-permute-start | bytes 122888 | tf_op jit(solution)/shard_map/ppermute | solution.py:20
  105.8 14.8 %all-to-all-start.2 = ((f32[8,8,2560]{2,1,0:T(8,128)}), f32[8,8,2560]{2,1,0:T(8,128)S(1)}, u32[]{:S(2)}, u32[]{:S(2)}) async-start(f32[8,8,2560]{2,1,0:T(8,128)} %bitcast.77), calls=%async_computation.2 | async-start | bytes 1310720 | tf_op jit(solution)/shard_map/all_to_all | solution.py:240
  122.2 5.1 %copy-start.1 = (s32[1,512]{1,0:T(1,128)S(1)}, s32[1,512]{1,0:T(1,128)}, u32[]{:S(2)}) copy-start(s32[1,512]{1,0:T(1,128)} %param.6) | copy-start | bytes 6148
  122.2 26.3 %all-to-all-start.3 = ((f32[8,8,2560]{2,1,0:T(8,128)}), f32[8,8,2560]{2,1,0:T(8,128)S(1)}, u32[]{:S(2)}, u32[]{:S(2)}) async-start(f32[8,8,2560]{2,1,0:T(8,128)} %bitcast.79), calls=%async_computation.3 | async-start | bytes 1310720 | tf_op jit(solution)/shard_map/all_to_all | solution.py:242

commit v7 on v3

--- a/solution.py
+++ b/solution.py
@@ -205,12 +205,14 @@
         ),
         axis=1,
     )
+    cols_of = o_col.reshape(-1, nblk)
+    pos = jnp.arange(nblk, dtype=jnp.int32)
     rank2 = jnp.sum(
-        (before & (dev[None, :] == dev[:, None]) & (o_col[None, :] == o_col[:, None])).astype(
-            jnp.int32
-        ),
-        axis=1,
-    )
+        (
+            (pos[None, :] < pos[:, None])[None] & (cols_of[:, :, None] == cols_of[:, None, :])
+        ).astype(jnp.int32),
+        axis=2,
+    ).reshape(-1)
     peer_r = jnp.arange(rows, dtype=jnp.int32)[:, None, None]
     peer_c = jnp.arange(cols, dtype=jnp.int32)[:, None, None]
     cell = jnp.arange(nblk, dtype=jnp.int32)[None, :, None]

time: 149 us -> 151 us (1.013)
  no operation moved by 1% of the time
where the time goes in v7:
time: 151 us; the launch traced here: 150 us
  waiting for transfers between devices  60.8 us (40%)
  starting transfers between devices  41.6 us (28%)
  local copies, waits for them, and re-layouts  23.8 us (16%)
  other arithmetic  9.16 us (6%)
  Pallas kernels  9.02 us (6%)
  matrix products  4.53 us (3%)
    all_to_all x1, waiting for transfers between devices, shards(): stage = lax.all_to_all(pick(stage, home), 'gy', 0, 0, tiled=True)  20.9 us
    all_to_all x1, waiting for transfers between devices, shards(): stage = lax.all_to_all(pick(levels[None], first), 'gy', 0, 0, tiled=True)  18.5 us
    ppermute x12, starting transfers between devices, shift_in(): return lax.ppermute(plane, axis, pairs)  16.1 us
    pallas_call x2, Pallas kernels, substep(): pl.pallas_call(substep_kernel, out_shape=jax.ShapeDtypeStruct(state.shape...  9.02 us
    gather x6, local copies, waits for them, and re-layouts, pick(): jnp.take(flat, index.reshape(-1), axis=0, mode='clip')  8.76 us
    all_to_all x1, waiting for transfers between devices, shards(): stage = lax.all_to_all(pick(stage, second), 'gz', 0, 0, tiled=True)  8.62 us
    all_to_all x1, starting transfers between devices, shards(): stage = lax.all_to_all(pick(levels[None], first), 'gy', 0, 0, tiled=True)  8.6 us
    all_to_all x1, starting transfers between devices, shards(): stage = lax.all_to_all(pick(restricted[None], back), 'gz', 0, 0, tiled=True)  7.49 us
  transfers between devices with their start and end apart: 16, of which 8 were waited for; matrix products, arithmetic and copies ran while one was open for 11% of the time, Pallas kernels for 0%

profile of v7, /device:TPU:8, one launch (start us, length us, event | category | flops | bytes accessed | tf_op | source)
XLA Modules:
  0.0 150.0 jit_solution(13089638194542070433)
XLA Ops:
  0.7 0.7 add_select_fusion.5
  1.4 0.7 broadcast_compare_fusion
  2.6 1.4 and_select_fusion
  5.4 0.9 fusion.70
  6.3 1.8 %gather_fusion = f32[64,3840]{1,0:T(8,128)} fusion(f32[8,3840]{1,0:T(8,128)S(1)} %pad_maximum_fusion, s32[1024]{0:T(1024)S(1)} %pad_clamp_fusion.6), kind=kCustom, calls=%fused_computation | custom fusion | bytes 1966336 | tf_op jit(solution)/shard_map/jit(_take)/gather | solution.py:171
  8.2 8.6 %all-to-all-start = ((f32[8,8,3840]{2,1,0:T(8,128)}), f32[8,8,3840]{2,1,0:T(8,128)S(1)}, u32[]{:S(2)}, u32[]{:S(2)}) async-start(f32[8,8,3840]{2,1,0:T(8,128)} %bitcast.8), calls=%async_computation | async-start | bytes 1966080 | tf_op jit(solution)/shard_map/all_to_all | solution.py:226
  16.8 3.9 %collective-permute-start.3 = (f32[5,16,128]{2,1,0:T(8,128)S(1)}, f32[5,16,128]{2,1,0:T(8,128)S(1)}, u32[]{:S(2)}, u32[]{:S(2)}) collective-permute-start(f32[5,16,128]{2,1,0:T(8,128)S(1)} %bitcast.222), channel_id=1, source_target_pairs={{8,0},{16,8},{24,16},{32,24},{40,32},{48,40},{56,48},{0,56},{9,1},... | collective-permute-start | bytes 122888 | tf_op jit(solution)/shard_map/ppermute | solution.py:20
  20.8 1.6 %collective-permute-start = (f32[5,16,128]{2,1,0:T(8,128)S(1)}, f32[5,16,128]{2,1,0:T(8,128)S(1)}, u32[]{:S(2)}, u32[]{:S(2)}) collective-permute-start(f32[5,16,128]{2,1,0:T(8,128)S(1)} %get-tuple-element.20), channel_id=1, source_target_pairs={{0,64},{64,128},{128,192},{192,0},{1,65},{65,129},{129,193},{193,1... | collective-permute-start | bytes 122888 | tf_op jit(solution)/shard_map/ppermute | solution.py:20
  22.4 1.7 %collective-permute-start.1 = (f32[5,16,128]{2,1,0:T(8,128)S(1)}, f32[5,16,128]{2,1,0:T(8,128)S(1)}, u32[]{:S(2)}, u32[]{:S(2)}) collective-permute-start(f32[5,16,128]{2,1,0:T(8,128)S(1)} %get-tuple-element.21), channel_id=1, source_target_pairs={{64,0},{128,64},{192,128},{0,192},{65,1},{129,65},{193,129},{1,193... | collective-permute-start | bytes 122888 | tf_op jit(solution)/shard_map/ppermute | solution.py:20
  25.5 0.6 gather_fusion.3
  26.1 0.7 gather_fusion.2
  26.9 18.5 %all-to-all-done = f32[8,8,3840]{2,1,0:T(8,128)S(1)} async-done(((f32[8,8,3840]{2,1,0:T(8,128)}), f32[8,8,3840]{2,1,0:T(8,128)S(1)}, u32[]{:S(2)}, u32[]{:S(2)}) %all-to-all-start) | async-done | bytes 983072 | tf_op jit(solution)/shard_map/all_to_all | solution.py:226
  45.4 1.8 %gather_fusion.1 = f32[64,3840]{1,0:T(8,128)} fusion(f32[64,3840]{1,0:T(8,128)S(1)} %bitcast.213, s32[1024]{0:T(1024)S(1)} %pad_clamp_fusion.5), kind=kCustom, calls=%fused_computation.1 | custom fusion | bytes 1966336 | tf_op jit(solution)/shard_map/jit(_take)/gather | solution.py:171
  47.2 4.9 %all-to-all-start.1 = ((f32[8,8,3840]{2,1,0:T(8,128)}), f32[8,8,3840]{2,1,0:T(8,128)S(1)}, u32[]{:S(2)}, u32[]{:S(2)}) async-start(f32[8,8,3840]{2,1,0:T(8,128)} %bitcast.10), calls=%async_computation.1 | async-start | bytes 1966080 | tf_op jit(solution)/shard_map/all_to_all | solution.py:228
  54.5 8.6 %all-to-all-done.1 = f32[8,8,3840]{2,1,0:T(8,128)S(1)} async-done(((f32[8,8,3840]{2,1,0:T(8,128)}), f32[8,8,3840]{2,1,0:T(8,128)S(1)}, u32[]{:S(2)}, u32[]{:S(2)}) %all-to-all-start.1) | async-done | bytes 983072 | tf_op jit(solution)/shard_map/all_to_all | solution.py:228
  63.1 0.6 gather_fusion.4
  63.7 1.1 reshape.934
  64.9 0.8 copy.80
  66.4 1.2 convolution_bitcast_fusion.1
  68.1 0.8 convolution_bitcast_fusion
  69.5 1.1 collective-permute-start.4
  70.6 0.6 pad_maximum_fusion.1.gx_ref
  71.2 0.7 copy.89.gy_ref
  72.0 1.6 %collective-permute-done.4 = f32[5,16,16]{2,1,0:T(8,128)S(1)} collective-permute-done((f32[5,16,16]{2,1,0:T(8,128)S(1)}, f32[5,16,16]{2,1,0:T(8,128)S(1)}, u32[]{:S(2)}, u32[]{:S(2)}) %collective-permute-start.4) | collective-permute-done | bytes 5152 | tf_op jit(solution)/shard_map/ppermute | solution.py:20
  73.5 1.2 fusion.5.zfix_ref
  74.8 0.6 broadcast_in_dim.268.zflag_ref
  75.4 4.5 %shard_map.59.u_ref = f32[5,16,16,128]{3,2,1,0:T(8,128)} custom-call(f32[5,16,16,128]{3,2,1,0:T(8,128)} %u_ref.1, f32[2,5,16,128]{3,2,1,0:T(8,128)} %pad_maximum_fusion.1.gx_ref, f32[2,16,5,1,128]{4,3,2,1,0:T(1,128)} %copy.89.gy_ref, f32[5,16,16,128]{3,2,1,0:T(8,128)} %fusion.5.zfix_ref, s32[2,16,128]{2,1,0:T(8,128)} %broadcast_in_dim.268.zflag_ref), custom_call_target="tpu_custom_call" | custom-call | tf_op jit(solution)/shard_map/pallas_call | solution.py:92
  79.9 1.9 %slice_reduce_fusion.1 = (f32[5,16,16]{2,1,0:T(8,128)S(1)}, f32[5,16,16]{2,1,0:T(8,128)S(1)}) fusion(f32[5,16,16,128]{3,2,1,0:T(8,128)} %shard_map.59.u_ref), kind=kLoop, calls=%fused_computation.21 | loop fusion | bytes 20480 | tf_op jit(solution)/shard_map/slice | solution.py:137
  81.8 1.1 fusion.67
  82.9 1.1 collective-permute-start.10
  84.0 2.4 %collective-permute-start.11 = (f32[5,16,16]{2,1,0:T(8,128)S(1)}, f32[5,16,16]{2,1,0:T(8,128)S(1)}, u32[]{:S(2)}, u32[]{:S(2)}) collective-permute-start(f32[5,16,16]{2,1,0:T(8,128)S(1)} %get-tuple-element.3), channel_id=1, source_target_pairs={{1,0},{2,1},{3,2},{4,3},{5,4},{6,5},{7,6},{0,7},{9,8},{10,9},{11,1... | collective-permute-start | bytes 15368 | tf_op jit(solution)/shard_map/ppermute | solution.py:20
  86.5 0.8 slice_bitcast_fusion.12
  87.3 1.5 collective-permute-start.6
  88.8 1.7 %collective-permute-start.7 = (f32[5,16,128]{2,1,0:T(8,128)S(1)}, f32[5,16,128]{2,1,0:T(8,128)S(1)}, u32[]{:S(2)}, u32[]{:S(2)}) collective-permute-start(f32[5,16,128]{2,1,0:T(8,128)S(1)} %get-tuple-element.15), channel_id=1, source_target_pairs={{64,0},{128,64},{192,128},{0,192},{65,1},{129,65},{193,129},{1,193... | collective-permute-start | bytes 122888 | tf_op jit(solution)/shard_map/ppermute | solution.py:20
  91.0 1.3 fusion.3.zfix_ref
  92.8 3.5 %collective-permute-done.8 = f32[5,16,128]{2,1,0:T(8,128)S(1)} collective-permute-done((f32[5,16,128]{2,1,0:T(8,128)S(1)}, f32[5,16,128]{2,1,0:T(8,128)S(1)}, u32[]{:S(2)}, u32[]{:S(2)}) %collective-permute-start.8) | collective-permute-done | bytes 40992 | tf_op jit(solution)/shard_map/ppermute | solution.py:20
  96.3 0.7 copy.94.gy_ref
  97.0 0.6 pad_maximum_fusion.2.gx_ref
  97.6 4.5 %shard_map.60 = f32[5,16,16,128]{3,2,1,0:T(8,128)} custom-call(f32[5,16,16,128]{3,2,1,0:T(8,128)} %shard_map.59.u_ref, f32[2,5,16,128]{3,2,1,0:T(8,128)} %pad_maximum_fusion.2.gx_ref, f32[2,16,5,1,128]{4,3,2,1,0:T(1,128)} %copy.94.gy_ref, f32[5,16,16,128]{3,2,1,0:T(8,128)} %fusion.3.zfix_ref, s32[2,16,128]{2,1,0:T(8,128)} %broadcast_in_dim.268.zflag_ref), custom_call_target="tpu_custom_call" | custom-call | tf_op jit(solution)/shard_map/pallas_call | solution.py:92
  102.1 1.3 fusion.9
  104.3 0.7 reshape_broadcast_in_dim_reshape.3
  105.0 1.6 %gather_fusion.5 = f32[64,2560]{1,0:T(8,128)} fusion(f32[8,2560]{1,0:T(8,128)S(1)} %reshape_broadcast_in_dim_reshape.3, s32[1024]{0:T(1024)S(1)} %pad_clamp_fusion.2), kind=kCustom, calls=%fused_computation.5 | custom fusion | bytes 1310976 | tf_op jit(solution)/shard_map/jit(_take)/gather | solution.py:171
  106.6 7.5 %all-to-all-start.2 = ((f32[8,8,2560]{2,1,0:T(8,128)}), f32[8,8,2560]{2,1,0:T(8,128)S(1)}, u32[]{:S(2)}, u32[]{:S(2)}) async-start(f32[8,8,2560]{2,1,0:T(8,128)} %bitcast.65), calls=%async_computation.2 | async-start | bytes 1310720 | tf_op jit(solution)/shard_map/all_to_all | solution.py:242
  114.2 7.2 %all-to-all-done.2 = f32[8,8,2560]{2,1,0:T(8,128)S(1)} async-done(((f32[8,8,2560]{2,1,0:T(8,128)}), f32[8,8,2560]{2,1,0:T(8,128)S(1)}, u32[]{:S(2)}, u32[]{:S(2)}) %all-to-all-start.2) | async-done | bytes 655392 | tf_op jit(solution)/shard_map/all_to_all | solution.py:242
  121.5 1.6 %gather_fusion.6 = f32[64,2560]{1,0:T(8,128)} fusion(f32[64,2560]{1,0:T(8,128)S(1)} %bitcast.214, s32[1024]{0:T(1024)S(1)} %pad_clamp_fusion.1), kind=kCustom, calls=%fused_computation.6 | custom fusion | bytes 1310976 | tf_op jit(solution)/shard_map/jit(_take)/gather | solution.py:171
  123.1 4.6 %all-to-all-start.3 = ((f32[8,8,2560]{2,1,0:T(8,128)}), f32[8,8,2560]{2,1,0:T(8,128)S(1)}, u32[]{:S(2)}, u32[]{:S(2)}) async-start(f32[8,8,2560]{2,1,0:T(8,128)} %bitcast.67), calls=%async_computation.3 | async-start | bytes 1310720 | tf_op jit(solution)/shard_map/all_to_all | solution.py:244
  127.9 20.9 %all-to-all-done.3 = f32[8,8,2560]{2,1,0:T(8,128)S(1)} async-done(((f32[8,8,2560]{2,1,0:T(8,128)}), f32[8,8,2560]{2,1,0:T(8,128)S(1)}, u32[]{:S(2)}, u32[]{:S(2)}) %all-to-all-start.3) | async-done | bytes 655392 | tf_op jit(solution)/shard_map/all_to_all | solution.py:244
  148.8 1.2 gather_fusion.7
  (104 shorter events, 9.9 us)
Async XLA Ops:
  8.2 8.6 %copy-start = (f32[5,16,16,128]{3,2,1,0:T(8,128)S(1)}, f32[5,16,16,128]{3,2,1,0:T(8,128)}, u32[]{:S(2)}) copy-start(f32[5,16,16,128]{3,2,1,0:T(8,128)} %u_ref.1) | copy-start | bytes 1966084
  8.2 37.2 %all-to-all-start = ((f32[8,8,3840]{2,1,0:T(8,128)}), f32[8,8,3840]{2,1,0:T(8,128)S(1)}, u32[]{:S(2)}, u32[]{:S(2)}) async-start(f32[8,8,3840]{2,1,0:T(8,128)} %bitcast.8), calls=%async_computation | async-start | bytes 1966080 | tf_op jit(solution)/shard_map/all_to_all | solution.py:226
  16.8 52.6 %collective-permute-start.3 = (f32[5,16,128]{2,1,0:T(8,128)S(1)}, f32[5,16,128]{2,1,0:T(8,128)S(1)}, u32[]{:S(2)}, u32[]{:S(2)}) collective-permute-start(f32[5,16,128]{2,1,0:T(8,128)S(1)} %bitcast.222), channel_id=1, source_target_pairs={{8,0},{16,8},{24,16},{32,24},{40,32},{48,40},{56,48},{0,56},{9,1},... | collective-permute-start | bytes 122888 | tf_op jit(solution)/shard_map/ppermute | solution.py:20
  20.8 49.8 %collective-permute-start.2 = (f32[5,16,128]{2,1,0:T(8,128)S(1)}, f32[5,16,128]{2,1,0:T(8,128)S(1)}, u32[]{:S(2)}, u32[]{:S(2)}) collective-permute-start(f32[5,16,128]{2,1,0:T(8,128)S(1)} %bitcast.221), channel_id=1, source_target_pairs={{0,8},{8,16},{16,24},{24,32},{32,40},{40,48},{48,56},{56,0},{1,9},... | collective-permute-start | bytes 122888 | tf_op jit(solution)/shard_map/ppermute | solution.py:20
  20.8 49.8 %collective-permute-start = (f32[5,16,128]{2,1,0:T(8,128)S(1)}, f32[5,16,128]{2,1,0:T(8,128)S(1)}, u32[]{:S(2)}, u32[]{:S(2)}) collective-permute-start(f32[5,16,128]{2,1,0:T(8,128)S(1)} %get-tuple-element.20), channel_id=1, source_target_pairs={{0,64},{64,128},{128,192},{192,0},{1,65},{65,129},{129,193},{193,1... | collective-permute-start | bytes 122888 | tf_op jit(solution)/shard_map/ppermute | solution.py:20
  22.4 48.2 %collective-permute-start.1 = (f32[5,16,128]{2,1,0:T(8,128)S(1)}, f32[5,16,128]{2,1,0:T(8,128)S(1)}, u32[]{:S(2)}, u32[]{:S(2)}) collective-permute-start(f32[5,16,128]{2,1,0:T(8,128)S(1)} %get-tuple-element.21), channel_id=1, source_target_pairs={{64,0},{128,64},{192,128},{0,192},{65,1},{129,65},{193,129},{1,193... | collective-permute-start | bytes 122888 | tf_op jit(solution)/shard_map/ppermute | solution.py:20
  24.3 2.4 %copy-start.2 = (s32[6,1,1,8]{3,2,1,0:T(1,128)S(1)}, s32[6,1,1,8]{3,2,1,0:T(1,128)}, u32[]{:S(2)}) copy-start(s32[6,1,1,8]{3,2,1,0:T(1,128)} %param.7) | copy-start | bytes 580
  24.9 47.1 %collective-permute-start.5 = (f32[5,16,16]{2,1,0:T(8,128)S(1)}, f32[5,16,16]{2,1,0:T(8,128)S(1)}, u32[]{:S(2)}, u32[]{:S(2)}) collective-permute-start(f32[5,16,16]{2,1,0:T(8,128)S(1)} %bitcast.225), channel_id=1, source_target_pairs={{1,0},{2,1},{3,2},{4,3},{5,4},{6,5},{7,6},{0,7},{9,8},{10,9},{11,1... | collective-permute-start | bytes 15368 | tf_op jit(solution)/shard_map/ppermute | solution.py:20
  47.2 15.9 %all-to-all-start.1 = ((f32[8,8,3840]{2,1,0:T(8,128)}), f32[8,8,3840]{2,1,0:T(8,128)S(1)}, u32[]{:S(2)}, u32[]{:S(2)}) async-start(f32[8,8,3840]{2,1,0:T(8,128)} %bitcast.10), calls=%async_computation.1 | async-start | bytes 1966080 | tf_op jit(solution)/shard_map/all_to_all | solution.py:228
  69.5 4.1 %collective-permute-start.4 = (f32[5,16,16]{2,1,0:T(8,128)S(1)}, f32[5,16,16]{2,1,0:T(8,128)S(1)}, u32[]{:S(2)}, u32[]{:S(2)}) collective-permute-start(f32[5,16,16]{2,1,0:T(8,128)S(1)} %bitcast.226), channel_id=1, source_target_pairs={{0,1},{1,2},{2,3},{3,4},{4,5},{5,6},{6,7},{7,0},{8,9},{9,10},{10,1... | collective-permute-start | bytes 15368 | tf_op jit(solution)/shard_map/ppermute | solution.py:20
  82.9 7.6 %collective-permute-start.10 = (f32[5,16,16]{2,1,0:T(8,128)S(1)}, f32[5,16,16]{2,1,0:T(8,128)S(1)}, u32[]{:S(2)}, u32[]{:S(2)}) collective-permute-start(f32[5,16,16]{2,1,0:T(8,128)S(1)} %get-tuple-element.2), channel_id=1, source_target_pairs={{0,1},{1,2},{2,3},{3,4},{4,5},{5,6},{6,7},{7,0},{8,9},{9,10},{10,1... | collective-permute-start | bytes 15368 | tf_op jit(solution)/shard_map/ppermute | solution.py:20
  84.0 7.0 %collective-permute-start.11 = (f32[5,16,16]{2,1,0:T(8,128)S(1)}, f32[5,16,16]{2,1,0:T(8,128)S(1)}, u32[]{:S(2)}, u32[]{:S(2)}) collective-permute-start(f32[5,16,16]{2,1,0:T(8,128)S(1)} %get-tuple-element.3), channel_id=1, source_target_pairs={{1,0},{2,1},{3,2},{4,3},{5,4},{6,5},{7,6},{0,7},{9,8},{10,9},{11,1... | collective-permute-start | bytes 15368 | tf_op jit(solution)/shard_map/ppermute | solution.py:20
  87.3 5.2 %collective-permute-start.6 = (f32[5,16,128]{2,1,0:T(8,128)S(1)}, f32[5,16,128]{2,1,0:T(8,128)S(1)}, u32[]{:S(2)}, u32[]{:S(2)}) collective-permute-start(f32[5,16,128]{2,1,0:T(8,128)S(1)} %get-tuple-element.14), channel_id=1, source_target_pairs={{0,64},{64,128},{128,192},{192,0},{1,65},{65,129},{129,193},{193,1... | collective-permute-start | bytes 122888 | tf_op jit(solution)/shard_map/ppermute | solution.py:20
  88.8 4.0 %collective-permute-start.7 = (f32[5,16,128]{2,1,0:T(8,128)S(1)}, f32[5,16,128]{2,1,0:T(8,128)S(1)}, u32[]{:S(2)}, u32[]{:S(2)}) collective-permute-start(f32[5,16,128]{2,1,0:T(8,128)S(1)} %get-tuple-element.15), channel_id=1, source_target_pairs={{64,0},{128,64},{192,128},{0,192},{65,1},{129,65},{193,129},{1,193... | collective-permute-start | bytes 122888 | tf_op jit(solution)/shard_map/ppermute | solution.py:20
  90.5 2.3 %collective-permute-start.9 = (f32[5,16,128]{2,1,0:T(8,128)S(1)}, f32[5,16,128]{2,1,0:T(8,128)S(1)}, u32[]{:S(2)}, u32[]{:S(2)}) collective-permute-start(f32[5,16,128]{2,1,0:T(8,128)S(1)} %bitcast.224), channel_id=1, source_target_pairs={{8,0},{16,8},{24,16},{32,24},{40,32},{48,40},{56,48},{0,56},{9,1},... | collective-permute-start | bytes 122888 | tf_op jit(solution)/shard_map/ppermute | solution.py:20
  90.5 5.7 %collective-permute-start.8 = (f32[5,16,128]{2,1,0:T(8,128)S(1)}, f32[5,16,128]{2,1,0:T(8,128)S(1)}, u32[]{:S(2)}, u32[]{:S(2)}) collective-permute-start(f32[5,16,128]{2,1,0:T(8,128)S(1)} %bitcast.223), channel_id=1, source_target_pairs={{0,8},{8,16},{16,24},{24,32},{32,40},{40,48},{48,56},{56,0},{1,9},... | collective-permute-start | bytes 122888 | tf_op jit(solution)/shard_map/ppermute | solution.py:20
  106.6 14.8 %all-to-all-start.2 = ((f32[8,8,2560]{2,1,0:T(8,128)}), f32[8,8,2560]{2,1,0:T(8,128)S(1)}, u32[]{:S(2)}, u32[]{:S(2)}) async-start(f32[8,8,2560]{2,1,0:T(8,128)} %bitcast.65), calls=%async_computation.2 | async-start | bytes 1310720 | tf_op jit(solution)/shard_map/all_to_all | solution.py:242
  123.1 4.6 %copy-start.1 = (s32[1,512]{1,0:T(1,128)S(1)}, s32[1,512]{1,0:T(1,128)}, u32[]{:S(2)}) copy-start(s32[1,512]{1,0:T(1,128)} %param.6) | copy-start | bytes 6148
  123.1 25.7 %all-to-all-start.3 = ((f32[8,8,2560]{2,1,0:T(8,128)}), f32[8,8,2560]{2,1,0:T(8,128)S(1)}, u32[]{:S(2)}, u32[]{:S(2)}) async-start(f32[8,8,2560]{2,1,0:T(8,128)} %bitcast.67), calls=%async_computation.3 | async-start | bytes 1310720 | tf_op jit(solution)/shard_map/all_to_all | solution.py:244
